TPU v7x, 512 devices: a whole 4x8x8 slice. The times are simulated.
512 devices in a mesh: tm: 16 (over z, core), space: 32 (over x, y).
Axes of the slice: x: 4, y: 8, z: 8, core: 2. Of those that a mesh axis runs over, the one named last changes fastest.
Arguments:
- hindcast_archive: bfloat16 [16, 4, 16, 4, 32768], P('tm', None, None, None, 'space'), may hold values from -6 to 6
- op_blocks: bfloat16 [16, 3072, 128, 128], P('tm', 'space'), may hold values from -0.5 to 0.5
- block_index: int32 [16, 3072], P('tm', 'space'), may hold values from 0 to 11
- obs_values: bfloat16 [16, 4, 393216], P('tm', None, 'space'), may hold values from -6 to 6
- obs_weights: bfloat16 [16, 4, 393216], P('tm', None, 'space'), may hold values from 0.049804688 to 0.5
- obs_counts: int32 [16, 32], P('tm', 'space'), may hold values from 3072 to 12288, as said below
Outputs:
- gradient: float32 [16, 16, 4, 32768], P('tm', None, None, 'space')
Inputs may be any that keep to these rules, and one draw needn't show every extreme that they name: `block_index`: A value below 2 names one of the last 2 blocks of the tile before, a value from 2 to 9 one of the tile's own blocks, a larger one the first blocks of the tile after. `obs_counts`: in every valid time some tile has all 12288 slots live; the live observations of a tile are its first slots.
All inputs are finite; a program needn't handle non-finite values.
Results may differ from a plain program's by a relative error of at most 0.0014.
Values may be sent and summed in bfloat16 or wider, within the bound.
No kernel may reach another device: no remote copies, remote signals or barrier semaphores. Data moves between devices by JAX's collectives and lax.ppermute only.
A program may use at most 128 MiB of HBM per device.

v0:
```python
import jax
import jax.numpy as jnp
from jax import lax
from jax.sharding import PartitionSpec as P

GROUP_SITE_SPAN = 128
EDGE = 2


def with_halo(block, sides, width):
    for axis, dim in sides:
        count = lax.axis_size(axis)
        forward = [(i, i + 1) for i in range(count - 1)]
        forward.append((count - 1, 0))
        backward = [(target, source) for source, target in forward]
        low = lax.ppermute(
            lax.slice_in_dim(block, block.shape[dim] - width, None, axis=dim), axis, forward
        )
        high = lax.ppermute(lax.slice_in_dim(block, 0, width, axis=dim), axis, backward)
        block = jnp.concatenate([low, block, high], axis=dim)
    return block


def passed_along(value, axis, steps):
    count = lax.axis_size(axis)
    pairs = [(source, (source + steps) % count) for source in range(count)]
    return lax.ppermute(value, axis, pairs)


def extend(grouped):
    return with_halo(grouped, (("space", 4),), EDGE * GROUP_SITE_SPAN)


def observe(extended, operator, indices, values, weights, counts):
    block_width = operator.shape[-1]
    lead_shape = extended.shape[:-1]
    blocks = extended.reshape(-1, extended.shape[-1] // block_width, block_width)
    collected_entries = jnp.take(blocks, indices, axis=1)
    images = jnp.einsum(
        "bij,cbj->cbi", operator, collected_entries, preferred_element_type=jnp.float32
    )
    obs_blocks = indices.shape[0]
    field_count = values.shape[0]
    images = images.reshape(-1, field_count, obs_blocks, block_width)
    position = lax.broadcasted_iota(
        jnp.int32, (obs_blocks, block_width), 0
    ) * block_width + lax.broadcasted_iota(jnp.int32, (obs_blocks, block_width), 1)
    live_mask = (position < counts[0]).astype(jnp.float32)
    observed = values.reshape(field_count, obs_blocks, block_width).astype(jnp.float32)
    scaling = weights.reshape(field_count, obs_blocks, block_width).astype(jnp.float32)
    misfit = ((images - observed) * scaling * live_mask).astype(jnp.bfloat16)
    misfit = misfit.reshape(-1, obs_blocks, block_width)
    adjoint = jnp.einsum("bij,cbi->cbj", operator, misfit, preferred_element_type=jnp.float32)
    selector = (indices[:, None] == jnp.arange(blocks.shape[1], dtype=jnp.int32)[None, :]).astype(
        jnp.float32
    )
    cell_sums = jnp.einsum("cbj,bk->ckj", adjoint, selector, precision=lax.Precision.HIGHEST)
    return cell_sums.reshape(lead_shape + (extended.shape[-1],))


def settle(adjoint_ext):
    rim_width = EDGE * GROUP_SITE_SPAN
    lower_rim = adjoint_ext[..., :rim_width]
    upper_rim = adjoint_ext[..., -rim_width:]
    interior = adjoint_ext[..., rim_width:-rim_width]
    from_above = passed_along(lower_rim, "space", -1)
    from_below = passed_along(upper_rim, "space", 1)
    interior = interior.at[..., -rim_width:].add(from_above)
    return interior.at[..., :rim_width].add(from_below)


def body(hindcast_archive, op_blocks, block_index, obs_values, obs_weights, obs_counts):
    tm_size = lax.axis_size("tm")
    lead_count = hindcast_archive.shape[1]
    regrouped = [hindcast_archive[:, 0]]
    for horizon_step in range(1, lead_count):
        regrouped.append(
            passed_along(
                hindcast_archive[:, horizon_step], "tm", horizon_step * tm_size // lead_count
            )
        )
    extended = extend(jnp.stack(regrouped, axis=1))
    adjoint_ext = jnp.stack(
        [
            observe(
                extended[0],
                op_blocks[0],
                block_index[0],
                obs_values[0],
                obs_weights[0],
                obs_counts[0],
            )
        ]
    )
    interior = settle(adjoint_ext)
    running = interior[:, 0]
    for horizon_step in range(1, lead_count):
        running = running + passed_along(
            interior[:, horizon_step], "tm", -(horizon_step * tm_size // lead_count)
        )
    return running


def solution(mesh):
    in_specs = (
        P("tm", None, None, None, "space"),
        P("tm", "space", None, None),
        P("tm", "space"),
        P("tm", None, "space"),
        P("tm", None, "space"),
        P("tm", "space"),
    )
    out_specs = P("tm", None, None, "space")
    return jax.shard_map(body, mesh=mesh, in_specs=in_specs, out_specs=out_specs, check_vma=False)
```

profile of v0, /device:TPU:64, one launch (start us, length us, event | category | flops | bytes accessed | tf_op | source)
XLA Modules:
  0.0 153.4 jit_solution(2797161531548876321)
XLA Ops:
  0.0 1.4 fusion.41
  1.4 6.1 %collective-permute-start = (bf16[1,16,4,1024]{3,2,1,0:T(4,128)(2,1)S(1)}, bf16[1,16,4,1024]{3,2,1,0:T(4,128)(2,1)S(1)}, u32[]{:S(2)}, u32[]{:S(2)}) collective-permute-start(bf16[1,16,4,1024]{3,2,1,0:T(4,128)(2,1)S(1)} %get-tuple-element.37), channel_id=1, source_target_pairs={{0,128},{32,160},{64,192},{96,224},{128,256},{160,288},{192,320},{... | collective-permute-start | bytes 393224 | tf_op jit(solution)/shard_map/ppermute | solution.py:27
  7.5 5.9 %collective-permute-start.2 = (bf16[1,16,4,1024]{3,2,1,0:T(4,128)(2,1)S(1)}, bf16[1,16,4,1024]{3,2,1,0:T(4,128)(2,1)S(1)}, u32[]{:S(2)}, u32[]{:S(2)}) collective-permute-start(bf16[1,16,4,1024]{3,2,1,0:T(4,128)(2,1)S(1)} %get-tuple-element.38), channel_id=1, source_target_pairs={{0,384},{32,416},{64,448},{96,480},{128,0},{160,32},{192,64},{224,... | collective-permute-start | bytes 393224 | tf_op jit(solution)/shard_map/ppermute | solution.py:27
  13.4 6.0 %collective-permute-start.1 = (bf16[1,16,4,1024]{3,2,1,0:T(4,128)(2,1)S(1)}, bf16[1,16,4,1024]{3,2,1,0:T(4,128)(2,1)S(1)}, u32[]{:S(2)}, u32[]{:S(2)}) collective-permute-start(bf16[1,16,4,1024]{3,2,1,0:T(4,128)(2,1)S(1)} %get-tuple-element.39), channel_id=1, source_target_pairs={{0,256},{32,288},{64,320},{96,352},{128,384},{160,416},{192,448},{... | collective-permute-start | bytes 393224 | tf_op jit(solution)/shard_map/ppermute | solution.py:27
  20.1 0.9 bitcast_convert_fusion.1
  21.0 0.9 bitcast_convert_fusion
  23.3 5.2 %collective-permute-done.1 = bf16[1,16,4,1024]{3,2,1,0:T(4,128)(2,1)S(1)} collective-permute-done((bf16[1,16,4,1024]{3,2,1,0:T(4,128)(2,1)S(1)}, bf16[1,16,4,1024]{3,2,1,0:T(4,128)(2,1)S(1)}, u32[]{:S(2)}, u32[]{:S(2)}) %collective-permute-start.1) | collective-permute-done | bytes 131104 | tf_op jit(solution)/shard_map/ppermute | solution.py:27
  28.7 3.5 %collective-permute-start.3 = (bf16[1,4,16,4,256]{4,3,2,1,0:T(4,128)(2,1)S(1)}, bf16[1,4,16,4,256]{4,3,2,1,0:T(4,128)(2,1)S(1)}, u32[]{:S(2)}, u32[]{:S(2)}) collective-permute-start(bf16[1,4,16,4,256]{4,3,2,1,0:T(4,128)(2,1)S(1)} %get-tuple-element.34), channel_id=1, source_target_pairs={{0,1},{1,2},{2,3},{3,4},{4,5},{5,6},{6,7},{7,8},{8,9},{9,10},{10,1... | collective-permute-start | bytes 393224 | tf_op jit(solution)/shard_map/ppermute | solution.py:16
  32.2 6.0 %collective-permute-start.4 = (bf16[1,4,16,4,256]{4,3,2,1,0:T(4,128)(2,1)S(1)}, bf16[1,4,16,4,256]{4,3,2,1,0:T(4,128)(2,1)S(1)}, u32[]{:S(2)}, u32[]{:S(2)}) collective-permute-start(bf16[1,4,16,4,256]{4,3,2,1,0:T(4,128)(2,1)S(1)} %get-tuple-element.35), channel_id=1, source_target_pairs={{1,0},{2,1},{3,2},{4,3},{5,4},{6,5},{7,6},{8,7},{9,8},{10,9},{11,1... | collective-permute-start | bytes 393224 | tf_op jit(solution)/shard_map/ppermute | solution.py:19
  38.8 1.0 collective-permute-done.3
  39.9 1.2 collective-permute-done.4
  41.1 1.3 pad_maximum_fusion
  42.3 2.6 %reshape_squeeze.2 = bf16[256,12,128]{2,1,0:T(8,128)(2,1)} reshape(bf16[1,4,16,4,1536]{4,3,2,1,0:T(4,128)(2,1)} %pad_maximum_fusion) | data formatting | bytes 1572864 | tf_op jit(solution)/shard_map/reshape;squeeze | solution.py:37
  44.9 2.4 %copy.9 = bf16[256,12,128]{2,0,1:T(8,128)(2,1)} copy(bf16[256,12,128]{2,1,0:T(8,128)(2,1)} %reshape_squeeze.2) | data formatting | bytes 1572864 | tf_op jit(solution)/shard_map/reshape;squeeze | solution.py:37
  47.3 7.1 %gather_fusion = bf16[96,256,128]{2,1,0:T(8,128)(2,1)} fusion(bf16[256,12,128]{2,0,1:T(8,128)(2,1)} %copy.9, s32[1024]{0:T(1024)S(1)} %pad_clamp_fusion), kind=kCustom, calls=%fused_computation | custom fusion | bytes 12583296 | tf_op jit(solution)/shard_map/jit(_take)/gather | solution.py:38
  54.4 6.1 %mul.27 = f32[64,4,96,128]{3,1,0,2:T(4,128)} broadcast(f32[4,96,128]{2,0,1:T(4,128)S(1)} %bitcast_convert_fusion), dimensions={1,2,3} | broadcast | bytes 12779520 | tf_op jit(solution)/shard_map/mul | solution.py:51
  60.5 6.2 %sub.11 = f32[64,4,96,128]{3,1,0,2:T(4,128)} broadcast(f32[4,96,128]{2,0,1:T(4,128)S(1)} %bitcast_convert_fusion.1), dimensions={1,2,3} | broadcast | bytes 12779520 | tf_op jit(solution)/shard_map/sub | solution.py:51
  66.7 17.1 %fusion.6 = f32[96,256,128]{2,1,0:T(8,128)} fusion(f32[256,96,128]{2,0,1:T(8,128)} %bitcast.74, f32[256,96,128]{2,0,1:T(8,128)} %bitcast.75, f32[96,128]{1,0:T(8,128)S(1)} %copy-done.1, bf16[1,96,128,128]{3,2,1,0:T(8,128)(2,1)S(1)} %copy-done, bf16[96,256,128]{2,1,0:T(8,128)(2,1)} %gather_fusion, pred[96]{0:T(512)(128)(4,1)S(1)} %compare_and_fusion), kind=kOutput, calls=%fused_computation.8 | convolution fusion | flops 1626341376 | bytes 47235168 | tf_op jit(solution)/shard_map/bij,cbi->cbj/dot_general | solution.py:53
  83.8 16.2 %fusion.25 = f32[256,12,128]{2,1,0:T(8,128)} fusion(f32[96,256,128]{2,1,0:T(8,128)} %fusion.6, s32[96]{0:T(128)S(1)} %bitcast.82), kind=kOutput, calls=%fused_computation.17 | convolution fusion | flops 452985984 | bytes 14156160 | tf_op jit(solution)/shard_map/cbj,bk->ckj/dot_general | solution.py:57
  100.1 2.8 %stack_reshape.3 = f32[1,4,16,4,1536]{4,3,2,1,0:T(4,128)} reshape(f32[256,12,128]{2,1,0:T(8,128)} %fusion.25) | data formatting | bytes 3145728 | tf_op jit(solution)/shard_map/stack;reshape | solution.py:83
  102.8 1.1 fusion.40
  103.9 7.7 %collective-permute-start.5 = (f32[1,4,16,4,256]{4,3,2,1,0:T(4,128)S(1)}, f32[1,4,16,4,256]{4,3,2,1,0:T(4,128)S(1)}, u32[]{:S(2)}, u32[]{:S(2)}) collective-permute-start(f32[1,4,16,4,256]{4,3,2,1,0:T(4,128)S(1)} %get-tuple-element.30), channel_id=1, source_target_pairs={{0,31},{1,0},{2,1},{3,2},{4,3},{5,4},{6,5},{7,6},{8,7},{9,8},{10,9... | collective-permute-start | bytes 786440 | tf_op jit(solution)/shard_map/ppermute | solution.py:27
  111.6 1.9 %collective-permute-start.6 = (f32[1,4,16,4,256]{4,3,2,1,0:T(4,128)S(1)}, f32[1,4,16,4,256]{4,3,2,1,0:T(4,128)S(1)}, u32[]{:S(2)}, u32[]{:S(2)}) collective-permute-start(f32[1,4,16,4,256]{4,3,2,1,0:T(4,128)S(1)} %get-tuple-element.29), channel_id=1, source_target_pairs={{0,1},{1,2},{2,3},{3,4},{4,5},{5,6},{6,7},{7,8},{8,9},{9,10},{10,1... | collective-permute-start | bytes 786440 | tf_op jit(solution)/shard_map/ppermute | solution.py:27
  113.6 1.3 slice.125
  114.9 1.6 %collective-permute-done.5 = f32[1,4,16,4,256]{4,3,2,1,0:T(4,128)S(1)} collective-permute-done((f32[1,4,16,4,256]{4,3,2,1,0:T(4,128)S(1)}, f32[1,4,16,4,256]{4,3,2,1,0:T(4,128)S(1)}, u32[]{:S(2)}, u32[]{:S(2)}) %collective-permute-start.5) | collective-permute-done | bytes 262176 | tf_op jit(solution)/shard_map/ppermute | solution.py:27
  116.5 1.0 fusion.32
  117.6 6.4 %collective-permute-done.6 = f32[1,4,16,4,256]{4,3,2,1,0:T(4,128)S(1)} collective-permute-done((f32[1,4,16,4,256]{4,3,2,1,0:T(4,128)S(1)}, f32[1,4,16,4,256]{4,3,2,1,0:T(4,128)S(1)}, u32[]{:S(2)}, u32[]{:S(2)}) %collective-permute-start.6) | collective-permute-done | bytes 262176 | tf_op jit(solution)/shard_map/ppermute | solution.py:27
  124.1 1.9 %collective-permute-start.7 = (f32[1,16,4,1024]{3,2,1,0:T(4,128)S(1)}, f32[1,16,4,1024]{3,2,1,0:T(4,128)S(1)}, u32[]{:S(2)}, u32[]{:S(2)}) collective-permute-start(f32[1,16,4,1024]{3,2,1,0:T(4,128)S(1)} %get-tuple-element.31), channel_id=1, source_target_pairs={{0,384},{32,416},{64,448},{96,480},{128,0},{160,32},{192,64},{224,... | collective-permute-start | bytes 786440 | tf_op jit(solution)/shard_map/ppermute | solution.py:27
  126.0 4.8 %collective-permute-start.9 = (f32[1,16,4,1024]{3,2,1,0:T(4,128)S(1)}, f32[1,16,4,1024]{3,2,1,0:T(4,128)S(1)}, u32[]{:S(2)}, u32[]{:S(2)}) collective-permute-start(f32[1,16,4,1024]{3,2,1,0:T(4,128)S(1)} %get-tuple-element.32), channel_id=1, source_target_pairs={{0,128},{32,160},{64,192},{96,224},{128,256},{160,288},{192,320},{... | collective-permute-start | bytes 786440 | tf_op jit(solution)/shard_map/ppermute | solution.py:27
  130.9 3.0 %collective-permute-start.8 = (f32[1,16,4,1024]{3,2,1,0:T(4,128)S(1)}, f32[1,16,4,1024]{3,2,1,0:T(4,128)S(1)}, u32[]{:S(2)}, u32[]{:S(2)}) collective-permute-start(f32[1,16,4,1024]{3,2,1,0:T(4,128)S(1)} %get-tuple-element.33), channel_id=1, source_target_pairs={{0,256},{32,288},{64,320},{96,352},{128,384},{160,416},{192,448},{... | collective-permute-start | bytes 786440 | tf_op jit(solution)/shard_map/ppermute | solution.py:27
  133.9 4.0 %collective-permute-done.7 = f32[1,16,4,1024]{3,2,1,0:T(4,128)S(1)} collective-permute-done((f32[1,16,4,1024]{3,2,1,0:T(4,128)S(1)}, f32[1,16,4,1024]{3,2,1,0:T(4,128)S(1)}, u32[]{:S(2)}, u32[]{:S(2)}) %collective-permute-start.7) | collective-permute-done | bytes 262176 | tf_op jit(solution)/shard_map/ppermute | solution.py:27
  138.0 14.6 %collective-permute-done.9 = f32[1,16,4,1024]{3,2,1,0:T(4,128)S(1)} collective-permute-done((f32[1,16,4,1024]{3,2,1,0:T(4,128)S(1)}, f32[1,16,4,1024]{3,2,1,0:T(4,128)S(1)}, u32[]{:S(2)}, u32[]{:S(2)}) %collective-permute-start.9) | collective-permute-done | bytes 262176 | tf_op jit(solution)/shard_map/ppermute | solution.py:27
  (18 shorter events, 3.2 us)
Async XLA Ops:
  0.0 66.7 %copy-start = (bf16[1,96,128,128]{3,2,1,0:T(8,128)(2,1)S(1)}, bf16[1,96,128,128]{3,2,1,0:T(8,128)(2,1)}, u32[]{:S(2)}) copy-start(bf16[1,96,128,128]{3,2,1,0:T(8,128)(2,1)} %param.11) | copy-start | bytes 9437188
  1.4 21.9 %collective-permute-start = (bf16[1,16,4,1024]{3,2,1,0:T(4,128)(2,1)S(1)}, bf16[1,16,4,1024]{3,2,1,0:T(4,128)(2,1)S(1)}, u32[]{:S(2)}, u32[]{:S(2)}) collective-permute-start(bf16[1,16,4,1024]{3,2,1,0:T(4,128)(2,1)S(1)} %get-tuple-element.37), channel_id=1, source_target_pairs={{0,128},{32,160},{64,192},{96,224},{128,256},{160,288},{192,320},{... | collective-permute-start | bytes 393224 | tf_op jit(solution)/shard_map/ppermute | solution.py:27
  7.5 15.8 %collective-permute-start.2 = (bf16[1,16,4,1024]{3,2,1,0:T(4,128)(2,1)S(1)}, bf16[1,16,4,1024]{3,2,1,0:T(4,128)(2,1)S(1)}, u32[]{:S(2)}, u32[]{:S(2)}) collective-permute-start(bf16[1,16,4,1024]{3,2,1,0:T(4,128)(2,1)S(1)} %get-tuple-element.38), channel_id=1, source_target_pairs={{0,384},{32,416},{64,448},{96,480},{128,0},{160,32},{192,64},{224,... | collective-permute-start | bytes 393224 | tf_op jit(solution)/shard_map/ppermute | solution.py:27
  13.4 15.1 %collective-permute-start.1 = (bf16[1,16,4,1024]{3,2,1,0:T(4,128)(2,1)S(1)}, bf16[1,16,4,1024]{3,2,1,0:T(4,128)(2,1)S(1)}, u32[]{:S(2)}, u32[]{:S(2)}) collective-permute-start(bf16[1,16,4,1024]{3,2,1,0:T(4,128)(2,1)S(1)} %get-tuple-element.39), channel_id=1, source_target_pairs={{0,256},{32,288},{64,320},{96,352},{128,384},{160,416},{192,448},{... | collective-permute-start | bytes 393224 | tf_op jit(solution)/shard_map/ppermute | solution.py:27
  28.7 11.2 %collective-permute-start.3 = (bf16[1,4,16,4,256]{4,3,2,1,0:T(4,128)(2,1)S(1)}, bf16[1,4,16,4,256]{4,3,2,1,0:T(4,128)(2,1)S(1)}, u32[]{:S(2)}, u32[]{:S(2)}) collective-permute-start(bf16[1,4,16,4,256]{4,3,2,1,0:T(4,128)(2,1)S(1)} %get-tuple-element.34), channel_id=1, source_target_pairs={{0,1},{1,2},{2,3},{3,4},{4,5},{5,6},{6,7},{7,8},{8,9},{9,10},{10,1... | collective-permute-start | bytes 393224 | tf_op jit(solution)/shard_map/ppermute | solution.py:16
  32.2 8.9 %collective-permute-start.4 = (bf16[1,4,16,4,256]{4,3,2,1,0:T(4,128)(2,1)S(1)}, bf16[1,4,16,4,256]{4,3,2,1,0:T(4,128)(2,1)S(1)}, u32[]{:S(2)}, u32[]{:S(2)}) collective-permute-start(bf16[1,4,16,4,256]{4,3,2,1,0:T(4,128)(2,1)S(1)} %get-tuple-element.35), channel_id=1, source_target_pairs={{1,0},{2,1},{3,2},{4,3},{5,4},{6,5},{7,6},{8,7},{9,8},{10,9},{11,1... | collective-permute-start | bytes 393224 | tf_op jit(solution)/shard_map/ppermute | solution.py:19
  60.5 6.2 %copy-start.1 = (f32[96,128]{1,0:T(8,128)S(1)}, f32[96,128]{1,0:T(8,128)}, u32[]{:S(2)}) copy-start(f32[96,128]{1,0:T(8,128)} %fusion.33) | copy-start | bytes 147460
  66.7 17.1 %copy-start.2 = (s32[1,96]{1,0:T(1,128)S(1)}, s32[1,96]{1,0:T(1,128)}, u32[]{:S(2)}) copy-start(s32[1,96]{1,0:T(1,128)} %param.12) | copy-start | bytes 1156
  103.9 12.6 %collective-permute-start.5 = (f32[1,4,16,4,256]{4,3,2,1,0:T(4,128)S(1)}, f32[1,4,16,4,256]{4,3,2,1,0:T(4,128)S(1)}, u32[]{:S(2)}, u32[]{:S(2)}) collective-permute-start(f32[1,4,16,4,256]{4,3,2,1,0:T(4,128)S(1)} %get-tuple-element.30), channel_id=1, source_target_pairs={{0,31},{1,0},{2,1},{3,2},{4,3},{5,4},{6,5},{7,6},{8,7},{9,8},{10,9... | collective-permute-start | bytes 786440 | tf_op jit(solution)/shard_map/ppermute | solution.py:27
  111.6 12.3 %collective-permute-start.6 = (f32[1,4,16,4,256]{4,3,2,1,0:T(4,128)S(1)}, f32[1,4,16,4,256]{4,3,2,1,0:T(4,128)S(1)}, u32[]{:S(2)}, u32[]{:S(2)}) collective-permute-start(f32[1,4,16,4,256]{4,3,2,1,0:T(4,128)S(1)} %get-tuple-element.29), channel_id=1, source_target_pairs={{0,1},{1,2},{2,3},{3,4},{4,5},{5,6},{6,7},{7,8},{8,9},{9,10},{10,1... | collective-permute-start | bytes 786440 | tf_op jit(solution)/shard_map/ppermute | solution.py:27
  124.1 13.8 %collective-permute-start.7 = (f32[1,16,4,1024]{3,2,1,0:T(4,128)S(1)}, f32[1,16,4,1024]{3,2,1,0:T(4,128)S(1)}, u32[]{:S(2)}, u32[]{:S(2)}) collective-permute-start(f32[1,16,4,1024]{3,2,1,0:T(4,128)S(1)} %get-tuple-element.31), channel_id=1, source_target_pairs={{0,384},{32,416},{64,448},{96,480},{128,0},{160,32},{192,64},{224,... | collective-permute-start | bytes 786440 | tf_op jit(solution)/shard_map/ppermute | solution.py:27
  126.0 26.5 %collective-permute-start.9 = (f32[1,16,4,1024]{3,2,1,0:T(4,128)S(1)}, f32[1,16,4,1024]{3,2,1,0:T(4,128)S(1)}, u32[]{:S(2)}, u32[]{:S(2)}) collective-permute-start(f32[1,16,4,1024]{3,2,1,0:T(4,128)S(1)} %get-tuple-element.32), channel_id=1, source_target_pairs={{0,128},{32,160},{64,192},{96,224},{128,256},{160,288},{192,320},{... | collective-permute-start | bytes 786440 | tf_op jit(solution)/shard_map/ppermute | solution.py:27
  130.9 21.7 %collective-permute-start.8 = (f32[1,16,4,1024]{3,2,1,0:T(4,128)S(1)}, f32[1,16,4,1024]{3,2,1,0:T(4,128)S(1)}, u32[]{:S(2)}, u32[]{:S(2)}) collective-permute-start(f32[1,16,4,1024]{3,2,1,0:T(4,128)S(1)} %get-tuple-element.33), channel_id=1, source_target_pairs={{0,256},{32,288},{64,320},{96,352},{128,384},{160,416},{192,448},{... | collective-permute-start | bytes 786440 | tf_op jit(solution)/shard_map/ppermute | solution.py:27
where the time goes:
time: 154 us; the launch traced here: 153 us
  starting transfers between devices  46.9 us (30%)
  waiting for transfers between devices  34.1 us (22%)
  matrix products  33.3 us (22%)
  local copies, waits for them, and re-layouts  31 us (20%)
  other arithmetic  7.26 us (5%)
    ppermute x8, starting transfers between devices, passed_along(): return lax.ppermute(value, axis, pairs)  37.4 us
    ppermute x8, waiting for transfers between devices, passed_along(): return lax.ppermute(value, axis, pairs)  31.9 us
    dot_general x1, matrix products, observe(): jnp.einsum('bij,cbi->cbj', operator, misfit, preferred_element_type=jnp.f...  17.1 us
    dot_general x1, matrix products, observe(): jnp.einsum('cbj,bk->ckj', adjoint, selector, precision=lax.Precision.HIGH...  16.2 us
    gather x1, local copies, waits for them, and re-layouts, observe(): collected_entries = jnp.take(blocks, indices, axis=1)  7.08 us
    sub x1, local copies, waits for them, and re-layouts, observe(): misfit = ((images - observed) * scaling * live_mask).astype(jnp.bfloat16)  6.21 us
    mul x1, local copies, waits for them, and re-layouts, observe(): misfit = ((images - observed) * scaling * live_mask).astype(jnp.bfloat16)  6.1 us
    ppermute x1, starting transfers between devices, with_halo(): lax.ppermute(lax.slice_in_dim(block, 0, width, axis=dim), axis, backward)  6.01 us
  transfers between devices with their start and end apart: 10, of which 7 were waited for; matrix products, arithmetic and copies ran while one was open for 4% of the time, Pallas kernels for 0%

commit v1 on v0

--- a/solution.py
+++ b/solution.py
@@ -1,10 +1,15 @@
+import functools
+
 import jax
 import jax.numpy as jnp
 from jax import lax
+from jax.experimental import pallas as pl
+from jax.experimental.pallas import tpu as pltpu
 from jax.sharding import PartitionSpec as P
 
 GROUP_SITE_SPAN = 128
 EDGE = 2
+BLOCKS_PER_STEP = 8
 
 
 def with_halo(block, sides, width):
@@ -31,31 +36,65 @@
     return with_halo(grouped, (("space", 4),), EDGE * GROUP_SITE_SPAN)
 
 
-def observe(extended, operator, indices, values, weights, counts):
-    block_width = operator.shape[-1]
-    lead_shape = extended.shape[:-1]
-    blocks = extended.reshape(-1, extended.shape[-1] // block_width, block_width)
-    collected_entries = jnp.take(blocks, indices, axis=1)
-    images = jnp.einsum(
-        "bij,cbj->cbi", operator, collected_entries, preferred_element_type=jnp.float32
+def observe_kernel(idx_ref, cnt_ref, ext_ref, op_ref, val_ref, wt_ref, out_ref):
+    step = pl.program_id(0)
+    width = GROUP_SITE_SPAN
+    fields = val_ref.shape[0]
+    rows = ext_ref.shape[0]
+
+    @pl.when(step == 0)
+    def _():
+        out_ref[...] = jnp.zeros_like(out_ref)
+
+    count = cnt_ref[0]
+    lane = lax.broadcasted_iota(jnp.int32, (1, 1, width), 2)
+    for k in range(BLOCKS_PER_STEP):
+        b = step * BLOCKS_PER_STEP + k
+        start = pl.multiple_of(idx_ref[b] * width, width)
+        x = ext_ref[:, pl.ds(start, width)]
+        op = op_ref[k]
+        images = lax.dot_general(
+            x, op, (((1,), (1,)), ((), ())), preferred_element_type=jnp.float32
+        ).reshape(fields, rows // fields, width)
+        observed = val_ref[:, k * width:(k + 1) * width].astype(jnp.float32)[:, None, :]
+        scaling = wt_ref[:, k * width:(k + 1) * width].astype(jnp.float32)[:, None, :]
+        live = (b * width + lane) < count
+        misfit = jnp.where(live, (images - observed) * scaling, 0.0).astype(jnp.bfloat16)
+        adjoint = jnp.dot(
+            misfit.reshape(rows, width), op, preferred_element_type=jnp.float32
+        )
+        out_ref[:, pl.ds(start, width)] += adjoint
+
+
+def observe(ext_rows, operator, indices, values, weights, counts):
+    rows, cells = ext_rows.shape
+    obs_blocks = operator.shape[0]
+    width = GROUP_SITE_SPAN
+    fields = values.shape[0]
+    steps = obs_blocks // BLOCKS_PER_STEP
+    span = BLOCKS_PER_STEP * width
+    grid_spec = pltpu.PrefetchScalarGridSpec(
+        num_scalar_prefetch=2,
+        grid=(steps,),
+        in_specs=[
+            pl.BlockSpec((rows, cells), lambda g, i, c: (0, 0)),
+            pl.BlockSpec((BLOCKS_PER_STEP, width, width), lambda g, i, c: (g, 0, 0)),
+            pl.BlockSpec((fields, span), lambda g, i, c: (0, g)),
+            pl.BlockSpec((fields, span), lambda g, i, c: (0, g)),
+        ],
+        out_specs=pl.BlockSpec((rows, cells), lambda g, i, c: (0, 0)),
     )
-    obs_blocks = indices.shape[0]
-    field_count = values.shape[0]
-    images = images.reshape(-1, field_count, obs_blocks, block_width)
-    position = lax.broadcasted_iota(
-        jnp.int32, (obs_blocks, block_width), 0
-    ) * block_width + lax.broadcasted_iota(jnp.int32, (obs_blocks, block_width), 1)
-    live_mask = (position < counts[0]).astype(jnp.float32)
-    observed = values.reshape(field_count, obs_blocks, block_width).astype(jnp.float32)
-    scaling = weights.reshape(field_count, obs_blocks, block_width).astype(jnp.float32)
-    misfit = ((images - observed) * scaling * live_mask).astype(jnp.bfloat16)
-    misfit = misfit.reshape(-1, obs_blocks, block_width)
-    adjoint = jnp.einsum("bij,cbi->cbj", operator, misfit, preferred_element_type=jnp.float32)
-    selector = (indices[:, None] == jnp.arange(blocks.shape[1], dtype=jnp.int32)[None, :]).astype(
-        jnp.float32
-    )
-    cell_sums = jnp.einsum("cbj,bk->ckj", adjoint, selector, precision=lax.Precision.HIGHEST)
-    return cell_sums.reshape(lead_shape + (extended.shape[-1],))
+    flops = 4 * obs_blocks * rows * width * width
+    bytes_accessed = operator.size * 2 + ext_rows.size * 2 + rows * cells * 4 + values.size * 4
+    return pl.pallas_call(
+        observe_kernel,
+        grid_spec=grid_spec,
+        out_shape=jax.ShapeDtypeStruct((rows, cells), jnp.float32),
+        compiler_params=pltpu.CompilerParams(dimension_semantics=("arbitrary",)),
+        cost_estimate=pl.CostEstimate(
+            flops=flops, bytes_accessed=bytes_accessed, transcendentals=0
+        ),
+    )(indices, counts, ext_rows, operator, values, weights)
 
 
 def settle(adjoint_ext):
@@ -79,19 +118,15 @@
                 hindcast_archive[:, horizon_step], "tm", horizon_step * tm_size // lead_count
             )
         )
-    extended = extend(jnp.stack(regrouped, axis=1))
-    adjoint_ext = jnp.stack(
-        [
-            observe(
-                extended[0],
-                op_blocks[0],
-                block_index[0],
-                obs_values[0],
-                obs_weights[0],
-                obs_counts[0],
-            )
-        ]
+    extended = extend(jnp.stack(regrouped, axis=1))[0]
+    leads, members, fields, cells = extended.shape
+    ext_rows = jnp.transpose(extended, (2, 0, 1, 3)).reshape(fields * leads * members, cells)
+    adjoint_rows = observe(
+        ext_rows, op_blocks[0], block_index[0], obs_values[0], obs_weights[0], obs_counts[0]
     )
+    adjoint_ext = jnp.transpose(
+        adjoint_rows.reshape(fields, leads, members, cells), (1, 2, 0, 3)
+    )[None]
     interior = settle(adjoint_ext)
     running = interior[:, 0]
     for horizon_step in range(1, lead_count):

time: 154 us -> 108 us (0.70)
  matrix products: 33.3 us -> 0 us
  local copies, waits for them, and re-layouts: 31 us -> 4.95 us
  Pallas kernels: 0 us -> 12.9 us
  waiting for transfers between devices: 34.1 us -> 40 us
  other arithmetic: 7.26 us -> 1.53 us
    dot_general x2 -> x0, matrix products: 33.3 us -> none  [the longest x1 17.1 us: observe(): jnp.einsum('bij,cbi->cbj', operator, misfit, preferred_element_type=jnp.f...]
    pallas_call x0 -> x1, Pallas kernels: none -> 12.9 us  [observe(): pl.pallas_call(observe_kernel, grid_spec=grid_spec, out_shape=jax.ShapeDt...]
    another operation x3 -> x0, local copies, waits for them, and re-layouts: 7.75 us -> none  [the longest x2 4.96 us: observe(): extended.reshape(-1, extended.shape[-1] // block_width, block_width)]
    gather x1 -> x0, local copies, waits for them, and re-layouts: 7.08 us -> none  [observe(): collected_entries = jnp.take(blocks, indices, axis=1)]
    sub x1 -> x0, local copies, waits for them, and re-layouts: 6.21 us -> none  [observe(): misfit = ((images - observed) * scaling * live_mask).astype(jnp.bfloat16)]
    mul x1 -> x0, local copies, waits for them, and re-layouts: 6.1 us -> none  [observe(): misfit = ((images - observed) * scaling * live_mask).astype(jnp.bfloat16)]
    ppermute x8, waiting for transfers between devices: 31.9 us -> 37.7 us  [passed_along(): return lax.ppermute(value, axis, pairs)]
    convert_element_type x3 -> x0, other arithmetic: 2.54 us -> none  [the longest x1 0.92 us: observe(): values.reshape(field_count, obs_blocks, block_width).astype(jnp.float32)]
  transfers between devices with their start and end apart: 10 -> 10, of which waited for: 7 -> 8; matrix products, arithmetic and copies ran while one was open for 4% -> 0% of each run, Pallas kernels for 0% -> 0%
where the time goes in v1:
time: 108 us; the launch traced here: 107 us
  starting transfers between devices  46.9 us (43%)
  waiting for transfers between devices  40 us (37%)
  Pallas kernels  12.9 us (12%)
  local copies, waits for them, and re-layouts  4.95 us (5%)
  other arithmetic  1.53 us (1%)
    ppermute x8, waiting for transfers between devices, passed_along(): return lax.ppermute(value, axis, pairs)  37.7 us
    ppermute x8, starting transfers between devices, passed_along(): return lax.ppermute(value, axis, pairs)  37.4 us
    pallas_call x1, Pallas kernels, observe(): pl.pallas_call(observe_kernel, grid_spec=grid_spec, out_shape=jax.ShapeDt...  12.9 us
    ppermute x1, starting transfers between devices, with_halo(): lax.ppermute(lax.slice_in_dim(block, 0, width, axis=dim), axis, backward)  6.01 us
    ppermute x1, starting transfers between devices, with_halo(): lax.ppermute(lax.slice_in_dim(block, block.shape[dim] - width, None, axis...  3.48 us
    reshape x1, local copies, waits for them, and re-layouts, body(): adjoint_rows.reshape(fields, leads, members, cells)  2.42 us
  transfers between devices with their start and end apart: 10, of which 8 were waited for; matrix products, arithmetic and copies ran while one was open for 0% of the time, Pallas kernels for 0%

profile of v1, /device:TPU:64, one launch (start us, length us, event | category | flops | bytes accessed | tf_op | source)
XLA Modules:
  0.0 107.0 jit_solution(2185507940047333966)
XLA Ops:
  0.0 1.3 %fusion.6 = (bf16[1,1,16,4,1024]{4,3,2,1,0:T(4,128)(2,1)S(1)}, bf16[1,16,4,1024]{3,2,1,0:T(4,128)(2,1)S(1)}, bf16[1,16,4,1024]{3,2,1,0:T(4,128)(2,1)S(1)}, bf16[1,16,4,1024]{3,2,1,0:T(4,128)(2,1)S(1)}) fusion(bf16[1,4,16,4,1024]{4,3,2,1,0:T(4,128)(2,1)} %param.10), kind=kLoop, calls=%fused_computation.21 | loop fusion | bytes 1048576 | tf_op jit(solution)/shard_map/slice | solution.py:114
  1.3 6.1 %collective-permute-start = (bf16[1,16,4,1024]{3,2,1,0:T(4,128)(2,1)S(1)}, bf16[1,16,4,1024]{3,2,1,0:T(4,128)(2,1)S(1)}, u32[]{:S(2)}, u32[]{:S(2)}) collective-permute-start(bf16[1,16,4,1024]{3,2,1,0:T(4,128)(2,1)S(1)} %get-tuple-element.37), channel_id=1, source_target_pairs={{0,128},{32,160},{64,192},{96,224},{128,256},{160,288},{192,320},{... | collective-permute-start | bytes 393224 | tf_op jit(solution)/shard_map/ppermute | solution.py:32
  7.4 5.9 %collective-permute-start.2 = (bf16[1,16,4,1024]{3,2,1,0:T(4,128)(2,1)S(1)}, bf16[1,16,4,1024]{3,2,1,0:T(4,128)(2,1)S(1)}, u32[]{:S(2)}, u32[]{:S(2)}) collective-permute-start(bf16[1,16,4,1024]{3,2,1,0:T(4,128)(2,1)S(1)} %get-tuple-element.38), channel_id=1, source_target_pairs={{0,384},{32,416},{64,448},{96,480},{128,0},{160,32},{192,64},{224,... | collective-permute-start | bytes 393224 | tf_op jit(solution)/shard_map/ppermute | solution.py:32
  13.3 6.0 %collective-permute-start.1 = (bf16[1,16,4,1024]{3,2,1,0:T(4,128)(2,1)S(1)}, bf16[1,16,4,1024]{3,2,1,0:T(4,128)(2,1)S(1)}, u32[]{:S(2)}, u32[]{:S(2)}) collective-permute-start(bf16[1,16,4,1024]{3,2,1,0:T(4,128)(2,1)S(1)} %get-tuple-element.39), channel_id=1, source_target_pairs={{0,256},{32,288},{64,320},{96,352},{128,384},{160,416},{192,448},{... | collective-permute-start | bytes 393224 | tf_op jit(solution)/shard_map/ppermute | solution.py:32
  19.3 0.0 collective-permute-done
  19.3 0.5 collective-permute-done.2
  19.8 8.6 %collective-permute-done.1 = bf16[1,16,4,1024]{3,2,1,0:T(4,128)(2,1)S(1)} collective-permute-done((bf16[1,16,4,1024]{3,2,1,0:T(4,128)(2,1)S(1)}, bf16[1,16,4,1024]{3,2,1,0:T(4,128)(2,1)S(1)}, u32[]{:S(2)}, u32[]{:S(2)}) %collective-permute-start.1) | collective-permute-done | bytes 131104 | tf_op jit(solution)/shard_map/ppermute | solution.py:32
  28.4 0.1 pad_maximum_fusion.3
  28.5 3.5 %collective-permute-start.3 = (bf16[1,4,16,4,256]{4,3,2,1,0:T(4,128)(2,1)S(1)}, bf16[1,4,16,4,256]{4,3,2,1,0:T(4,128)(2,1)S(1)}, u32[]{:S(2)}, u32[]{:S(2)}) collective-permute-start(bf16[1,4,16,4,256]{4,3,2,1,0:T(4,128)(2,1)S(1)} %get-tuple-element.34), channel_id=1, source_target_pairs={{0,1},{1,2},{2,3},{3,4},{4,5},{5,6},{6,7},{7,8},{8,9},{9,10},{10,1... | collective-permute-start | bytes 393224 | tf_op jit(solution)/shard_map/ppermute | solution.py:21
  32.0 6.0 %collective-permute-start.4 = (bf16[1,4,16,4,256]{4,3,2,1,0:T(4,128)(2,1)S(1)}, bf16[1,4,16,4,256]{4,3,2,1,0:T(4,128)(2,1)S(1)}, u32[]{:S(2)}, u32[]{:S(2)}) collective-permute-start(bf16[1,4,16,4,256]{4,3,2,1,0:T(4,128)(2,1)S(1)} %get-tuple-element.35), channel_id=1, source_target_pairs={{1,0},{2,1},{3,2},{4,3},{5,4},{6,5},{7,6},{8,7},{9,8},{10,9},{11,1... | collective-permute-start | bytes 393224 | tf_op jit(solution)/shard_map/ppermute | solution.py:24
  38.7 1.1 collective-permute-done.3
  39.7 1.2 %collective-permute-done.4 = bf16[1,4,16,4,256]{4,3,2,1,0:T(4,128)(2,1)S(1)} collective-permute-done((bf16[1,4,16,4,256]{4,3,2,1,0:T(4,128)(2,1)S(1)}, bf16[1,4,16,4,256]{4,3,2,1,0:T(4,128)(2,1)S(1)}, u32[]{:S(2)}, u32[]{:S(2)}) %collective-permute-start.4) | collective-permute-done | bytes 131104 | tf_op jit(solution)/shard_map/ppermute | solution.py:24
  40.9 0.3 maximum_bitcast_fusion
  41.3 1.0 copy.7
  42.3 12.9 %shard_map.64 = f32[256,1536]{1,0:T(8,128)} custom-call(s32[96]{0:T(128)} %bitcast.54, s32[1]{0:T(128)} %bitcast.39.cnt_ref, bf16[256,1536]{1,0:T(8,128)(2,1)} %bitcast.44, bf16[96,128,128]{2,1,0:T(8,128)(2,1)} %bitcast.51, bf16[4,12288]{1,0:T(4,128)(2,1)} %bitcast.52, bf16[4,12288]{1,0:T(4,128)(2,1)} %bitcast.53), custom_call_target="tpu_custom_call" | custom-call | flops 1610612736 | bytes 5701632 | tf_op jit(solution)/shard_map/pallas_call | solution.py:89
  55.2 2.4 %copy.10 = f32[4,4,16,1536]{3,0,2,1:T(4,128)S(1)} copy(f32[4,4,16,1536]{3,2,1,0:T(8,128)} %bitcast.43) | data formatting | bytes 3145728 | tf_op jit(solution)/shard_map/reshape | solution.py:128
  57.6 7.7 %collective-permute-start.5 = (f32[1,4,16,4,256]{4,3,2,1,0:T(4,128)S(1)}, f32[1,4,16,4,256]{4,3,2,1,0:T(4,128)S(1)}, u32[]{:S(2)}, u32[]{:S(2)}) collective-permute-start(f32[1,4,16,4,256]{4,3,2,1,0:T(4,128)S(1)} %get-tuple-element.30), channel_id=1, source_target_pairs={{0,31},{1,0},{2,1},{3,2},{4,3},{5,4},{6,5},{7,6},{8,7},{9,8},{10,9... | collective-permute-start | bytes 786440 | tf_op jit(solution)/shard_map/ppermute | solution.py:32
  65.4 1.9 %collective-permute-start.6 = (f32[1,4,16,4,256]{4,3,2,1,0:T(4,128)S(1)}, f32[1,4,16,4,256]{4,3,2,1,0:T(4,128)S(1)}, u32[]{:S(2)}, u32[]{:S(2)}) collective-permute-start(f32[1,4,16,4,256]{4,3,2,1,0:T(4,128)S(1)} %get-tuple-element.29), channel_id=1, source_target_pairs={{0,1},{1,2},{2,3},{3,4},{4,5},{5,6},{6,7},{7,8},{8,9},{9,10},{10,1... | collective-permute-start | bytes 786440 | tf_op jit(solution)/shard_map/ppermute | solution.py:32
  67.3 0.1 slice.123
  67.4 2.8 %collective-permute-done.5 = f32[1,4,16,4,256]{4,3,2,1,0:T(4,128)S(1)} collective-permute-done((f32[1,4,16,4,256]{4,3,2,1,0:T(4,128)S(1)}, f32[1,4,16,4,256]{4,3,2,1,0:T(4,128)S(1)}, u32[]{:S(2)}, u32[]{:S(2)}) %collective-permute-start.5) | collective-permute-done | bytes 262176 | tf_op jit(solution)/shard_map/ppermute | solution.py:32
  70.2 0.1 fusion.4
  70.3 7.3 %collective-permute-done.6 = f32[1,4,16,4,256]{4,3,2,1,0:T(4,128)S(1)} collective-permute-done((f32[1,4,16,4,256]{4,3,2,1,0:T(4,128)S(1)}, f32[1,4,16,4,256]{4,3,2,1,0:T(4,128)S(1)}, u32[]{:S(2)}, u32[]{:S(2)}) %collective-permute-start.6) | collective-permute-done | bytes 262176 | tf_op jit(solution)/shard_map/ppermute | solution.py:32
  77.6 0.1 fusion.3
  77.7 0.1 slice_bitcast_fusion.2
  77.8 1.9 %collective-permute-start.7 = (f32[1,16,4,1024]{3,2,1,0:T(4,128)S(1)}, f32[1,16,4,1024]{3,2,1,0:T(4,128)S(1)}, u32[]{:S(2)}, u32[]{:S(2)}) collective-permute-start(f32[1,16,4,1024]{3,2,1,0:T(4,128)S(1)} %get-tuple-element.31), channel_id=1, source_target_pairs={{0,384},{32,416},{64,448},{96,480},{128,0},{160,32},{192,64},{224,... | collective-permute-start | bytes 786440 | tf_op jit(solution)/shard_map/ppermute | solution.py:32
  79.7 4.8 %collective-permute-start.9 = (f32[1,16,4,1024]{3,2,1,0:T(4,128)S(1)}, f32[1,16,4,1024]{3,2,1,0:T(4,128)S(1)}, u32[]{:S(2)}, u32[]{:S(2)}) collective-permute-start(f32[1,16,4,1024]{3,2,1,0:T(4,128)S(1)} %get-tuple-element.32), channel_id=1, source_target_pairs={{0,128},{32,160},{64,192},{96,224},{128,256},{160,288},{192,320},{... | collective-permute-start | bytes 786440 | tf_op jit(solution)/shard_map/ppermute | solution.py:32
  84.6 3.1 %collective-permute-start.8 = (f32[1,16,4,1024]{3,2,1,0:T(4,128)S(1)}, f32[1,16,4,1024]{3,2,1,0:T(4,128)S(1)}, u32[]{:S(2)}, u32[]{:S(2)}) collective-permute-start(f32[1,16,4,1024]{3,2,1,0:T(4,128)S(1)} %get-tuple-element.33), channel_id=1, source_target_pairs={{0,256},{32,288},{64,320},{96,352},{128,384},{160,416},{192,448},{... | collective-permute-start | bytes 786440 | tf_op jit(solution)/shard_map/ppermute | solution.py:32
  87.6 3.6 %collective-permute-done.7 = f32[1,16,4,1024]{3,2,1,0:T(4,128)S(1)} collective-permute-done((f32[1,16,4,1024]{3,2,1,0:T(4,128)S(1)}, f32[1,16,4,1024]{3,2,1,0:T(4,128)S(1)}, u32[]{:S(2)}, u32[]{:S(2)}) %collective-permute-start.7) | collective-permute-done | bytes 262176 | tf_op jit(solution)/shard_map/ppermute | solution.py:32
  91.2 14.9 %collective-permute-done.9 = f32[1,16,4,1024]{3,2,1,0:T(4,128)S(1)} collective-permute-done((f32[1,16,4,1024]{3,2,1,0:T(4,128)S(1)}, f32[1,16,4,1024]{3,2,1,0:T(4,128)S(1)}, u32[]{:S(2)}, u32[]{:S(2)}) %collective-permute-start.9) | collective-permute-done | bytes 262176 | tf_op jit(solution)/shard_map/ppermute | solution.py:32
  106.1 0.0 collective-permute-done.8
  106.1 0.9 fusion.2
  (1 shorter events, 0.0 us)
Async XLA Ops:
  1.3 18.0 %collective-permute-start = (bf16[1,16,4,1024]{3,2,1,0:T(4,128)(2,1)S(1)}, bf16[1,16,4,1024]{3,2,1,0:T(4,128)(2,1)S(1)}, u32[]{:S(2)}, u32[]{:S(2)}) collective-permute-start(bf16[1,16,4,1024]{3,2,1,0:T(4,128)(2,1)S(1)} %get-tuple-element.37), channel_id=1, source_target_pairs={{0,128},{32,160},{64,192},{96,224},{128,256},{160,288},{192,320},{... | collective-permute-start | bytes 393224 | tf_op jit(solution)/shard_map/ppermute | solution.py:32
  7.4 12.4 %collective-permute-start.2 = (bf16[1,16,4,1024]{3,2,1,0:T(4,128)(2,1)S(1)}, bf16[1,16,4,1024]{3,2,1,0:T(4,128)(2,1)S(1)}, u32[]{:S(2)}, u32[]{:S(2)}) collective-permute-start(bf16[1,16,4,1024]{3,2,1,0:T(4,128)(2,1)S(1)} %get-tuple-element.38), channel_id=1, source_target_pairs={{0,384},{32,416},{64,448},{96,480},{128,0},{160,32},{192,64},{224,... | collective-permute-start | bytes 393224 | tf_op jit(solution)/shard_map/ppermute | solution.py:32
  13.3 15.1 %collective-permute-start.1 = (bf16[1,16,4,1024]{3,2,1,0:T(4,128)(2,1)S(1)}, bf16[1,16,4,1024]{3,2,1,0:T(4,128)(2,1)S(1)}, u32[]{:S(2)}, u32[]{:S(2)}) collective-permute-start(bf16[1,16,4,1024]{3,2,1,0:T(4,128)(2,1)S(1)} %get-tuple-element.39), channel_id=1, source_target_pairs={{0,256},{32,288},{64,320},{96,352},{128,384},{160,416},{192,448},{... | collective-permute-start | bytes 393224 | tf_op jit(solution)/shard_map/ppermute | solution.py:32
  28.5 11.2 %collective-permute-start.3 = (bf16[1,4,16,4,256]{4,3,2,1,0:T(4,128)(2,1)S(1)}, bf16[1,4,16,4,256]{4,3,2,1,0:T(4,128)(2,1)S(1)}, u32[]{:S(2)}, u32[]{:S(2)}) collective-permute-start(bf16[1,4,16,4,256]{4,3,2,1,0:T(4,128)(2,1)S(1)} %get-tuple-element.34), channel_id=1, source_target_pairs={{0,1},{1,2},{2,3},{3,4},{4,5},{5,6},{6,7},{7,8},{8,9},{9,10},{10,1... | collective-permute-start | bytes 393224 | tf_op jit(solution)/shard_map/ppermute | solution.py:21
  32.0 8.9 %collective-permute-start.4 = (bf16[1,4,16,4,256]{4,3,2,1,0:T(4,128)(2,1)S(1)}, bf16[1,4,16,4,256]{4,3,2,1,0:T(4,128)(2,1)S(1)}, u32[]{:S(2)}, u32[]{:S(2)}) collective-permute-start(bf16[1,4,16,4,256]{4,3,2,1,0:T(4,128)(2,1)S(1)} %get-tuple-element.35), channel_id=1, source_target_pairs={{1,0},{2,1},{3,2},{4,3},{5,4},{6,5},{7,6},{8,7},{9,8},{10,9},{11,1... | collective-permute-start | bytes 393224 | tf_op jit(solution)/shard_map/ppermute | solution.py:24
  57.6 12.5 %collective-permute-start.5 = (f32[1,4,16,4,256]{4,3,2,1,0:T(4,128)S(1)}, f32[1,4,16,4,256]{4,3,2,1,0:T(4,128)S(1)}, u32[]{:S(2)}, u32[]{:S(2)}) collective-permute-start(f32[1,4,16,4,256]{4,3,2,1,0:T(4,128)S(1)} %get-tuple-element.30), channel_id=1, source_target_pairs={{0,31},{1,0},{2,1},{3,2},{4,3},{5,4},{6,5},{7,6},{8,7},{9,8},{10,9... | collective-permute-start | bytes 786440 | tf_op jit(solution)/shard_map/ppermute | solution.py:32
  65.4 12.3 %collective-permute-start.6 = (f32[1,4,16,4,256]{4,3,2,1,0:T(4,128)S(1)}, f32[1,4,16,4,256]{4,3,2,1,0:T(4,128)S(1)}, u32[]{:S(2)}, u32[]{:S(2)}) collective-permute-start(f32[1,4,16,4,256]{4,3,2,1,0:T(4,128)S(1)} %get-tuple-element.29), channel_id=1, source_target_pairs={{0,1},{1,2},{2,3},{3,4},{4,5},{5,6},{6,7},{7,8},{8,9},{9,10},{10,1... | collective-permute-start | bytes 786440 | tf_op jit(solution)/shard_map/ppermute | solution.py:32
  77.8 13.4 %collective-permute-start.7 = (f32[1,16,4,1024]{3,2,1,0:T(4,128)S(1)}, f32[1,16,4,1024]{3,2,1,0:T(4,128)S(1)}, u32[]{:S(2)}, u32[]{:S(2)}) collective-permute-start(f32[1,16,4,1024]{3,2,1,0:T(4,128)S(1)} %get-tuple-element.31), channel_id=1, source_target_pairs={{0,384},{32,416},{64,448},{96,480},{128,0},{160,32},{192,64},{224,... | collective-permute-start | bytes 786440 | tf_op jit(solution)/shard_map/ppermute | solution.py:32
  79.7 26.4 %collective-permute-start.9 = (f32[1,16,4,1024]{3,2,1,0:T(4,128)S(1)}, f32[1,16,4,1024]{3,2,1,0:T(4,128)S(1)}, u32[]{:S(2)}, u32[]{:S(2)}) collective-permute-start(f32[1,16,4,1024]{3,2,1,0:T(4,128)S(1)} %get-tuple-element.32), channel_id=1, source_target_pairs={{0,128},{32,160},{64,192},{96,224},{128,256},{160,288},{192,320},{... | collective-permute-start | bytes 786440 | tf_op jit(solution)/shard_map/ppermute | solution.py:32
  84.6 21.6 %collective-permute-start.8 = (f32[1,16,4,1024]{3,2,1,0:T(4,128)S(1)}, f32[1,16,4,1024]{3,2,1,0:T(4,128)S(1)}, u32[]{:S(2)}, u32[]{:S(2)}) collective-permute-start(f32[1,16,4,1024]{3,2,1,0:T(4,128)S(1)} %get-tuple-element.33), channel_id=1, source_target_pairs={{0,256},{32,288},{64,320},{96,352},{128,384},{160,416},{192,448},{... | collective-permute-start | bytes 786440 | tf_op jit(solution)/shard_map/ppermute | solution.py:32

commit v2 on v1

v2 whole, which is shorter than its diff:
```python
import jax
import jax.numpy as jnp
from jax import lax
from jax.experimental import pallas as pl
from jax.experimental.pallas import tpu as pltpu
from jax.sharding import Mesh
from jax.sharding import PartitionSpec as P

GROUP_SITE_SPAN = 128
EDGE = 2
BLOCKS_PER_STEP = 8


def ring_pairs(count, steps):
    return [(source, (source + steps) % count) for source in range(count)]


def observe_kernel(members, idx_ref, cnt_ref, ext_ref, op_ref, val_ref, wt_ref, out_ref):
    step = pl.program_id(0)
    width = GROUP_SITE_SPAN
    fields = val_ref.shape[0]
    rows = ext_ref.shape[0]

    @pl.when(step == 0)
    def _():
        out_ref[...] = jnp.zeros_like(out_ref)

    count = cnt_ref[0]
    lane = lax.broadcasted_iota(jnp.int32, (1, 1, 1, width), 3)
    for k in range(BLOCKS_PER_STEP):
        b = step * BLOCKS_PER_STEP + k
        start = pl.multiple_of(idx_ref[b] * width, width)
        x = ext_ref[:, pl.ds(start, width)]
        op = op_ref[k]
        images = lax.dot_general(
            x, op, (((1,), (1,)), ((), ())), preferred_element_type=jnp.float32
        ).reshape(rows // (fields * members), fields, members, width)
        observed = val_ref[:, k * width:(k + 1) * width].astype(jnp.float32)[None, :, None, :]
        scaling = wt_ref[:, k * width:(k + 1) * width].astype(jnp.float32)[None, :, None, :]
        live = (b * width + lane) < count
        misfit = jnp.where(live, (images - observed) * scaling, 0.0)
        misfit = misfit.reshape(rows, width).astype(jnp.bfloat16)
        adjoint = jnp.dot(misfit, op, preferred_element_type=jnp.float32)
        out_ref[:, pl.ds(start, width)] += adjoint


def observe(ext_rows, operator, indices, values, weights, counts, members):
    rows, cells = ext_rows.shape
    obs_blocks = operator.shape[0]
    width = GROUP_SITE_SPAN
    fields = values.shape[0]
    steps = obs_blocks // BLOCKS_PER_STEP
    span = BLOCKS_PER_STEP * width
    grid_spec = pltpu.PrefetchScalarGridSpec(
        num_scalar_prefetch=2,
        grid=(steps,),
        in_specs=[
            pl.BlockSpec((rows, cells), lambda g, i, c: (0, 0)),
            pl.BlockSpec((BLOCKS_PER_STEP, width, width), lambda g, i, c: (g, 0, 0)),
            pl.BlockSpec((fields, span), lambda g, i, c: (0, g)),
            pl.BlockSpec((fields, span), lambda g, i, c: (0, g)),
        ],
        out_specs=pl.BlockSpec((rows, cells), lambda g, i, c: (0, 0)),
    )
    flops = 4 * obs_blocks * rows * width * width
    bytes_accessed = operator.size * 2 + ext_rows.size * 2 + rows * cells * 4 + values.size * 4
    return pl.pallas_call(
        lambda *refs: observe_kernel(members, *refs),
        grid_spec=grid_spec,
        out_shape=jax.ShapeDtypeStruct((rows, cells), jnp.float32),
        compiler_params=pltpu.CompilerParams(dimension_semantics=("arbitrary",)),
        cost_estimate=pl.CostEstimate(
            flops=flops, bytes_accessed=bytes_accessed, transcendentals=0
        ),
    )(indices, counts, ext_rows, operator, values, weights)


def body(hindcast_archive, op_blocks, block_index, obs_values, obs_weights, obs_counts):
    rim = EDGE * GROUP_SITE_SPAN
    space = lax.axis_size("space")
    ring = lax.axis_size("tq")
    here = lax.axis_index("tq")
    own = hindcast_archive[0]
    leads, members, fields, cells = own.shape
    low = lax.ppermute(own[..., cells - rim:], "space", ring_pairs(space, 1))
    high = lax.ppermute(own[..., :rim], "space", ring_pairs(space, -1))
    extended = jnp.concatenate([low, own, high], axis=-1)
    extended = jnp.transpose(extended, (0, 2, 1, 3))
    outgoing = jnp.roll(extended, here, axis=0)
    incoming = lax.all_to_all(outgoing, "tq", 0, 0, tiled=True)
    width = cells + 2 * rim
    adjoint_rows = observe(
        incoming.reshape(leads * fields * members, width),
        op_blocks[0],
        block_index[0],
        obs_values[0],
        obs_weights[0],
        obs_counts[0],
        members,
    )
    summed = lax.psum_scatter(
        adjoint_rows.reshape(ring, fields * members, width), "tq", scatter_dimension=0, tiled=True
    )[0]
    from_above = lax.ppermute(summed[:, :rim], "space", ring_pairs(space, -1))
    from_below = lax.ppermute(summed[:, width - rim:], "space", ring_pairs(space, 1))
    interior = summed[:, rim:width - rim]
    interior = interior.at[:, cells - rim:].add(from_above)
    interior = interior.at[:, :rim].add(from_below)
    gradient = jnp.transpose(interior.reshape(fields, members, cells), (1, 0, 2))
    return gradient[None]


def solution(mesh):
    tm_size = mesh.shape["tm"]
    lead_count = 4
    devices = mesh.devices.reshape(lead_count, tm_size // lead_count, mesh.shape["space"])
    ring_mesh = Mesh(devices, ("tq", "tr", "space"))
    tm = ("tq", "tr")
    in_specs = (
        P(tm, None, None, None, "space"),
        P(tm, "space", None, None),
        P(tm, "space"),
        P(tm, None, "space"),
        P(tm, None, "space"),
        P(tm, "space"),
    )
    out_specs = P(tm, None, None, "space")
    return jax.shard_map(body, mesh=ring_mesh, in_specs=in_specs, out_specs=out_specs, check_vma=False)
```

time: 108 us -> 136 us (1.26)
  the two profiles are of different devices: /device:TPU:64 before, /device:TPU:1 now
where the time goes in v2:
time: 136 us
  waiting for transfers between devices  69.7 us (51%)
  starting transfers between devices  28.8 us (21%)
  between operations  14.1 us (10%)
  Pallas kernels  12.9 us (9%)
  other arithmetic  5.42 us (4%)
  local copies, waits for them, and re-layouts  4.83 us (4%)
    reduce_scatter x1, waiting for transfers between devices, body(): lax.psum_scatter(adjoint_rows.reshape(ring, fields * members, width), 'tq...  48.5 us
    all_to_all x1, waiting for transfers between devices, body(): incoming = lax.all_to_all(outgoing, 'tq', 0, 0, tiled=True)  13.7 us
    pallas_call x1, Pallas kernels, observe(): pl.pallas_call(lambda *refs: observe_kernel(members, *refs), grid_spec=gr...  12.9 us
    all_to_all x1, starting transfers between devices, body(): incoming = lax.all_to_all(outgoing, 'tq', 0, 0, tiled=True)  10.2 us
    ppermute x1, starting transfers between devices, body(): from_above = lax.ppermute(summed[:, :rim], 'space', ring_pairs(space, -1))  6.59 us
    ppermute x1, starting transfers between devices, body(): high = lax.ppermute(own[..., :rim], 'space', ring_pairs(space, -1))  6.01 us
    ppermute x1, waiting for transfers between devices, body(): lax.ppermute(summed[:, width - rim:], 'space', ring_pairs(space, 1))  5.54 us
    ppermute x1, starting transfers between devices, body(): low = lax.ppermute(own[..., cells - rim:], 'space', ring_pairs(space, 1))  4.03 us
  transfers between devices with their start and end apart: 6, of which 5 were waited for; matrix products, arithmetic and copies ran while one was open for 2% of the time, Pallas kernels for 0%

profile of v2, /device:TPU:1, one launch (start us, length us, event | category | flops | bytes accessed | tf_op | source)
XLA Modules:
  0.0 135.7 jit_solution(3684476192362542838)
XLA Ops:
  6.5 1.1 fusion.3
  7.6 4.0 %collective-permute-start = (bf16[4,16,4,256]{3,2,1,0:T(4,128)(2,1)S(1)}, bf16[4,16,4,256]{3,2,1,0:T(4,128)(2,1)S(1)}, u32[]{:S(2)}, u32[]{:S(2)}) collective-permute-start(bf16[4,16,4,256]{3,2,1,0:T(4,128)(2,1)S(1)} %get-tuple-element.29), channel_id=1, source_target_pairs={{0,1},{1,2},{2,3},{3,4},{4,5},{5,6},{6,7},{7,8},{8,9},{9,10},{10,1... | collective-permute-start | bytes 393224 | tf_op jit(solution)/shard_map/ppermute | solution.py:85
  11.6 6.0 %collective-permute-start.1 = (bf16[4,16,4,256]{3,2,1,0:T(4,128)(2,1)S(1)}, bf16[4,16,4,256]{3,2,1,0:T(4,128)(2,1)S(1)}, u32[]{:S(2)}, u32[]{:S(2)}) collective-permute-start(bf16[4,16,4,256]{3,2,1,0:T(4,128)(2,1)S(1)} %get-tuple-element.30), channel_id=1, source_target_pairs={{0,31},{1,0},{2,1},{3,2},{4,3},{5,4},{6,5},{7,6},{8,7},{9,8},{10,9... | collective-permute-start | bytes 393224 | tf_op jit(solution)/shard_map/ppermute | solution.py:86
  17.7 0.4 collective-permute-done
  18.1 1.5 %collective-permute-done.1 = bf16[4,16,4,256]{3,2,1,0:T(4,128)(2,1)S(1)} collective-permute-done((bf16[4,16,4,256]{3,2,1,0:T(4,128)(2,1)S(1)}, bf16[4,16,4,256]{3,2,1,0:T(4,128)(2,1)S(1)}, u32[]{:S(2)}, u32[]{:S(2)}) %collective-permute-start.1) | collective-permute-done | bytes 131104 | tf_op jit(solution)/shard_map/ppermute | solution.py:86
  19.6 1.4 %maximum_bitcast_fusion = bf16[4,4,16,1536]{3,1,2,0:T(4,128)(2,1)S(1)} fusion(bf16[4,16,4,256]{3,2,1,0:T(4,128)(2,1)S(1)} %collective-permute-done.1, bf16[4,16,4,1024]{3,2,1,0:T(4,128)(2,1)} %bitcast.20, bf16[4,16,4,256]{3,2,1,0:T(4,128)(2,1)S(1)} %collective-permute-done), kind=kLoop, calls=%fused_computation.3 | loop fusion | flops 2359296 | bytes 1572864 | tf_op jit(solution)/shard_map/transpose | solution.py:88
  21.0 1.9 %fusion = bf16[4,4,16,1536]{3,1,2,0:T(4,128)(2,1)} fusion(s32[]{:T(128)S(6)} %select_n.14, bf16[4,4,16,1536]{3,1,2,0:T(4,128)(2,1)S(1)} %maximum_bitcast_fusion), kind=kLoop, calls=%fused_computation.2 | loop fusion | flops 393216 | bytes 1572868 | tf_op jit(solution)/shard_map/jit(_roll_dynamic)/concatenate | solution.py:89
  22.8 10.2 %all-to-all-start = ((bf16[4,4,16,1536]{3,1,2,0:T(4,128)(2,1)}), bf16[4,4,16,1536]{3,1,2,0:T(4,128)(2,1)S(1)}, u32[]{:S(2)}, u32[]{:S(2)}) async-start(bf16[4,4,16,1536]{3,1,2,0:T(4,128)(2,1)} %fusion), calls=%async_computation | async-start | bytes 1572864 | tf_op jit(solution)/shard_map/all_to_all | solution.py:90
  33.1 0.0 reduce-scatter.2.cloned.1.call-start
  33.7 13.7 %all-to-all-done = bf16[4,4,16,1536]{3,1,2,0:T(4,128)(2,1)S(1)} async-done(((bf16[4,4,16,1536]{3,1,2,0:T(4,128)(2,1)}), bf16[4,4,16,1536]{3,1,2,0:T(4,128)(2,1)S(1)}, u32[]{:S(2)}, u32[]{:S(2)}) %all-to-all-start) | async-done | bytes 786464 | tf_op jit(solution)/shard_map/all_to_all | solution.py:90
  47.5 1.0 copy.8
  48.5 12.9 %shard_map.64 = f32[256,1536]{1,0:T(8,128)} custom-call(s32[96]{0:T(128)} %bitcast.28, s32[1]{0:T(128)} %bitcast.16.refs_1_, bf16[256,1536]{1,0:T(8,128)(2,1)} %bitcast.21, bf16[96,128,128]{2,1,0:T(8,128)(2,1)} %bitcast.25, bf16[4,12288]{1,0:T(4,128)(2,1)} %bitcast.26, bf16[4,12288]{1,0:T(4,128)(2,1)} %bitcast.27), custom_call_target="tpu_custom_call" | custom-call | flops 1610612736 | bytes 5701632 | tf_op jit(solution)/shard_map/pallas_call | solution.py:67
  61.4 0.0 reduce-scatter.2.cloned.1.call-update
  61.4 48.5 %reduce-scatter.2.cloned.1.call-done = f32[1,64,1536]{2,1,0:T(8,128)} async-done(((f32[4,64,1536]{2,1,0:T(8,128)}), f32[1,64,1536]{2,1,0:T(8,128)}) %reduce-scatter.2.cloned.1.call-update) | async-done | bytes 393232 | tf_op jit(solution)/shard_map/reduce_scatter | solution.py:101
  109.9 0.9 fusion.4
  110.8 6.6 %collective-permute-start.2 = (f32[64,256]{1,0:T(8,128)S(1)}, f32[64,256]{1,0:T(8,128)S(1)}, u32[]{:S(2)}, u32[]{:S(2)}) collective-permute-start(f32[64,256]{1,0:T(8,128)S(1)} %get-tuple-element.32), channel_id=1, source_target_pairs={{0,31},{1,0},{2,1},{3,2},{4,3},{5,4},{6,5},{7,6},{8,7},{9,8},{10,9... | collective-permute-start | bytes 196616 | tf_op jit(solution)/shard_map/ppermute | solution.py:104
  117.4 0.6 compare_reduce_fusion
  118.1 1.0 slice.63
  119.0 1.9 %collective-permute-start.3 = (f32[64,256]{1,0:T(8,128)S(1)}, f32[64,256]{1,0:T(8,128)S(1)}, u32[]{:S(2)}, u32[]{:S(2)}) collective-permute-start(f32[64,256]{1,0:T(8,128)S(1)} %get-tuple-element.31), channel_id=1, source_target_pairs={{0,1},{1,2},{2,3},{3,4},{4,5},{5,6},{6,7},{7,8},{8,9},{9,10},{10,1... | collective-permute-start | bytes 196616 | tf_op jit(solution)/shard_map/ppermute | solution.py:105
  121.0 0.0 collective-permute-done.2
  121.0 0.9 fusion.2
  121.8 5.5 %collective-permute-done.3 = f32[64,256]{1,0:T(8,128)S(1)} collective-permute-done((f32[64,256]{1,0:T(8,128)S(1)}, f32[64,256]{1,0:T(8,128)S(1)}, u32[]{:S(2)}, u32[]{:S(2)}) %collective-permute-start.3) | collective-permute-done | bytes 65568 | tf_op jit(solution)/shard_map/ppermute | solution.py:105
  127.4 0.7 fusion.1
  128.0 0.9 copy.9
Async XLA Ops:
  7.6 10.5 %collective-permute-start = (bf16[4,16,4,256]{3,2,1,0:T(4,128)(2,1)S(1)}, bf16[4,16,4,256]{3,2,1,0:T(4,128)(2,1)S(1)}, u32[]{:S(2)}, u32[]{:S(2)}) collective-permute-start(bf16[4,16,4,256]{3,2,1,0:T(4,128)(2,1)S(1)} %get-tuple-element.29), channel_id=1, source_target_pairs={{0,1},{1,2},{2,3},{3,4},{4,5},{5,6},{6,7},{7,8},{8,9},{9,10},{10,1... | collective-permute-start | bytes 393224 | tf_op jit(solution)/shard_map/ppermute | solution.py:85
  11.6 7.9 %collective-permute-start.1 = (bf16[4,16,4,256]{3,2,1,0:T(4,128)(2,1)S(1)}, bf16[4,16,4,256]{3,2,1,0:T(4,128)(2,1)S(1)}, u32[]{:S(2)}, u32[]{:S(2)}) collective-permute-start(bf16[4,16,4,256]{3,2,1,0:T(4,128)(2,1)S(1)} %get-tuple-element.30), channel_id=1, source_target_pairs={{0,31},{1,0},{2,1},{3,2},{4,3},{5,4},{6,5},{7,6},{8,7},{9,8},{10,9... | collective-permute-start | bytes 393224 | tf_op jit(solution)/shard_map/ppermute | solution.py:86
  22.8 24.6 %all-to-all-start = ((bf16[4,4,16,1536]{3,1,2,0:T(4,128)(2,1)}), bf16[4,4,16,1536]{3,1,2,0:T(4,128)(2,1)S(1)}, u32[]{:S(2)}, u32[]{:S(2)}) async-start(bf16[4,4,16,1536]{3,1,2,0:T(4,128)(2,1)} %fusion), calls=%async_computation | async-start | bytes 1572864 | tf_op jit(solution)/shard_map/all_to_all | solution.py:90
  33.1 76.9 %reduce-scatter.2.cloned.1.call-start = ((), (), s32[]{:S(2)}) async-start(), calls=%async_computation.2 | async-start | bytes 1966080 | tf_op jit(solution)/shard_map/reduce_scatter | solution.py:101
  110.8 10.1 %collective-permute-start.2 = (f32[64,256]{1,0:T(8,128)S(1)}, f32[64,256]{1,0:T(8,128)S(1)}, u32[]{:S(2)}, u32[]{:S(2)}) collective-permute-start(f32[64,256]{1,0:T(8,128)S(1)} %get-tuple-element.32), channel_id=1, source_target_pairs={{0,31},{1,0},{2,1},{3,2},{4,3},{5,4},{6,5},{7,6},{8,7},{9,8},{10,9... | collective-permute-start | bytes 196616 | tf_op jit(solution)/shard_map/ppermute | solution.py:104
  119.0 8.3 %collective-permute-start.3 = (f32[64,256]{1,0:T(8,128)S(1)}, f32[64,256]{1,0:T(8,128)S(1)}, u32[]{:S(2)}, u32[]{:S(2)}) collective-permute-start(f32[64,256]{1,0:T(8,128)S(1)} %get-tuple-element.31), channel_id=1, source_target_pairs={{0,1},{1,2},{2,3},{3,4},{4,5},{5,6},{6,7},{7,8},{8,9},{9,10},{10,1... | collective-permute-start | bytes 196616 | tf_op jit(solution)/shard_map/ppermute | solution.py:105
Sparse Core Ops, SparseCore 0:
  61.5 48.3 reduce-scatter.1

commit v3 on v1

--- a/solution.py
+++ b/solution.py
@@ -9,7 +9,7 @@
 
 GROUP_SITE_SPAN = 128
 EDGE = 2
-BLOCKS_PER_STEP = 8
+BLOCKS_PER_STEP = 16
 
 
 def with_halo(block, sides, width):
@@ -47,23 +47,35 @@
         out_ref[...] = jnp.zeros_like(out_ref)
 
     count = cnt_ref[0]
-    lane = lax.broadcasted_iota(jnp.int32, (1, 1, width), 2)
-    for k in range(BLOCKS_PER_STEP):
+    pair = 2 * width
+    lane = lax.broadcasted_iota(jnp.int32, (1, 1, pair), 2)
+    zero = jnp.zeros((width, width), op_ref.dtype)
+    for k in range(0, BLOCKS_PER_STEP, 2):
         b = step * BLOCKS_PER_STEP + k
-        start = pl.multiple_of(idx_ref[b] * width, width)
-        x = ext_ref[:, pl.ds(start, width)]
-        op = op_ref[k]
+        first = pl.multiple_of(idx_ref[b] * width, width)
+        second = pl.multiple_of(idx_ref[b + 1] * width, width)
+        x = jnp.concatenate(
+            [ext_ref[:, pl.ds(first, width)], ext_ref[:, pl.ds(second, width)]], axis=1
+        )
+        op = jnp.concatenate(
+            [
+                jnp.concatenate([op_ref[k], zero], axis=1),
+                jnp.concatenate([zero, op_ref[k + 1]], axis=1),
+            ],
+            axis=0,
+        )
         images = lax.dot_general(
             x, op, (((1,), (1,)), ((), ())), preferred_element_type=jnp.float32
-        ).reshape(fields, rows // fields, width)
-        observed = val_ref[:, k * width:(k + 1) * width].astype(jnp.float32)[:, None, :]
-        scaling = wt_ref[:, k * width:(k + 1) * width].astype(jnp.float32)[:, None, :]
+        ).reshape(fields, rows // fields, pair)
+        observed = val_ref[:, k * width:k * width + pair].astype(jnp.float32)[:, None, :]
+        scaling = wt_ref[:, k * width:k * width + pair].astype(jnp.float32)[:, None, :]
         live = (b * width + lane) < count
         misfit = jnp.where(live, (images - observed) * scaling, 0.0).astype(jnp.bfloat16)
         adjoint = jnp.dot(
-            misfit.reshape(rows, width), op, preferred_element_type=jnp.float32
+            misfit.reshape(rows, pair), op, preferred_element_type=jnp.float32
         )
-        out_ref[:, pl.ds(start, width)] += adjoint
+        out_ref[:, pl.ds(first, width)] += adjoint[:, :width]
+        out_ref[:, pl.ds(second, width)] += adjoint[:, width:]
 
 
 def observe(ext_rows, operator, indices, values, weights, counts):

time: 108 us -> 104 us (0.963)
  Pallas kernels: 12.9 us -> 9.86 us
    pallas_call x1, Pallas kernels: 12.9 us -> 9.86 us  [observe(): pl.pallas_call(observe_kernel, grid_spec=grid_spec, out_shape=jax.ShapeDt...]
where the time goes in v3:
time: 104 us
  starting transfers between devices  46.9 us (45%)
  waiting for transfers between devices  40 us (38%)
  Pallas kernels  9.86 us (9%)
  local copies, waits for them, and re-layouts  4.95 us (5%)
  other arithmetic  1.53 us (1%)
    ppermute x8, waiting for transfers between devices, passed_along(): return lax.ppermute(value, axis, pairs)  37.8 us
    ppermute x8, starting transfers between devices, passed_along(): return lax.ppermute(value, axis, pairs)  37.4 us
    pallas_call x1, Pallas kernels, observe(): pl.pallas_call(observe_kernel, grid_spec=grid_spec, out_shape=jax.ShapeDt...  9.86 us
    ppermute x1, starting transfers between devices, with_halo(): lax.ppermute(lax.slice_in_dim(block, 0, width, axis=dim), axis, backward)  6.01 us
    ppermute x1, starting transfers between devices, with_halo(): lax.ppermute(lax.slice_in_dim(block, block.shape[dim] - width, None, axis...  3.48 us
    reshape x1, local copies, waits for them, and re-layouts, body(): adjoint_rows.reshape(fields, leads, members, cells)  2.42 us
  transfers between devices with their start and end apart: 10, of which 8 were waited for; matrix products, arithmetic and copies ran while one was open for 0% of the time, Pallas kernels for 0%

profile of v3, /device:TPU:64, one launch (start us, length us, event | category | flops | bytes accessed | tf_op | source)
XLA Modules:
  0.0 104.0 jit_solution(360067630611582251)
XLA Ops:
  0.0 1.3 %fusion.6 = (bf16[1,1,16,4,1024]{4,3,2,1,0:T(4,128)(2,1)S(1)}, bf16[1,16,4,1024]{3,2,1,0:T(4,128)(2,1)S(1)}, bf16[1,16,4,1024]{3,2,1,0:T(4,128)(2,1)S(1)}, bf16[1,16,4,1024]{3,2,1,0:T(4,128)(2,1)S(1)}) fusion(bf16[1,4,16,4,1024]{4,3,2,1,0:T(4,128)(2,1)} %param.10), kind=kLoop, calls=%fused_computation.21 | loop fusion | bytes 1048576 | tf_op jit(solution)/shard_map/slice | solution.py:126
  1.3 6.1 %collective-permute-start = (bf16[1,16,4,1024]{3,2,1,0:T(4,128)(2,1)S(1)}, bf16[1,16,4,1024]{3,2,1,0:T(4,128)(2,1)S(1)}, u32[]{:S(2)}, u32[]{:S(2)}) collective-permute-start(bf16[1,16,4,1024]{3,2,1,0:T(4,128)(2,1)S(1)} %get-tuple-element.37), channel_id=1, source_target_pairs={{0,128},{32,160},{64,192},{96,224},{128,256},{160,288},{192,320},{... | collective-permute-start | bytes 393224 | tf_op jit(solution)/shard_map/ppermute | solution.py:32
  7.4 5.9 %collective-permute-start.2 = (bf16[1,16,4,1024]{3,2,1,0:T(4,128)(2,1)S(1)}, bf16[1,16,4,1024]{3,2,1,0:T(4,128)(2,1)S(1)}, u32[]{:S(2)}, u32[]{:S(2)}) collective-permute-start(bf16[1,16,4,1024]{3,2,1,0:T(4,128)(2,1)S(1)} %get-tuple-element.38), channel_id=1, source_target_pairs={{0,384},{32,416},{64,448},{96,480},{128,0},{160,32},{192,64},{224,... | collective-permute-start | bytes 393224 | tf_op jit(solution)/shard_map/ppermute | solution.py:32
  13.3 6.0 %collective-permute-start.1 = (bf16[1,16,4,1024]{3,2,1,0:T(4,128)(2,1)S(1)}, bf16[1,16,4,1024]{3,2,1,0:T(4,128)(2,1)S(1)}, u32[]{:S(2)}, u32[]{:S(2)}) collective-permute-start(bf16[1,16,4,1024]{3,2,1,0:T(4,128)(2,1)S(1)} %get-tuple-element.39), channel_id=1, source_target_pairs={{0,256},{32,288},{64,320},{96,352},{128,384},{160,416},{192,448},{... | collective-permute-start | bytes 393224 | tf_op jit(solution)/shard_map/ppermute | solution.py:32
  19.3 0.0 collective-permute-done
  19.3 0.5 collective-permute-done.2
  19.8 8.6 %collective-permute-done.1 = bf16[1,16,4,1024]{3,2,1,0:T(4,128)(2,1)S(1)} collective-permute-done((bf16[1,16,4,1024]{3,2,1,0:T(4,128)(2,1)S(1)}, bf16[1,16,4,1024]{3,2,1,0:T(4,128)(2,1)S(1)}, u32[]{:S(2)}, u32[]{:S(2)}) %collective-permute-start.1) | collective-permute-done | bytes 131104 | tf_op jit(solution)/shard_map/ppermute | solution.py:32
  28.4 0.1 pad_maximum_fusion.3
  28.5 3.5 %collective-permute-start.3 = (bf16[1,4,16,4,256]{4,3,2,1,0:T(4,128)(2,1)S(1)}, bf16[1,4,16,4,256]{4,3,2,1,0:T(4,128)(2,1)S(1)}, u32[]{:S(2)}, u32[]{:S(2)}) collective-permute-start(bf16[1,4,16,4,256]{4,3,2,1,0:T(4,128)(2,1)S(1)} %get-tuple-element.34), channel_id=1, source_target_pairs={{0,1},{1,2},{2,3},{3,4},{4,5},{5,6},{6,7},{7,8},{8,9},{9,10},{10,1... | collective-permute-start | bytes 393224 | tf_op jit(solution)/shard_map/ppermute | solution.py:21
  32.0 6.0 %collective-permute-start.4 = (bf16[1,4,16,4,256]{4,3,2,1,0:T(4,128)(2,1)S(1)}, bf16[1,4,16,4,256]{4,3,2,1,0:T(4,128)(2,1)S(1)}, u32[]{:S(2)}, u32[]{:S(2)}) collective-permute-start(bf16[1,4,16,4,256]{4,3,2,1,0:T(4,128)(2,1)S(1)} %get-tuple-element.35), channel_id=1, source_target_pairs={{1,0},{2,1},{3,2},{4,3},{5,4},{6,5},{7,6},{8,7},{9,8},{10,9},{11,1... | collective-permute-start | bytes 393224 | tf_op jit(solution)/shard_map/ppermute | solution.py:24
  38.7 1.1 %collective-permute-done.3 = bf16[1,4,16,4,256]{4,3,2,1,0:T(4,128)(2,1)S(1)} collective-permute-done((bf16[1,4,16,4,256]{4,3,2,1,0:T(4,128)(2,1)S(1)}, bf16[1,4,16,4,256]{4,3,2,1,0:T(4,128)(2,1)S(1)}, u32[]{:S(2)}, u32[]{:S(2)}) %collective-permute-start.3) | collective-permute-done | bytes 131104 | tf_op jit(solution)/shard_map/ppermute | solution.py:21
  39.7 1.2 %collective-permute-done.4 = bf16[1,4,16,4,256]{4,3,2,1,0:T(4,128)(2,1)S(1)} collective-permute-done((bf16[1,4,16,4,256]{4,3,2,1,0:T(4,128)(2,1)S(1)}, bf16[1,4,16,4,256]{4,3,2,1,0:T(4,128)(2,1)S(1)}, u32[]{:S(2)}, u32[]{:S(2)}) %collective-permute-start.4) | collective-permute-done | bytes 131104 | tf_op jit(solution)/shard_map/ppermute | solution.py:24
  40.9 0.3 maximum_bitcast_fusion
  41.3 1.0 copy.7
  42.3 9.9 %shard_map.64 = f32[256,1536]{1,0:T(8,128)} custom-call(s32[96]{0:T(128)} %bitcast.54, s32[1]{0:T(128)} %bitcast.39.cnt_ref, bf16[256,1536]{1,0:T(8,128)(2,1)} %bitcast.44, bf16[96,128,128]{2,1,0:T(8,128)(2,1)} %bitcast.51, bf16[4,12288]{1,0:T(4,128)(2,1)} %bitcast.52, bf16[4,12288]{1,0:T(4,128)(2,1)} %bitcast.53), custom_call_target="tpu_custom_call" | custom-call | flops 1610612736 | bytes 5701632 | tf_op jit(solution)/shard_map/pallas_call | solution.py:101
  52.1 2.4 %copy.10 = f32[4,4,16,1536]{3,0,2,1:T(4,128)S(1)} copy(f32[4,4,16,1536]{3,2,1,0:T(8,128)} %bitcast.43) | data formatting | bytes 3145728 | tf_op jit(solution)/shard_map/reshape | solution.py:140
  54.6 7.7 %collective-permute-start.5 = (f32[1,4,16,4,256]{4,3,2,1,0:T(4,128)S(1)}, f32[1,4,16,4,256]{4,3,2,1,0:T(4,128)S(1)}, u32[]{:S(2)}, u32[]{:S(2)}) collective-permute-start(f32[1,4,16,4,256]{4,3,2,1,0:T(4,128)S(1)} %get-tuple-element.30), channel_id=1, source_target_pairs={{0,31},{1,0},{2,1},{3,2},{4,3},{5,4},{6,5},{7,6},{8,7},{9,8},{10,9... | collective-permute-start | bytes 786440 | tf_op jit(solution)/shard_map/ppermute | solution.py:32
  62.3 1.9 %collective-permute-start.6 = (f32[1,4,16,4,256]{4,3,2,1,0:T(4,128)S(1)}, f32[1,4,16,4,256]{4,3,2,1,0:T(4,128)S(1)}, u32[]{:S(2)}, u32[]{:S(2)}) collective-permute-start(f32[1,4,16,4,256]{4,3,2,1,0:T(4,128)S(1)} %get-tuple-element.29), channel_id=1, source_target_pairs={{0,1},{1,2},{2,3},{3,4},{4,5},{5,6},{6,7},{7,8},{8,9},{9,10},{10,1... | collective-permute-start | bytes 786440 | tf_op jit(solution)/shard_map/ppermute | solution.py:32
  64.3 0.1 slice.123
  64.4 2.8 %collective-permute-done.5 = f32[1,4,16,4,256]{4,3,2,1,0:T(4,128)S(1)} collective-permute-done((f32[1,4,16,4,256]{4,3,2,1,0:T(4,128)S(1)}, f32[1,4,16,4,256]{4,3,2,1,0:T(4,128)S(1)}, u32[]{:S(2)}, u32[]{:S(2)}) %collective-permute-start.5) | collective-permute-done | bytes 262176 | tf_op jit(solution)/shard_map/ppermute | solution.py:32
  67.2 0.1 fusion.4
  67.3 7.3 %collective-permute-done.6 = f32[1,4,16,4,256]{4,3,2,1,0:T(4,128)S(1)} collective-permute-done((f32[1,4,16,4,256]{4,3,2,1,0:T(4,128)S(1)}, f32[1,4,16,4,256]{4,3,2,1,0:T(4,128)S(1)}, u32[]{:S(2)}, u32[]{:S(2)}) %collective-permute-start.6) | collective-permute-done | bytes 262176 | tf_op jit(solution)/shard_map/ppermute | solution.py:32
  74.6 0.1 fusion.3
  74.7 0.1 slice_bitcast_fusion.2
  74.8 1.9 %collective-permute-start.7 = (f32[1,16,4,1024]{3,2,1,0:T(4,128)S(1)}, f32[1,16,4,1024]{3,2,1,0:T(4,128)S(1)}, u32[]{:S(2)}, u32[]{:S(2)}) collective-permute-start(f32[1,16,4,1024]{3,2,1,0:T(4,128)S(1)} %get-tuple-element.31), channel_id=1, source_target_pairs={{0,384},{32,416},{64,448},{96,480},{128,0},{160,32},{192,64},{224,... | collective-permute-start | bytes 786440 | tf_op jit(solution)/shard_map/ppermute | solution.py:32
  76.7 4.8 %collective-permute-start.9 = (f32[1,16,4,1024]{3,2,1,0:T(4,128)S(1)}, f32[1,16,4,1024]{3,2,1,0:T(4,128)S(1)}, u32[]{:S(2)}, u32[]{:S(2)}) collective-permute-start(f32[1,16,4,1024]{3,2,1,0:T(4,128)S(1)} %get-tuple-element.32), channel_id=1, source_target_pairs={{0,128},{32,160},{64,192},{96,224},{128,256},{160,288},{192,320},{... | collective-permute-start | bytes 786440 | tf_op jit(solution)/shard_map/ppermute | solution.py:32
  81.5 3.0 %collective-permute-start.8 = (f32[1,16,4,1024]{3,2,1,0:T(4,128)S(1)}, f32[1,16,4,1024]{3,2,1,0:T(4,128)S(1)}, u32[]{:S(2)}, u32[]{:S(2)}) collective-permute-start(f32[1,16,4,1024]{3,2,1,0:T(4,128)S(1)} %get-tuple-element.33), channel_id=1, source_target_pairs={{0,256},{32,288},{64,320},{96,352},{128,384},{160,416},{192,448},{... | collective-permute-start | bytes 786440 | tf_op jit(solution)/shard_map/ppermute | solution.py:32
  84.6 3.5 %collective-permute-done.7 = f32[1,16,4,1024]{3,2,1,0:T(4,128)S(1)} collective-permute-done((f32[1,16,4,1024]{3,2,1,0:T(4,128)S(1)}, f32[1,16,4,1024]{3,2,1,0:T(4,128)S(1)}, u32[]{:S(2)}, u32[]{:S(2)}) %collective-permute-start.7) | collective-permute-done | bytes 262176 | tf_op jit(solution)/shard_map/ppermute | solution.py:32
  88.1 15.1 %collective-permute-done.9 = f32[1,16,4,1024]{3,2,1,0:T(4,128)S(1)} collective-permute-done((f32[1,16,4,1024]{3,2,1,0:T(4,128)S(1)}, f32[1,16,4,1024]{3,2,1,0:T(4,128)S(1)}, u32[]{:S(2)}, u32[]{:S(2)}) %collective-permute-start.9) | collective-permute-done | bytes 262176 | tf_op jit(solution)/shard_map/ppermute | solution.py:32
  103.2 0.0 collective-permute-done.8
  103.2 0.9 fusion.2
  (1 shorter events, 0.0 us)
Async XLA Ops:
  1.3 18.0 %collective-permute-start = (bf16[1,16,4,1024]{3,2,1,0:T(4,128)(2,1)S(1)}, bf16[1,16,4,1024]{3,2,1,0:T(4,128)(2,1)S(1)}, u32[]{:S(2)}, u32[]{:S(2)}) collective-permute-start(bf16[1,16,4,1024]{3,2,1,0:T(4,128)(2,1)S(1)} %get-tuple-element.37), channel_id=1, source_target_pairs={{0,128},{32,160},{64,192},{96,224},{128,256},{160,288},{192,320},{... | collective-permute-start | bytes 393224 | tf_op jit(solution)/shard_map/ppermute | solution.py:32
  7.4 12.4 %collective-permute-start.2 = (bf16[1,16,4,1024]{3,2,1,0:T(4,128)(2,1)S(1)}, bf16[1,16,4,1024]{3,2,1,0:T(4,128)(2,1)S(1)}, u32[]{:S(2)}, u32[]{:S(2)}) collective-permute-start(bf16[1,16,4,1024]{3,2,1,0:T(4,128)(2,1)S(1)} %get-tuple-element.38), channel_id=1, source_target_pairs={{0,384},{32,416},{64,448},{96,480},{128,0},{160,32},{192,64},{224,... | collective-permute-start | bytes 393224 | tf_op jit(solution)/shard_map/ppermute | solution.py:32
  13.3 15.1 %collective-permute-start.1 = (bf16[1,16,4,1024]{3,2,1,0:T(4,128)(2,1)S(1)}, bf16[1,16,4,1024]{3,2,1,0:T(4,128)(2,1)S(1)}, u32[]{:S(2)}, u32[]{:S(2)}) collective-permute-start(bf16[1,16,4,1024]{3,2,1,0:T(4,128)(2,1)S(1)} %get-tuple-element.39), channel_id=1, source_target_pairs={{0,256},{32,288},{64,320},{96,352},{128,384},{160,416},{192,448},{... | collective-permute-start | bytes 393224 | tf_op jit(solution)/shard_map/ppermute | solution.py:32
  28.5 11.2 %collective-permute-start.3 = (bf16[1,4,16,4,256]{4,3,2,1,0:T(4,128)(2,1)S(1)}, bf16[1,4,16,4,256]{4,3,2,1,0:T(4,128)(2,1)S(1)}, u32[]{:S(2)}, u32[]{:S(2)}) collective-permute-start(bf16[1,4,16,4,256]{4,3,2,1,0:T(4,128)(2,1)S(1)} %get-tuple-element.34), channel_id=1, source_target_pairs={{0,1},{1,2},{2,3},{3,4},{4,5},{5,6},{6,7},{7,8},{8,9},{9,10},{10,1... | collective-permute-start | bytes 393224 | tf_op jit(solution)/shard_map/ppermute | solution.py:21
  32.0 8.9 %collective-permute-start.4 = (bf16[1,4,16,4,256]{4,3,2,1,0:T(4,128)(2,1)S(1)}, bf16[1,4,16,4,256]{4,3,2,1,0:T(4,128)(2,1)S(1)}, u32[]{:S(2)}, u32[]{:S(2)}) collective-permute-start(bf16[1,4,16,4,256]{4,3,2,1,0:T(4,128)(2,1)S(1)} %get-tuple-element.35), channel_id=1, source_target_pairs={{1,0},{2,1},{3,2},{4,3},{5,4},{6,5},{7,6},{8,7},{9,8},{10,9},{11,1... | collective-permute-start | bytes 393224 | tf_op jit(solution)/shard_map/ppermute | solution.py:24
  54.6 12.6 %collective-permute-start.5 = (f32[1,4,16,4,256]{4,3,2,1,0:T(4,128)S(1)}, f32[1,4,16,4,256]{4,3,2,1,0:T(4,128)S(1)}, u32[]{:S(2)}, u32[]{:S(2)}) collective-permute-start(f32[1,4,16,4,256]{4,3,2,1,0:T(4,128)S(1)} %get-tuple-element.30), channel_id=1, source_target_pairs={{0,31},{1,0},{2,1},{3,2},{4,3},{5,4},{6,5},{7,6},{8,7},{9,8},{10,9... | collective-permute-start | bytes 786440 | tf_op jit(solution)/shard_map/ppermute | solution.py:32
  62.3 12.3 %collective-permute-start.6 = (f32[1,4,16,4,256]{4,3,2,1,0:T(4,128)S(1)}, f32[1,4,16,4,256]{4,3,2,1,0:T(4,128)S(1)}, u32[]{:S(2)}, u32[]{:S(2)}) collective-permute-start(f32[1,4,16,4,256]{4,3,2,1,0:T(4,128)S(1)} %get-tuple-element.29), channel_id=1, source_target_pairs={{0,1},{1,2},{2,3},{3,4},{4,5},{5,6},{6,7},{7,8},{8,9},{9,10},{10,1... | collective-permute-start | bytes 786440 | tf_op jit(solution)/shard_map/ppermute | solution.py:32
  74.8 13.3 %collective-permute-start.7 = (f32[1,16,4,1024]{3,2,1,0:T(4,128)S(1)}, f32[1,16,4,1024]{3,2,1,0:T(4,128)S(1)}, u32[]{:S(2)}, u32[]{:S(2)}) collective-permute-start(f32[1,16,4,1024]{3,2,1,0:T(4,128)S(1)} %get-tuple-element.31), channel_id=1, source_target_pairs={{0,384},{32,416},{64,448},{96,480},{128,0},{160,32},{192,64},{224,... | collective-permute-start | bytes 786440 | tf_op jit(solution)/shard_map/ppermute | solution.py:32
  76.7 26.4 %collective-permute-start.9 = (f32[1,16,4,1024]{3,2,1,0:T(4,128)S(1)}, f32[1,16,4,1024]{3,2,1,0:T(4,128)S(1)}, u32[]{:S(2)}, u32[]{:S(2)}) collective-permute-start(f32[1,16,4,1024]{3,2,1,0:T(4,128)S(1)} %get-tuple-element.32), channel_id=1, source_target_pairs={{0,128},{32,160},{64,192},{96,224},{128,256},{160,288},{192,320},{... | collective-permute-start | bytes 786440 | tf_op jit(solution)/shard_map/ppermute | solution.py:32
  81.5 21.6 %collective-permute-start.8 = (f32[1,16,4,1024]{3,2,1,0:T(4,128)S(1)}, f32[1,16,4,1024]{3,2,1,0:T(4,128)S(1)}, u32[]{:S(2)}, u32[]{:S(2)}) collective-permute-start(f32[1,16,4,1024]{3,2,1,0:T(4,128)S(1)} %get-tuple-element.33), channel_id=1, source_target_pairs={{0,256},{32,288},{64,320},{96,352},{128,384},{160,416},{192,448},{... | collective-permute-start | bytes 786440 | tf_op jit(solution)/shard_map/ppermute | solution.py:32

commit v4 on v3

--- a/solution.py
+++ b/solution.py
@@ -48,6 +48,7 @@
 
     count = cnt_ref[0]
     pair = 2 * width
+    period = 8
     lane = lax.broadcasted_iota(jnp.int32, (1, 1, pair), 2)
     zero = jnp.zeros((width, width), op_ref.dtype)
     for k in range(0, BLOCKS_PER_STEP, 2):
@@ -66,9 +67,11 @@
         )
         images = lax.dot_general(
             x, op, (((1,), (1,)), ((), ())), preferred_element_type=jnp.float32
-        ).reshape(fields, rows // fields, pair)
-        observed = val_ref[:, k * width:k * width + pair].astype(jnp.float32)[:, None, :]
-        scaling = wt_ref[:, k * width:k * width + pair].astype(jnp.float32)[:, None, :]
+        ).reshape(rows // period, period, pair)
+        observed = val_ref[:, k * width:k * width + pair].astype(jnp.float32)
+        observed = jnp.concatenate([observed] * (period // fields), axis=0)[None]
+        scaling = wt_ref[:, k * width:k * width + pair].astype(jnp.float32)
+        scaling = jnp.concatenate([scaling] * (period // fields), axis=0)[None]
         live = (b * width + lane) < count
         misfit = jnp.where(live, (images - observed) * scaling, 0.0).astype(jnp.bfloat16)
         adjoint = jnp.dot(
@@ -132,13 +135,11 @@
         )
     extended = extend(jnp.stack(regrouped, axis=1))[0]
     leads, members, fields, cells = extended.shape
-    ext_rows = jnp.transpose(extended, (2, 0, 1, 3)).reshape(fields * leads * members, cells)
+    ext_rows = extended.reshape(leads * members * fields, cells)
     adjoint_rows = observe(
         ext_rows, op_blocks[0], block_index[0], obs_values[0], obs_weights[0], obs_counts[0]
     )
-    adjoint_ext = jnp.transpose(
-        adjoint_rows.reshape(fields, leads, members, cells), (1, 2, 0, 3)
-    )[None]
+    adjoint_ext = adjoint_rows.reshape(leads, members, fields, cells)[None]
     interior = settle(adjoint_ext)
     running = interior[:, 0]
     for horizon_step in range(1, lead_count):

time: 104 us -> 104 us (level)
    another operation x0 -> x2, local copies, waits for them, and re-layouts: none -> 2.82 us  [the longest x1 1.76 us: body(): adjoint_ext = adjoint_rows.reshape(leads, members, fields, cells)[None]]
    reshape x1 -> x0, local copies, waits for them, and re-layouts: 2.42 us -> none  [body(): adjoint_rows.reshape(fields, leads, members, cells)]
where the time goes in v4:
time: 104 us; the launch traced here: 103 us
  starting transfers between devices  46.9 us (45%)
  waiting for transfers between devices  40.1 us (39%)
  Pallas kernels  9.87 us (9%)
  local copies, waits for them, and re-layouts  4.3 us (4%)
  other arithmetic  1.51 us (1%)
    ppermute x8, waiting for transfers between devices, passed_along(): return lax.ppermute(value, axis, pairs)  37.9 us
    ppermute x8, starting transfers between devices, passed_along(): return lax.ppermute(value, axis, pairs)  37.4 us
    pallas_call x1, Pallas kernels, observe(): pl.pallas_call(observe_kernel, grid_spec=grid_spec, out_shape=jax.ShapeDt...  9.87 us
    ppermute x1, starting transfers between devices, with_halo(): lax.ppermute(lax.slice_in_dim(block, 0, width, axis=dim), axis, backward)  6.01 us
    ppermute x1, starting transfers between devices, with_halo(): lax.ppermute(lax.slice_in_dim(block, block.shape[dim] - width, None, axis...  3.48 us
  transfers between devices with their start and end apart: 10, of which 8 were waited for; matrix products, arithmetic and copies ran while one was open for 0% of the time, Pallas kernels for 0%

profile of v4, /device:TPU:64, one launch (start us, length us, event | category | flops | bytes accessed | tf_op | source)
XLA Modules:
  0.0 103.5 jit_solution(8711740957532101603)
XLA Ops:
  0.0 1.3 %fusion.6 = (bf16[1,1,16,4,1024]{4,3,2,1,0:T(4,128)(2,1)S(1)}, bf16[1,16,4,1024]{3,2,1,0:T(4,128)(2,1)S(1)}, bf16[1,16,4,1024]{3,2,1,0:T(4,128)(2,1)S(1)}, bf16[1,16,4,1024]{3,2,1,0:T(4,128)(2,1)S(1)}) fusion(bf16[1,4,16,4,1024]{4,3,2,1,0:T(4,128)(2,1)} %param.10), kind=kLoop, calls=%fused_computation.20 | loop fusion | bytes 1048576 | tf_op jit(solution)/shard_map/slice | solution.py:129
  1.3 6.1 %collective-permute-start = (bf16[1,16,4,1024]{3,2,1,0:T(4,128)(2,1)S(1)}, bf16[1,16,4,1024]{3,2,1,0:T(4,128)(2,1)S(1)}, u32[]{:S(2)}, u32[]{:S(2)}) collective-permute-start(bf16[1,16,4,1024]{3,2,1,0:T(4,128)(2,1)S(1)} %get-tuple-element.37), channel_id=1, source_target_pairs={{0,128},{32,160},{64,192},{96,224},{128,256},{160,288},{192,320},{... | collective-permute-start | bytes 393224 | tf_op jit(solution)/shard_map/ppermute | solution.py:32
  7.4 5.9 %collective-permute-start.2 = (bf16[1,16,4,1024]{3,2,1,0:T(4,128)(2,1)S(1)}, bf16[1,16,4,1024]{3,2,1,0:T(4,128)(2,1)S(1)}, u32[]{:S(2)}, u32[]{:S(2)}) collective-permute-start(bf16[1,16,4,1024]{3,2,1,0:T(4,128)(2,1)S(1)} %get-tuple-element.38), channel_id=1, source_target_pairs={{0,384},{32,416},{64,448},{96,480},{128,0},{160,32},{192,64},{224,... | collective-permute-start | bytes 393224 | tf_op jit(solution)/shard_map/ppermute | solution.py:32
  13.3 6.0 %collective-permute-start.1 = (bf16[1,16,4,1024]{3,2,1,0:T(4,128)(2,1)S(1)}, bf16[1,16,4,1024]{3,2,1,0:T(4,128)(2,1)S(1)}, u32[]{:S(2)}, u32[]{:S(2)}) collective-permute-start(bf16[1,16,4,1024]{3,2,1,0:T(4,128)(2,1)S(1)} %get-tuple-element.39), channel_id=1, source_target_pairs={{0,256},{32,288},{64,320},{96,352},{128,384},{160,416},{192,448},{... | collective-permute-start | bytes 393224 | tf_op jit(solution)/shard_map/ppermute | solution.py:32
  19.3 0.0 collective-permute-done
  19.3 0.5 collective-permute-done.2
  19.8 8.6 %collective-permute-done.1 = bf16[1,16,4,1024]{3,2,1,0:T(4,128)(2,1)S(1)} collective-permute-done((bf16[1,16,4,1024]{3,2,1,0:T(4,128)(2,1)S(1)}, bf16[1,16,4,1024]{3,2,1,0:T(4,128)(2,1)S(1)}, u32[]{:S(2)}, u32[]{:S(2)}) %collective-permute-start.1) | collective-permute-done | bytes 131104 | tf_op jit(solution)/shard_map/ppermute | solution.py:32
  28.4 0.1 pad_maximum_fusion.4
  28.5 3.5 %collective-permute-start.3 = (bf16[1,4,16,4,256]{4,3,2,1,0:T(4,128)(2,1)S(1)}, bf16[1,4,16,4,256]{4,3,2,1,0:T(4,128)(2,1)S(1)}, u32[]{:S(2)}, u32[]{:S(2)}) collective-permute-start(bf16[1,4,16,4,256]{4,3,2,1,0:T(4,128)(2,1)S(1)} %get-tuple-element.34), channel_id=1, source_target_pairs={{0,1},{1,2},{2,3},{3,4},{4,5},{5,6},{6,7},{7,8},{8,9},{9,10},{10,1... | collective-permute-start | bytes 393224 | tf_op jit(solution)/shard_map/ppermute | solution.py:21
  32.0 6.0 %collective-permute-start.4 = (bf16[1,4,16,4,256]{4,3,2,1,0:T(4,128)(2,1)S(1)}, bf16[1,4,16,4,256]{4,3,2,1,0:T(4,128)(2,1)S(1)}, u32[]{:S(2)}, u32[]{:S(2)}) collective-permute-start(bf16[1,4,16,4,256]{4,3,2,1,0:T(4,128)(2,1)S(1)} %get-tuple-element.35), channel_id=1, source_target_pairs={{1,0},{2,1},{3,2},{4,3},{5,4},{6,5},{7,6},{8,7},{9,8},{10,9},{11,1... | collective-permute-start | bytes 393224 | tf_op jit(solution)/shard_map/ppermute | solution.py:24
  38.7 1.1 %collective-permute-done.3 = bf16[1,4,16,4,256]{4,3,2,1,0:T(4,128)(2,1)S(1)} collective-permute-done((bf16[1,4,16,4,256]{4,3,2,1,0:T(4,128)(2,1)S(1)}, bf16[1,4,16,4,256]{4,3,2,1,0:T(4,128)(2,1)S(1)}, u32[]{:S(2)}, u32[]{:S(2)}) %collective-permute-start.3) | collective-permute-done | bytes 131104 | tf_op jit(solution)/shard_map/ppermute | solution.py:21
  39.7 1.2 %collective-permute-done.4 = bf16[1,4,16,4,256]{4,3,2,1,0:T(4,128)(2,1)S(1)} collective-permute-done((bf16[1,4,16,4,256]{4,3,2,1,0:T(4,128)(2,1)S(1)}, bf16[1,4,16,4,256]{4,3,2,1,0:T(4,128)(2,1)S(1)}, u32[]{:S(2)}, u32[]{:S(2)}) %collective-permute-start.4) | collective-permute-done | bytes 131104 | tf_op jit(solution)/shard_map/ppermute | solution.py:24
  40.9 0.3 pad_maximum_fusion
  41.3 1.1 %reshape_squeeze.3.ext_ref = bf16[256,1536]{1,0:T(8,128)(2,1)} reshape(bf16[1,4,16,4,1536]{4,3,2,1,0:T(4,128)(2,1)S(1)} %pad_maximum_fusion) | data formatting | bytes 1572864 | tf_op jit(solution)/shard_map/reshape;squeeze | solution.py:138
  42.3 9.9 %shard_map.64 = f32[256,1536]{1,0:T(8,128)} custom-call(s32[96]{0:T(128)} %bitcast.38, s32[1]{0:T(128)} %bitcast.28.cnt_ref, bf16[256,1536]{1,0:T(8,128)(2,1)} %reshape_squeeze.3.ext_ref, bf16[96,128,128]{2,1,0:T(8,128)(2,1)} %bitcast.35, bf16[4,12288]{1,0:T(4,128)(2,1)} %bitcast.36, bf16[4,12288]{1,0:T(4,128)(2,1)} %bitcast.37), custom_call_target="tpu_custom_call" | custom-call | flops 1610612736 | bytes 5701632 | tf_op jit(solution)/shard_map/pallas_call | solution.py:104
  52.2 1.8 %broadcast_in_dim_reshape.3 = f32[1,4,16,4,1536]{4,3,2,1,0:T(4,128)S(1)} reshape(f32[256,1536]{1,0:T(8,128)} %shard_map.64) | data formatting | bytes 3145728 | tf_op jit(solution)/shard_map/broadcast_in_dim;reshape | solution.py:142
  54.0 7.7 %collective-permute-start.5 = (f32[1,4,16,4,256]{4,3,2,1,0:T(4,128)S(1)}, f32[1,4,16,4,256]{4,3,2,1,0:T(4,128)S(1)}, u32[]{:S(2)}, u32[]{:S(2)}) collective-permute-start(f32[1,4,16,4,256]{4,3,2,1,0:T(4,128)S(1)} %get-tuple-element.30), channel_id=1, source_target_pairs={{0,31},{1,0},{2,1},{3,2},{4,3},{5,4},{6,5},{7,6},{8,7},{9,8},{10,9... | collective-permute-start | bytes 786440 | tf_op jit(solution)/shard_map/ppermute | solution.py:32
  61.7 1.9 %collective-permute-start.6 = (f32[1,4,16,4,256]{4,3,2,1,0:T(4,128)S(1)}, f32[1,4,16,4,256]{4,3,2,1,0:T(4,128)S(1)}, u32[]{:S(2)}, u32[]{:S(2)}) collective-permute-start(f32[1,4,16,4,256]{4,3,2,1,0:T(4,128)S(1)} %get-tuple-element.29), channel_id=1, source_target_pairs={{0,1},{1,2},{2,3},{3,4},{4,5},{5,6},{6,7},{7,8},{8,9},{9,10},{10,1... | collective-permute-start | bytes 786440 | tf_op jit(solution)/shard_map/ppermute | solution.py:32
  63.7 0.1 slice.123
  63.8 2.8 %collective-permute-done.5 = f32[1,4,16,4,256]{4,3,2,1,0:T(4,128)S(1)} collective-permute-done((f32[1,4,16,4,256]{4,3,2,1,0:T(4,128)S(1)}, f32[1,4,16,4,256]{4,3,2,1,0:T(4,128)S(1)}, u32[]{:S(2)}, u32[]{:S(2)}) %collective-permute-start.5) | collective-permute-done | bytes 262176 | tf_op jit(solution)/shard_map/ppermute | solution.py:32
  66.6 0.1 fusion.4
  66.7 7.3 %collective-permute-done.6 = f32[1,4,16,4,256]{4,3,2,1,0:T(4,128)S(1)} collective-permute-done((f32[1,4,16,4,256]{4,3,2,1,0:T(4,128)S(1)}, f32[1,4,16,4,256]{4,3,2,1,0:T(4,128)S(1)}, u32[]{:S(2)}, u32[]{:S(2)}) %collective-permute-start.6) | collective-permute-done | bytes 262176 | tf_op jit(solution)/shard_map/ppermute | solution.py:32
  74.0 0.1 fusion.3
  74.1 0.1 slice_bitcast_fusion.2
  74.2 1.9 %collective-permute-start.7 = (f32[1,16,4,1024]{3,2,1,0:T(4,128)S(1)}, f32[1,16,4,1024]{3,2,1,0:T(4,128)S(1)}, u32[]{:S(2)}, u32[]{:S(2)}) collective-permute-start(f32[1,16,4,1024]{3,2,1,0:T(4,128)S(1)} %get-tuple-element.31), channel_id=1, source_target_pairs={{0,384},{32,416},{64,448},{96,480},{128,0},{160,32},{192,64},{224,... | collective-permute-start | bytes 786440 | tf_op jit(solution)/shard_map/ppermute | solution.py:32
  76.1 4.8 %collective-permute-start.9 = (f32[1,16,4,1024]{3,2,1,0:T(4,128)S(1)}, f32[1,16,4,1024]{3,2,1,0:T(4,128)S(1)}, u32[]{:S(2)}, u32[]{:S(2)}) collective-permute-start(f32[1,16,4,1024]{3,2,1,0:T(4,128)S(1)} %get-tuple-element.32), channel_id=1, source_target_pairs={{0,128},{32,160},{64,192},{96,224},{128,256},{160,288},{192,320},{... | collective-permute-start | bytes 786440 | tf_op jit(solution)/shard_map/ppermute | solution.py:32
  81.0 3.0 %collective-permute-start.8 = (f32[1,16,4,1024]{3,2,1,0:T(4,128)S(1)}, f32[1,16,4,1024]{3,2,1,0:T(4,128)S(1)}, u32[]{:S(2)}, u32[]{:S(2)}) collective-permute-start(f32[1,16,4,1024]{3,2,1,0:T(4,128)S(1)} %get-tuple-element.33), channel_id=1, source_target_pairs={{0,256},{32,288},{64,320},{96,352},{128,384},{160,416},{192,448},{... | collective-permute-start | bytes 786440 | tf_op jit(solution)/shard_map/ppermute | solution.py:32
  84.0 3.9 %collective-permute-done.7 = f32[1,16,4,1024]{3,2,1,0:T(4,128)S(1)} collective-permute-done((f32[1,16,4,1024]{3,2,1,0:T(4,128)S(1)}, f32[1,16,4,1024]{3,2,1,0:T(4,128)S(1)}, u32[]{:S(2)}, u32[]{:S(2)}) %collective-permute-start.7) | collective-permute-done | bytes 262176 | tf_op jit(solution)/shard_map/ppermute | solution.py:32
  87.9 14.7 %collective-permute-done.9 = f32[1,16,4,1024]{3,2,1,0:T(4,128)S(1)} collective-permute-done((f32[1,16,4,1024]{3,2,1,0:T(4,128)S(1)}, f32[1,16,4,1024]{3,2,1,0:T(4,128)S(1)}, u32[]{:S(2)}, u32[]{:S(2)}) %collective-permute-start.9) | collective-permute-done | bytes 262176 | tf_op jit(solution)/shard_map/ppermute | solution.py:32
  102.6 0.0 collective-permute-done.8
  102.6 0.9 fusion.2
  (1 shorter events, 0.0 us)
Async XLA Ops:
  1.3 18.0 %collective-permute-start = (bf16[1,16,4,1024]{3,2,1,0:T(4,128)(2,1)S(1)}, bf16[1,16,4,1024]{3,2,1,0:T(4,128)(2,1)S(1)}, u32[]{:S(2)}, u32[]{:S(2)}) collective-permute-start(bf16[1,16,4,1024]{3,2,1,0:T(4,128)(2,1)S(1)} %get-tuple-element.37), channel_id=1, source_target_pairs={{0,128},{32,160},{64,192},{96,224},{128,256},{160,288},{192,320},{... | collective-permute-start | bytes 393224 | tf_op jit(solution)/shard_map/ppermute | solution.py:32
  7.4 12.4 %collective-permute-start.2 = (bf16[1,16,4,1024]{3,2,1,0:T(4,128)(2,1)S(1)}, bf16[1,16,4,1024]{3,2,1,0:T(4,128)(2,1)S(1)}, u32[]{:S(2)}, u32[]{:S(2)}) collective-permute-start(bf16[1,16,4,1024]{3,2,1,0:T(4,128)(2,1)S(1)} %get-tuple-element.38), channel_id=1, source_target_pairs={{0,384},{32,416},{64,448},{96,480},{128,0},{160,32},{192,64},{224,... | collective-permute-start | bytes 393224 | tf_op jit(solution)/shard_map/ppermute | solution.py:32
  13.3 15.1 %collective-permute-start.1 = (bf16[1,16,4,1024]{3,2,1,0:T(4,128)(2,1)S(1)}, bf16[1,16,4,1024]{3,2,1,0:T(4,128)(2,1)S(1)}, u32[]{:S(2)}, u32[]{:S(2)}) collective-permute-start(bf16[1,16,4,1024]{3,2,1,0:T(4,128)(2,1)S(1)} %get-tuple-element.39), channel_id=1, source_target_pairs={{0,256},{32,288},{64,320},{96,352},{128,384},{160,416},{192,448},{... | collective-permute-start | bytes 393224 | tf_op jit(solution)/shard_map/ppermute | solution.py:32
  28.5 11.2 %collective-permute-start.3 = (bf16[1,4,16,4,256]{4,3,2,1,0:T(4,128)(2,1)S(1)}, bf16[1,4,16,4,256]{4,3,2,1,0:T(4,128)(2,1)S(1)}, u32[]{:S(2)}, u32[]{:S(2)}) collective-permute-start(bf16[1,4,16,4,256]{4,3,2,1,0:T(4,128)(2,1)S(1)} %get-tuple-element.34), channel_id=1, source_target_pairs={{0,1},{1,2},{2,3},{3,4},{4,5},{5,6},{6,7},{7,8},{8,9},{9,10},{10,1... | collective-permute-start | bytes 393224 | tf_op jit(solution)/shard_map/ppermute | solution.py:21
  32.0 8.9 %collective-permute-start.4 = (bf16[1,4,16,4,256]{4,3,2,1,0:T(4,128)(2,1)S(1)}, bf16[1,4,16,4,256]{4,3,2,1,0:T(4,128)(2,1)S(1)}, u32[]{:S(2)}, u32[]{:S(2)}) collective-permute-start(bf16[1,4,16,4,256]{4,3,2,1,0:T(4,128)(2,1)S(1)} %get-tuple-element.35), channel_id=1, source_target_pairs={{1,0},{2,1},{3,2},{4,3},{5,4},{6,5},{7,6},{8,7},{9,8},{10,9},{11,1... | collective-permute-start | bytes 393224 | tf_op jit(solution)/shard_map/ppermute | solution.py:24
  54.0 12.6 %collective-permute-start.5 = (f32[1,4,16,4,256]{4,3,2,1,0:T(4,128)S(1)}, f32[1,4,16,4,256]{4,3,2,1,0:T(4,128)S(1)}, u32[]{:S(2)}, u32[]{:S(2)}) collective-permute-start(f32[1,4,16,4,256]{4,3,2,1,0:T(4,128)S(1)} %get-tuple-element.30), channel_id=1, source_target_pairs={{0,31},{1,0},{2,1},{3,2},{4,3},{5,4},{6,5},{7,6},{8,7},{9,8},{10,9... | collective-permute-start | bytes 786440 | tf_op jit(solution)/shard_map/ppermute | solution.py:32
  61.7 12.3 %collective-permute-start.6 = (f32[1,4,16,4,256]{4,3,2,1,0:T(4,128)S(1)}, f32[1,4,16,4,256]{4,3,2,1,0:T(4,128)S(1)}, u32[]{:S(2)}, u32[]{:S(2)}) collective-permute-start(f32[1,4,16,4,256]{4,3,2,1,0:T(4,128)S(1)} %get-tuple-element.29), channel_id=1, source_target_pairs={{0,1},{1,2},{2,3},{3,4},{4,5},{5,6},{6,7},{7,8},{8,9},{9,10},{10,1... | collective-permute-start | bytes 786440 | tf_op jit(solution)/shard_map/ppermute | solution.py:32
  74.2 13.7 %collective-permute-start.7 = (f32[1,16,4,1024]{3,2,1,0:T(4,128)S(1)}, f32[1,16,4,1024]{3,2,1,0:T(4,128)S(1)}, u32[]{:S(2)}, u32[]{:S(2)}) collective-permute-start(f32[1,16,4,1024]{3,2,1,0:T(4,128)S(1)} %get-tuple-element.31), channel_id=1, source_target_pairs={{0,384},{32,416},{64,448},{96,480},{128,0},{160,32},{192,64},{224,... | collective-permute-start | bytes 786440 | tf_op jit(solution)/shard_map/ppermute | solution.py:32
  76.1 26.5 %collective-permute-start.9 = (f32[1,16,4,1024]{3,2,1,0:T(4,128)S(1)}, f32[1,16,4,1024]{3,2,1,0:T(4,128)S(1)}, u32[]{:S(2)}, u32[]{:S(2)}) collective-permute-start(f32[1,16,4,1024]{3,2,1,0:T(4,128)S(1)} %get-tuple-element.32), channel_id=1, source_target_pairs={{0,128},{32,160},{64,192},{96,224},{128,256},{160,288},{192,320},{... | collective-permute-start | bytes 786440 | tf_op jit(solution)/shard_map/ppermute | solution.py:32
  81.0 21.7 %collective-permute-start.8 = (f32[1,16,4,1024]{3,2,1,0:T(4,128)S(1)}, f32[1,16,4,1024]{3,2,1,0:T(4,128)S(1)}, u32[]{:S(2)}, u32[]{:S(2)}) collective-permute-start(f32[1,16,4,1024]{3,2,1,0:T(4,128)S(1)} %get-tuple-element.33), channel_id=1, source_target_pairs={{0,256},{32,288},{64,320},{96,352},{128,384},{160,416},{192,448},{... | collective-permute-start | bytes 786440 | tf_op jit(solution)/shard_map/ppermute | solution.py:32

commit v5 on v4

--- a/solution.py
+++ b/solution.py
@@ -5,6 +5,7 @@
 from jax import lax
 from jax.experimental import pallas as pl
 from jax.experimental.pallas import tpu as pltpu
+from jax.sharding import Mesh
 from jax.sharding import PartitionSpec as P
 
 GROUP_SITE_SPAN = 128
@@ -124,39 +125,39 @@
 
 
 def body(hindcast_archive, op_blocks, block_index, obs_values, obs_weights, obs_counts):
-    tm_size = lax.axis_size("tm")
-    lead_count = hindcast_archive.shape[1]
-    regrouped = [hindcast_archive[:, 0]]
-    for horizon_step in range(1, lead_count):
-        regrouped.append(
-            passed_along(
-                hindcast_archive[:, horizon_step], "tm", horizon_step * tm_size // lead_count
-            )
-        )
-    extended = extend(jnp.stack(regrouped, axis=1))[0]
+    ring = lax.axis_size("tq")
+    here = lax.axis_index("tq")
+    own = hindcast_archive[0]
+    outgoing = jnp.roll(own, here, axis=0)
+    incoming = lax.all_to_all(outgoing, "tq", 0, 0, tiled=True)
+    extended = extend(incoming[None])[0]
     leads, members, fields, cells = extended.shape
     ext_rows = extended.reshape(leads * members * fields, cells)
     adjoint_rows = observe(
         ext_rows, op_blocks[0], block_index[0], obs_values[0], obs_weights[0], obs_counts[0]
     )
     adjoint_ext = adjoint_rows.reshape(leads, members, fields, cells)[None]
-    interior = settle(adjoint_ext)
-    running = interior[:, 0]
-    for horizon_step in range(1, lead_count):
-        running = running + passed_along(
-            interior[:, horizon_step], "tm", -(horizon_step * tm_size // lead_count)
-        )
-    return running
+    interior = settle(adjoint_ext)[0]
+    running = lax.dynamic_index_in_dim(interior, here, axis=0, keepdims=False)
+    for shift in range(1, ring):
+        back = lax.dynamic_index_in_dim(interior, (here - shift) % ring, axis=0, keepdims=False)
+        running = running + passed_along(back, "tq", -shift)
+    return running[None]
 
 
 def solution(mesh):
+    tm_size = mesh.shape["tm"]
+    lead_count = 4
+    devices = mesh.devices.reshape(lead_count, tm_size // lead_count, mesh.shape["space"])
+    ring_mesh = Mesh(devices, ("tq", "tr", "space"))
+    tm = ("tq", "tr")
     in_specs = (
-        P("tm", None, None, None, "space"),
-        P("tm", "space", None, None),
-        P("tm", "space"),
-        P("tm", None, "space"),
-        P("tm", None, "space"),
-        P("tm", "space"),
+        P(tm, None, None, None, "space"),
+        P(tm, "space", None, None),
+        P(tm, "space"),
+        P(tm, None, "space"),
+        P(tm, None, "space"),
+        P(tm, "space"),
     )
-    out_specs = P("tm", None, None, "space")
-    return jax.shard_map(body, mesh=mesh, in_specs=in_specs, out_specs=out_specs, check_vma=False)
+    out_specs = P(tm, None, None, "space")
+    return jax.shard_map(body, mesh=ring_mesh, in_specs=in_specs, out_specs=out_specs, check_vma=False)

time: 104 us -> 100 us (0.962)
  blocking collectives: 0 us -> 25.8 us
  starting transfers between devices: 46.9 us -> 29.9 us
  waiting for transfers between devices: 40.1 us -> 27.1 us
  other arithmetic: 1.51 us -> 3.66 us
  local copies, waits for them, and re-layouts: 4.3 us -> 2.34 us
    all_to_all x0 -> x1, blocking collectives: none -> 25.8 us  [body(): incoming = lax.all_to_all(outgoing, 'tq', 0, 0, tiled=True)]
    ppermute x8 -> x5, starting transfers between devices: 37.4 us -> 20.4 us  [passed_along(): return lax.ppermute(value, axis, pairs)]
    ppermute x8 -> x5, waiting for transfers between devices: 37.9 us -> 25.4 us  [passed_along(): return lax.ppermute(value, axis, pairs)]
    concatenate x0 -> x1, other arithmetic: none -> 1.69 us  [body(): outgoing = jnp.roll(own, here, axis=0)]
    slice x1, local copies, waits for them, and re-layouts: 1.28 us -> 0.09 us  [with_halo(): lax.slice_in_dim(block, block.shape[dim] - width, None, axis=dim)]
    another operation x1 -> x0, local copies, waits for them, and re-layouts: 1.06 us -> none  [body(): ext_rows = extended.reshape(leads * members * fields, cells)]
  transfers between devices with their start and end apart: 10 -> 7, of which waited for: 8 -> 6; matrix products, arithmetic and copies ran while one was open for 0% -> 0% of each run, Pallas kernels for 0% -> 0%
where the time goes in v5:
time: 100 us; the launch traced here: 99.5 us
  starting transfers between devices  29.9 us (30%)
  waiting for transfers between devices  27.1 us (27%)
  blocking collectives  25.8 us (26%)
  Pallas kernels  9.87 us (10%)
  other arithmetic  3.66 us (4%)
  local copies, waits for them, and re-layouts  2.34 us (2%)
    all_to_all x1, blocking collectives, body(): incoming = lax.all_to_all(outgoing, 'tq', 0, 0, tiled=True)  25.8 us
    ppermute x5, waiting for transfers between devices, passed_along(): return lax.ppermute(value, axis, pairs)  25.4 us
    ppermute x5, starting transfers between devices, passed_along(): return lax.ppermute(value, axis, pairs)  20.4 us
    pallas_call x1, Pallas kernels, observe(): pl.pallas_call(observe_kernel, grid_spec=grid_spec, out_shape=jax.ShapeDt...  9.87 us
    ppermute x1, starting transfers between devices, with_halo(): lax.ppermute(lax.slice_in_dim(block, 0, width, axis=dim), axis, backward)  6.01 us
    ppermute x1, starting transfers between devices, with_halo(): lax.ppermute(lax.slice_in_dim(block, block.shape[dim] - width, None, axis...  3.48 us
  transfers between devices with their start and end apart: 7, of which 6 were waited for; matrix products, arithmetic and copies ran while one was open for 0% of the time, Pallas kernels for 0%

profile of v5, /device:TPU:64, one launch (start us, length us, event | category | flops | bytes accessed | tf_op | source)
XLA Modules:
  0.0 99.5 jit_solution(5773534412002094411)
XLA Ops:
  0.0 1.7 %fusion = bf16[4,16,4,1024]{3,2,1,0:T(4,128)(2,1)S(1)} fusion(s32[]{:T(128)S(6)} %select_n.41, bf16[4,16,4,1024]{3,2,1,0:T(4,128)(2,1)} %bitcast.31), kind=kLoop, calls=%fused_computation.3 | loop fusion | flops 262144 | bytes 1048580 | tf_op jit(solution)/shard_map/jit(_roll_dynamic)/concatenate | solution.py:131
  1.7 25.8 %all_to_all.5 = bf16[4,16,4,1024]{3,2,1,0:T(4,128)(2,1)S(1)} all-to-all(bf16[4,16,4,1024]{3,2,1,0:T(4,128)(2,1)S(1)} %fusion), channel_id=1, replica_groups=mesh['tq'=4,'tr'=4,'space'=32] {'tq'}, dimensions={0} | all-to-all | bytes 1048576 | tf_op jit(solution)/shard_map/all_to_all | solution.py:132
  27.5 0.1 fusion.8
  27.6 3.5 %collective-permute-start = (bf16[1,4,16,4,256]{4,3,2,1,0:T(4,128)(2,1)S(1)}, bf16[1,4,16,4,256]{4,3,2,1,0:T(4,128)(2,1)S(1)}, u32[]{:S(2)}, u32[]{:S(2)}) collective-permute-start(bf16[1,4,16,4,256]{4,3,2,1,0:T(4,128)(2,1)S(1)} %get-tuple-element.34), channel_id=1, source_target_pairs={{0,1},{1,2},{2,3},{3,4},{4,5},{5,6},{6,7},{7,8},{8,9},{9,10},{10,1... | collective-permute-start | bytes 393224 | tf_op jit(solution)/shard_map/ppermute | solution.py:22
  31.1 6.0 %collective-permute-start.1 = (bf16[1,4,16,4,256]{4,3,2,1,0:T(4,128)(2,1)S(1)}, bf16[1,4,16,4,256]{4,3,2,1,0:T(4,128)(2,1)S(1)}, u32[]{:S(2)}, u32[]{:S(2)}) collective-permute-start(bf16[1,4,16,4,256]{4,3,2,1,0:T(4,128)(2,1)S(1)} %get-tuple-element.35), channel_id=1, source_target_pairs={{1,0},{2,1},{3,2},{4,3},{5,4},{6,5},{7,6},{8,7},{9,8},{10,9},{11,1... | collective-permute-start | bytes 393224 | tf_op jit(solution)/shard_map/ppermute | solution.py:25
  37.7 0.1 concatenate.20
  37.8 0.2 collective-permute-done
  38.1 1.5 %collective-permute-done.1 = bf16[1,4,16,4,256]{4,3,2,1,0:T(4,128)(2,1)S(1)} collective-permute-done((bf16[1,4,16,4,256]{4,3,2,1,0:T(4,128)(2,1)S(1)}, bf16[1,4,16,4,256]{4,3,2,1,0:T(4,128)(2,1)S(1)}, u32[]{:S(2)}, u32[]{:S(2)}) %collective-permute-start.1) | collective-permute-done | bytes 131104 | tf_op jit(solution)/shard_map/ppermute | solution.py:25
  39.6 0.9 pad_maximum_fusion.ext_ref
  40.5 9.9 %shard_map.64 = f32[256,1536]{1,0:T(8,128)} custom-call(s32[96]{0:T(128)} %bitcast.35, s32[1]{0:T(128)} %bitcast.28.cnt_ref, bf16[256,1536]{1,0:T(8,128)(2,1)} %pad_maximum_fusion.ext_ref, bf16[96,128,128]{2,1,0:T(8,128)(2,1)} %bitcast.32, bf16[4,12288]{1,0:T(4,128)(2,1)} %bitcast.33, bf16[4,12288]{1,0:T(4,128)(2,1)} %bitcast.34), custom_call_target="tpu_custom_call" | custom-call | flops 1610612736 | bytes 5701632 | tf_op jit(solution)/shard_map/pallas_call | solution.py:105
  50.4 1.8 %broadcast_in_dim_reshape.3 = f32[1,4,16,4,1536]{4,3,2,1,0:T(4,128)S(1)} reshape(f32[256,1536]{1,0:T(8,128)} %shard_map.64) | data formatting | bytes 3145728 | tf_op jit(solution)/shard_map/broadcast_in_dim;reshape | solution.py:139
  52.2 7.7 %collective-permute-start.2 = (f32[1,4,16,4,256]{4,3,2,1,0:T(4,128)S(1)}, f32[1,4,16,4,256]{4,3,2,1,0:T(4,128)S(1)}, u32[]{:S(2)}, u32[]{:S(2)}) collective-permute-start(f32[1,4,16,4,256]{4,3,2,1,0:T(4,128)S(1)} %get-tuple-element.30), channel_id=1, source_target_pairs={{0,31},{1,0},{2,1},{3,2},{4,3},{5,4},{6,5},{7,6},{8,7},{9,8},{10,9... | collective-permute-start | bytes 786440 | tf_op jit(solution)/shard_map/ppermute | solution.py:33
  59.9 1.9 %collective-permute-start.3 = (f32[1,4,16,4,256]{4,3,2,1,0:T(4,128)S(1)}, f32[1,4,16,4,256]{4,3,2,1,0:T(4,128)S(1)}, u32[]{:S(2)}, u32[]{:S(2)}) collective-permute-start(f32[1,4,16,4,256]{4,3,2,1,0:T(4,128)S(1)} %get-tuple-element.29), channel_id=1, source_target_pairs={{0,1},{1,2},{2,3},{3,4},{4,5},{5,6},{6,7},{7,8},{8,9},{9,10},{10,1... | collective-permute-start | bytes 786440 | tf_op jit(solution)/shard_map/ppermute | solution.py:33
  61.9 0.1 slice.93
  62.0 1.8 %collective-permute-done.2 = f32[1,4,16,4,256]{4,3,2,1,0:T(4,128)S(1)} collective-permute-done((f32[1,4,16,4,256]{4,3,2,1,0:T(4,128)S(1)}, f32[1,4,16,4,256]{4,3,2,1,0:T(4,128)S(1)}, u32[]{:S(2)}, u32[]{:S(2)}) %collective-permute-start.2) | collective-permute-done | bytes 262176 | tf_op jit(solution)/shard_map/ppermute | solution.py:33
  63.8 0.1 fusion.3
  63.9 0.1 copy.8
  63.9 7.5 %collective-permute-done.3 = f32[1,4,16,4,256]{4,3,2,1,0:T(4,128)S(1)} collective-permute-done((f32[1,4,16,4,256]{4,3,2,1,0:T(4,128)S(1)}, f32[1,4,16,4,256]{4,3,2,1,0:T(4,128)S(1)}, u32[]{:S(2)}, u32[]{:S(2)}) %collective-permute-start.3) | collective-permute-done | bytes 262176 | tf_op jit(solution)/shard_map/ppermute | solution.py:33
  71.5 0.1 fusion.2
  71.6 0.1 dynamic-slice_bitcast_fusion.2
  71.7 4.1 %collective-permute-start.4 = (f32[16,4,1024]{2,1,0:T(4,128)S(1)}, f32[16,4,1024]{2,1,0:T(4,128)S(1)}, u32[]{:S(2)}, u32[]{:S(2)}) collective-permute-start(f32[16,4,1024]{2,1,0:T(4,128)S(1)} %get-tuple-element.31), channel_id=1, source_target_pairs={{0,384},{128,0},{256,128},{384,256},{1,385},{129,1},{257,129},{385... | collective-permute-start | bytes 786440 | tf_op jit(solution)/shard_map/ppermute | solution.py:33
  75.7 3.9 %collective-permute-start.5 = (f32[16,4,1024]{2,1,0:T(4,128)S(1)}, f32[16,4,1024]{2,1,0:T(4,128)S(1)}, u32[]{:S(2)}, u32[]{:S(2)}) collective-permute-start(f32[16,4,1024]{2,1,0:T(4,128)S(1)} %get-tuple-element.33), channel_id=1, source_target_pairs={{0,256},{128,384},{256,0},{384,128},{1,257},{129,385},{257,1},{385... | collective-permute-start | bytes 786440 | tf_op jit(solution)/shard_map/ppermute | solution.py:33
  79.6 2.9 %collective-permute-start.6 = (f32[16,4,1024]{2,1,0:T(4,128)S(1)}, f32[16,4,1024]{2,1,0:T(4,128)S(1)}, u32[]{:S(2)}, u32[]{:S(2)}) collective-permute-start(f32[16,4,1024]{2,1,0:T(4,128)S(1)} %get-tuple-element.32), channel_id=1, source_target_pairs={{0,128},{128,256},{256,384},{384,0},{1,129},{129,257},{257,385},{3... | collective-permute-start | bytes 786440 | tf_op jit(solution)/shard_map/ppermute | solution.py:33
  82.5 9.1 %collective-permute-done.4 = f32[16,4,1024]{2,1,0:T(4,128)S(1)} collective-permute-done((f32[16,4,1024]{2,1,0:T(4,128)S(1)}, f32[16,4,1024]{2,1,0:T(4,128)S(1)}, u32[]{:S(2)}, u32[]{:S(2)}) %collective-permute-start.4) | collective-permute-done | bytes 262176 | tf_op jit(solution)/shard_map/ppermute | solution.py:33
  91.6 0.0 collective-permute-done.5
  91.6 7.0 %collective-permute-done.6 = f32[16,4,1024]{2,1,0:T(4,128)S(1)} collective-permute-done((f32[16,4,1024]{2,1,0:T(4,128)S(1)}, f32[16,4,1024]{2,1,0:T(4,128)S(1)}, u32[]{:S(2)}, u32[]{:S(2)}) %collective-permute-start.6) | collective-permute-done | bytes 262176 | tf_op jit(solution)/shard_map/ppermute | solution.py:33
  98.7 0.9 fusion.6
  (3 shorter events, 0.1 us)
Async XLA Ops:
  27.6 10.5 %collective-permute-start = (bf16[1,4,16,4,256]{4,3,2,1,0:T(4,128)(2,1)S(1)}, bf16[1,4,16,4,256]{4,3,2,1,0:T(4,128)(2,1)S(1)}, u32[]{:S(2)}, u32[]{:S(2)}) collective-permute-start(bf16[1,4,16,4,256]{4,3,2,1,0:T(4,128)(2,1)S(1)} %get-tuple-element.34), channel_id=1, source_target_pairs={{0,1},{1,2},{2,3},{3,4},{4,5},{5,6},{6,7},{7,8},{8,9},{9,10},{10,1... | collective-permute-start | bytes 393224 | tf_op jit(solution)/shard_map/ppermute | solution.py:22
  31.1 8.5 %collective-permute-start.1 = (bf16[1,4,16,4,256]{4,3,2,1,0:T(4,128)(2,1)S(1)}, bf16[1,4,16,4,256]{4,3,2,1,0:T(4,128)(2,1)S(1)}, u32[]{:S(2)}, u32[]{:S(2)}) collective-permute-start(bf16[1,4,16,4,256]{4,3,2,1,0:T(4,128)(2,1)S(1)} %get-tuple-element.35), channel_id=1, source_target_pairs={{1,0},{2,1},{3,2},{4,3},{5,4},{6,5},{7,6},{8,7},{9,8},{10,9},{11,1... | collective-permute-start | bytes 393224 | tf_op jit(solution)/shard_map/ppermute | solution.py:25
  52.2 11.5 %collective-permute-start.2 = (f32[1,4,16,4,256]{4,3,2,1,0:T(4,128)S(1)}, f32[1,4,16,4,256]{4,3,2,1,0:T(4,128)S(1)}, u32[]{:S(2)}, u32[]{:S(2)}) collective-permute-start(f32[1,4,16,4,256]{4,3,2,1,0:T(4,128)S(1)} %get-tuple-element.30), channel_id=1, source_target_pairs={{0,31},{1,0},{2,1},{3,2},{4,3},{5,4},{6,5},{7,6},{8,7},{9,8},{10,9... | collective-permute-start | bytes 786440 | tf_op jit(solution)/shard_map/ppermute | solution.py:33
  59.9 11.6 %collective-permute-start.3 = (f32[1,4,16,4,256]{4,3,2,1,0:T(4,128)S(1)}, f32[1,4,16,4,256]{4,3,2,1,0:T(4,128)S(1)}, u32[]{:S(2)}, u32[]{:S(2)}) collective-permute-start(f32[1,4,16,4,256]{4,3,2,1,0:T(4,128)S(1)} %get-tuple-element.29), channel_id=1, source_target_pairs={{0,1},{1,2},{2,3},{3,4},{4,5},{5,6},{6,7},{7,8},{8,9},{9,10},{10,1... | collective-permute-start | bytes 786440 | tf_op jit(solution)/shard_map/ppermute | solution.py:33
  71.7 20.0 %collective-permute-start.4 = (f32[16,4,1024]{2,1,0:T(4,128)S(1)}, f32[16,4,1024]{2,1,0:T(4,128)S(1)}, u32[]{:S(2)}, u32[]{:S(2)}) collective-permute-start(f32[16,4,1024]{2,1,0:T(4,128)S(1)} %get-tuple-element.31), channel_id=1, source_target_pairs={{0,384},{128,0},{256,128},{384,256},{1,385},{129,1},{257,129},{385... | collective-permute-start | bytes 786440 | tf_op jit(solution)/shard_map/ppermute | solution.py:33
  75.7 15.9 %collective-permute-start.5 = (f32[16,4,1024]{2,1,0:T(4,128)S(1)}, f32[16,4,1024]{2,1,0:T(4,128)S(1)}, u32[]{:S(2)}, u32[]{:S(2)}) collective-permute-start(f32[16,4,1024]{2,1,0:T(4,128)S(1)} %get-tuple-element.33), channel_id=1, source_target_pairs={{0,256},{128,384},{256,0},{384,128},{1,257},{129,385},{257,1},{385... | collective-permute-start | bytes 786440 | tf_op jit(solution)/shard_map/ppermute | solution.py:33
  79.6 19.1 %collective-permute-start.6 = (f32[16,4,1024]{2,1,0:T(4,128)S(1)}, f32[16,4,1024]{2,1,0:T(4,128)S(1)}, u32[]{:S(2)}, u32[]{:S(2)}) collective-permute-start(f32[16,4,1024]{2,1,0:T(4,128)S(1)} %get-tuple-element.32), channel_id=1, source_target_pairs={{0,128},{128,256},{256,384},{384,0},{1,129},{129,257},{257,385},{3... | collective-permute-start | bytes 786440 | tf_op jit(solution)/shard_map/ppermute | solution.py:33

commit v6 on v5

--- a/solution.py
+++ b/solution.py
@@ -10,7 +10,7 @@
 
 GROUP_SITE_SPAN = 128
 EDGE = 2
-BLOCKS_PER_STEP = 16
+BLOCKS_PER_STEP = 32
 
 
 def with_halo(block, sides, width):
@@ -42,44 +42,30 @@
     width = GROUP_SITE_SPAN
     fields = val_ref.shape[0]
     rows = ext_ref.shape[0]
+    period = 8
 
     @pl.when(step == 0)
     def _():
         out_ref[...] = jnp.zeros_like(out_ref)
 
     count = cnt_ref[0]
-    pair = 2 * width
-    period = 8
-    lane = lax.broadcasted_iota(jnp.int32, (1, 1, pair), 2)
-    zero = jnp.zeros((width, width), op_ref.dtype)
-    for k in range(0, BLOCKS_PER_STEP, 2):
+    lane = lax.broadcasted_iota(jnp.int32, (1, width), 1)
+    for k in range(BLOCKS_PER_STEP):
         b = step * BLOCKS_PER_STEP + k
-        first = pl.multiple_of(idx_ref[b] * width, width)
-        second = pl.multiple_of(idx_ref[b + 1] * width, width)
-        x = jnp.concatenate(
-            [ext_ref[:, pl.ds(first, width)], ext_ref[:, pl.ds(second, width)]], axis=1
-        )
-        op = jnp.concatenate(
-            [
-                jnp.concatenate([op_ref[k], zero], axis=1),
-                jnp.concatenate([zero, op_ref[k + 1]], axis=1),
-            ],
-            axis=0,
-        )
+        start = pl.multiple_of(idx_ref[b] * width, width)
+        x = ext_ref[:, pl.ds(start, width)]
+        op = op_ref[k]
         images = lax.dot_general(
             x, op, (((1,), (1,)), ((), ())), preferred_element_type=jnp.float32
-        ).reshape(rows // period, period, pair)
-        observed = val_ref[:, k * width:k * width + pair].astype(jnp.float32)
+        ).reshape(rows // period, period, width)
+        observed = val_ref[:, k * width:(k + 1) * width].astype(jnp.float32)
         observed = jnp.concatenate([observed] * (period // fields), axis=0)[None]
-        scaling = wt_ref[:, k * width:k * width + pair].astype(jnp.float32)
+        live = (b * width + lane) < count
+        scaling = jnp.where(live, wt_ref[:, k * width:(k + 1) * width].astype(jnp.float32), 0.0)
         scaling = jnp.concatenate([scaling] * (period // fields), axis=0)[None]
-        live = (b * width + lane) < count
-        misfit = jnp.where(live, (images - observed) * scaling, 0.0).astype(jnp.bfloat16)
-        adjoint = jnp.dot(
-            misfit.reshape(rows, pair), op, preferred_element_type=jnp.float32
-        )
-        out_ref[:, pl.ds(first, width)] += adjoint[:, :width]
-        out_ref[:, pl.ds(second, width)] += adjoint[:, width:]
+        misfit = ((images - observed) * scaling).reshape(rows, width).astype(jnp.bfloat16)
+        adjoint = jnp.dot(misfit, op, preferred_element_type=jnp.float32)
+        out_ref[:, pl.ds(start, width)] += adjoint
 
 
 def observe(ext_rows, operator, indices, values, weights, counts):

time: 100 us -> 98.2 us (0.982)
  Pallas kernels: 9.87 us -> 8.01 us
    pallas_call x1, Pallas kernels: 9.87 us -> 8.01 us  [observe(): pl.pallas_call(observe_kernel, grid_spec=grid_spec, out_shape=jax.ShapeDt...]
where the time goes in v6:
time: 98.2 us; the launch traced here: 97.6 us
  starting transfers between devices  29.9 us (30%)
  waiting for transfers between devices  27.1 us (28%)
  blocking collectives  25.8 us (26%)
  Pallas kernels  8.01 us (8%)
  other arithmetic  3.66 us (4%)
  local copies, waits for them, and re-layouts  2.34 us (2%)
    all_to_all x1, blocking collectives, body(): incoming = lax.all_to_all(outgoing, 'tq', 0, 0, tiled=True)  25.8 us
    ppermute x5, waiting for transfers between devices, passed_along(): return lax.ppermute(value, axis, pairs)  25.4 us
    ppermute x5, starting transfers between devices, passed_along(): return lax.ppermute(value, axis, pairs)  20.4 us
    pallas_call x1, Pallas kernels, observe(): pl.pallas_call(observe_kernel, grid_spec=grid_spec, out_shape=jax.ShapeDt...  8.01 us
    ppermute x1, starting transfers between devices, with_halo(): lax.ppermute(lax.slice_in_dim(block, 0, width, axis=dim), axis, backward)  6.01 us
    ppermute x1, starting transfers between devices, with_halo(): lax.ppermute(lax.slice_in_dim(block, block.shape[dim] - width, None, axis...  3.48 us
  transfers between devices with their start and end apart: 7, of which 6 were waited for; matrix products, arithmetic and copies ran while one was open for 0% of the time, Pallas kernels for 0%

profile of v6, /device:TPU:64, one launch (start us, length us, event | category | flops | bytes accessed | tf_op | source)
XLA Modules:
  0.0 97.6 jit_solution(16903948795186389648)
XLA Ops:
  0.0 1.7 %fusion = bf16[4,16,4,1024]{3,2,1,0:T(4,128)(2,1)S(1)} fusion(s32[]{:T(128)S(6)} %select_n.41, bf16[4,16,4,1024]{3,2,1,0:T(4,128)(2,1)} %bitcast.31), kind=kLoop, calls=%fused_computation.3 | loop fusion | flops 262144 | bytes 1048580 | tf_op jit(solution)/shard_map/jit(_roll_dynamic)/concatenate | solution.py:117
  1.7 25.8 %all_to_all.5 = bf16[4,16,4,1024]{3,2,1,0:T(4,128)(2,1)S(1)} all-to-all(bf16[4,16,4,1024]{3,2,1,0:T(4,128)(2,1)S(1)} %fusion), channel_id=1, replica_groups=mesh['tq'=4,'tr'=4,'space'=32] {'tq'}, dimensions={0} | all-to-all | bytes 1048576 | tf_op jit(solution)/shard_map/all_to_all | solution.py:118
  27.5 0.1 fusion.8
  27.6 3.5 %collective-permute-start = (bf16[1,4,16,4,256]{4,3,2,1,0:T(4,128)(2,1)S(1)}, bf16[1,4,16,4,256]{4,3,2,1,0:T(4,128)(2,1)S(1)}, u32[]{:S(2)}, u32[]{:S(2)}) collective-permute-start(bf16[1,4,16,4,256]{4,3,2,1,0:T(4,128)(2,1)S(1)} %get-tuple-element.34), channel_id=1, source_target_pairs={{0,1},{1,2},{2,3},{3,4},{4,5},{5,6},{6,7},{7,8},{8,9},{9,10},{10,1... | collective-permute-start | bytes 393224 | tf_op jit(solution)/shard_map/ppermute | solution.py:22
  31.1 6.0 %collective-permute-start.1 = (bf16[1,4,16,4,256]{4,3,2,1,0:T(4,128)(2,1)S(1)}, bf16[1,4,16,4,256]{4,3,2,1,0:T(4,128)(2,1)S(1)}, u32[]{:S(2)}, u32[]{:S(2)}) collective-permute-start(bf16[1,4,16,4,256]{4,3,2,1,0:T(4,128)(2,1)S(1)} %get-tuple-element.35), channel_id=1, source_target_pairs={{1,0},{2,1},{3,2},{4,3},{5,4},{6,5},{7,6},{8,7},{9,8},{10,9},{11,1... | collective-permute-start | bytes 393224 | tf_op jit(solution)/shard_map/ppermute | solution.py:25
  37.7 0.1 concatenate.20
  37.8 0.2 collective-permute-done
  38.1 1.5 %collective-permute-done.1 = bf16[1,4,16,4,256]{4,3,2,1,0:T(4,128)(2,1)S(1)} collective-permute-done((bf16[1,4,16,4,256]{4,3,2,1,0:T(4,128)(2,1)S(1)}, bf16[1,4,16,4,256]{4,3,2,1,0:T(4,128)(2,1)S(1)}, u32[]{:S(2)}, u32[]{:S(2)}) %collective-permute-start.1) | collective-permute-done | bytes 131104 | tf_op jit(solution)/shard_map/ppermute | solution.py:25
  39.6 0.9 pad_maximum_fusion.ext_ref
  40.5 8.0 %shard_map.64 = f32[256,1536]{1,0:T(8,128)} custom-call(s32[96]{0:T(128)} %bitcast.35, s32[1]{0:T(128)} %bitcast.28.cnt_ref, bf16[256,1536]{1,0:T(8,128)(2,1)} %pad_maximum_fusion.ext_ref, bf16[96,128,128]{2,1,0:T(8,128)(2,1)} %bitcast.32, bf16[4,12288]{1,0:T(4,128)(2,1)} %bitcast.33, bf16[4,12288]{1,0:T(4,128)(2,1)} %bitcast.34), custom_call_target="tpu_custom_call" | custom-call | flops 1610612736 | bytes 5701632 | tf_op jit(solution)/shard_map/pallas_call | solution.py:91
  48.5 1.8 %broadcast_in_dim_reshape.3 = f32[1,4,16,4,1536]{4,3,2,1,0:T(4,128)S(1)} reshape(f32[256,1536]{1,0:T(8,128)} %shard_map.64) | data formatting | bytes 3145728 | tf_op jit(solution)/shard_map/broadcast_in_dim;reshape | solution.py:125
  50.4 7.7 %collective-permute-start.2 = (f32[1,4,16,4,256]{4,3,2,1,0:T(4,128)S(1)}, f32[1,4,16,4,256]{4,3,2,1,0:T(4,128)S(1)}, u32[]{:S(2)}, u32[]{:S(2)}) collective-permute-start(f32[1,4,16,4,256]{4,3,2,1,0:T(4,128)S(1)} %get-tuple-element.30), channel_id=1, source_target_pairs={{0,31},{1,0},{2,1},{3,2},{4,3},{5,4},{6,5},{7,6},{8,7},{9,8},{10,9... | collective-permute-start | bytes 786440 | tf_op jit(solution)/shard_map/ppermute | solution.py:33
  58.0 1.9 %collective-permute-start.3 = (f32[1,4,16,4,256]{4,3,2,1,0:T(4,128)S(1)}, f32[1,4,16,4,256]{4,3,2,1,0:T(4,128)S(1)}, u32[]{:S(2)}, u32[]{:S(2)}) collective-permute-start(f32[1,4,16,4,256]{4,3,2,1,0:T(4,128)S(1)} %get-tuple-element.29), channel_id=1, source_target_pairs={{0,1},{1,2},{2,3},{3,4},{4,5},{5,6},{6,7},{7,8},{8,9},{9,10},{10,1... | collective-permute-start | bytes 786440 | tf_op jit(solution)/shard_map/ppermute | solution.py:33
  60.0 0.1 slice.93
  60.2 1.8 %collective-permute-done.2 = f32[1,4,16,4,256]{4,3,2,1,0:T(4,128)S(1)} collective-permute-done((f32[1,4,16,4,256]{4,3,2,1,0:T(4,128)S(1)}, f32[1,4,16,4,256]{4,3,2,1,0:T(4,128)S(1)}, u32[]{:S(2)}, u32[]{:S(2)}) %collective-permute-start.2) | collective-permute-done | bytes 262176 | tf_op jit(solution)/shard_map/ppermute | solution.py:33
  61.9 0.1 fusion.3
  62.0 0.1 copy.8
  62.1 7.5 %collective-permute-done.3 = f32[1,4,16,4,256]{4,3,2,1,0:T(4,128)S(1)} collective-permute-done((f32[1,4,16,4,256]{4,3,2,1,0:T(4,128)S(1)}, f32[1,4,16,4,256]{4,3,2,1,0:T(4,128)S(1)}, u32[]{:S(2)}, u32[]{:S(2)}) %collective-permute-start.3) | collective-permute-done | bytes 262176 | tf_op jit(solution)/shard_map/ppermute | solution.py:33
  69.6 0.1 fusion.2
  69.7 0.1 dynamic-slice_bitcast_fusion.2
  69.8 4.1 %collective-permute-start.4 = (f32[16,4,1024]{2,1,0:T(4,128)S(1)}, f32[16,4,1024]{2,1,0:T(4,128)S(1)}, u32[]{:S(2)}, u32[]{:S(2)}) collective-permute-start(f32[16,4,1024]{2,1,0:T(4,128)S(1)} %get-tuple-element.31), channel_id=1, source_target_pairs={{0,384},{128,0},{256,128},{384,256},{1,385},{129,1},{257,129},{385... | collective-permute-start | bytes 786440 | tf_op jit(solution)/shard_map/ppermute | solution.py:33
  73.9 3.9 %collective-permute-start.5 = (f32[16,4,1024]{2,1,0:T(4,128)S(1)}, f32[16,4,1024]{2,1,0:T(4,128)S(1)}, u32[]{:S(2)}, u32[]{:S(2)}) collective-permute-start(f32[16,4,1024]{2,1,0:T(4,128)S(1)} %get-tuple-element.33), channel_id=1, source_target_pairs={{0,256},{128,384},{256,0},{384,128},{1,257},{129,385},{257,1},{385... | collective-permute-start | bytes 786440 | tf_op jit(solution)/shard_map/ppermute | solution.py:33
  77.7 2.9 %collective-permute-start.6 = (f32[16,4,1024]{2,1,0:T(4,128)S(1)}, f32[16,4,1024]{2,1,0:T(4,128)S(1)}, u32[]{:S(2)}, u32[]{:S(2)}) collective-permute-start(f32[16,4,1024]{2,1,0:T(4,128)S(1)} %get-tuple-element.32), channel_id=1, source_target_pairs={{0,128},{128,256},{256,384},{384,0},{1,129},{129,257},{257,385},{3... | collective-permute-start | bytes 786440 | tf_op jit(solution)/shard_map/ppermute | solution.py:33
  80.7 9.1 %collective-permute-done.4 = f32[16,4,1024]{2,1,0:T(4,128)S(1)} collective-permute-done((f32[16,4,1024]{2,1,0:T(4,128)S(1)}, f32[16,4,1024]{2,1,0:T(4,128)S(1)}, u32[]{:S(2)}, u32[]{:S(2)}) %collective-permute-start.4) | collective-permute-done | bytes 262176 | tf_op jit(solution)/shard_map/ppermute | solution.py:33
  89.8 0.0 collective-permute-done.5
  89.8 7.0 %collective-permute-done.6 = f32[16,4,1024]{2,1,0:T(4,128)S(1)} collective-permute-done((f32[16,4,1024]{2,1,0:T(4,128)S(1)}, f32[16,4,1024]{2,1,0:T(4,128)S(1)}, u32[]{:S(2)}, u32[]{:S(2)}) %collective-permute-start.6) | collective-permute-done | bytes 262176 | tf_op jit(solution)/shard_map/ppermute | solution.py:33
  96.8 0.9 fusion.6
  (3 shorter events, 0.1 us)
Async XLA Ops:
  27.6 10.5 %collective-permute-start = (bf16[1,4,16,4,256]{4,3,2,1,0:T(4,128)(2,1)S(1)}, bf16[1,4,16,4,256]{4,3,2,1,0:T(4,128)(2,1)S(1)}, u32[]{:S(2)}, u32[]{:S(2)}) collective-permute-start(bf16[1,4,16,4,256]{4,3,2,1,0:T(4,128)(2,1)S(1)} %get-tuple-element.34), channel_id=1, source_target_pairs={{0,1},{1,2},{2,3},{3,4},{4,5},{5,6},{6,7},{7,8},{8,9},{9,10},{10,1... | collective-permute-start | bytes 393224 | tf_op jit(solution)/shard_map/ppermute | solution.py:22
  31.1 8.5 %collective-permute-start.1 = (bf16[1,4,16,4,256]{4,3,2,1,0:T(4,128)(2,1)S(1)}, bf16[1,4,16,4,256]{4,3,2,1,0:T(4,128)(2,1)S(1)}, u32[]{:S(2)}, u32[]{:S(2)}) collective-permute-start(bf16[1,4,16,4,256]{4,3,2,1,0:T(4,128)(2,1)S(1)} %get-tuple-element.35), channel_id=1, source_target_pairs={{1,0},{2,1},{3,2},{4,3},{5,4},{6,5},{7,6},{8,7},{9,8},{10,9},{11,1... | collective-permute-start | bytes 393224 | tf_op jit(solution)/shard_map/ppermute | solution.py:25
  50.4 11.6 %collective-permute-start.2 = (f32[1,4,16,4,256]{4,3,2,1,0:T(4,128)S(1)}, f32[1,4,16,4,256]{4,3,2,1,0:T(4,128)S(1)}, u32[]{:S(2)}, u32[]{:S(2)}) collective-permute-start(f32[1,4,16,4,256]{4,3,2,1,0:T(4,128)S(1)} %get-tuple-element.30), channel_id=1, source_target_pairs={{0,31},{1,0},{2,1},{3,2},{4,3},{5,4},{6,5},{7,6},{8,7},{9,8},{10,9... | collective-permute-start | bytes 786440 | tf_op jit(solution)/shard_map/ppermute | solution.py:33
  58.0 11.6 %collective-permute-start.3 = (f32[1,4,16,4,256]{4,3,2,1,0:T(4,128)S(1)}, f32[1,4,16,4,256]{4,3,2,1,0:T(4,128)S(1)}, u32[]{:S(2)}, u32[]{:S(2)}) collective-permute-start(f32[1,4,16,4,256]{4,3,2,1,0:T(4,128)S(1)} %get-tuple-element.29), channel_id=1, source_target_pairs={{0,1},{1,2},{2,3},{3,4},{4,5},{5,6},{6,7},{7,8},{8,9},{9,10},{10,1... | collective-permute-start | bytes 786440 | tf_op jit(solution)/shard_map/ppermute | solution.py:33
  69.8 20.0 %collective-permute-start.4 = (f32[16,4,1024]{2,1,0:T(4,128)S(1)}, f32[16,4,1024]{2,1,0:T(4,128)S(1)}, u32[]{:S(2)}, u32[]{:S(2)}) collective-permute-start(f32[16,4,1024]{2,1,0:T(4,128)S(1)} %get-tuple-element.31), channel_id=1, source_target_pairs={{0,384},{128,0},{256,128},{384,256},{1,385},{129,1},{257,129},{385... | collective-permute-start | bytes 786440 | tf_op jit(solution)/shard_map/ppermute | solution.py:33
  73.9 15.9 %collective-permute-start.5 = (f32[16,4,1024]{2,1,0:T(4,128)S(1)}, f32[16,4,1024]{2,1,0:T(4,128)S(1)}, u32[]{:S(2)}, u32[]{:S(2)}) collective-permute-start(f32[16,4,1024]{2,1,0:T(4,128)S(1)} %get-tuple-element.33), channel_id=1, source_target_pairs={{0,256},{128,384},{256,0},{384,128},{1,257},{129,385},{257,1},{385... | collective-permute-start | bytes 786440 | tf_op jit(solution)/shard_map/ppermute | solution.py:33
  77.7 19.0 %collective-permute-start.6 = (f32[16,4,1024]{2,1,0:T(4,128)S(1)}, f32[16,4,1024]{2,1,0:T(4,128)S(1)}, u32[]{:S(2)}, u32[]{:S(2)}) collective-permute-start(f32[16,4,1024]{2,1,0:T(4,128)S(1)} %get-tuple-element.32), channel_id=1, source_target_pairs={{0,128},{128,256},{256,384},{384,0},{1,129},{129,257},{257,385},{3... | collective-permute-start | bytes 786440 | tf_op jit(solution)/shard_map/ppermute | solution.py:33

commit v7 on v6

--- a/solution.py
+++ b/solution.py
@@ -34,7 +34,7 @@
 
 
 def extend(grouped):
-    return with_halo(grouped, (("space", 4),), EDGE * GROUP_SITE_SPAN)
+    return with_halo(grouped, (("space", grouped.ndim - 1),), EDGE * GROUP_SITE_SPAN)
 
 
 def observe_kernel(idx_ref, cnt_ref, ext_ref, op_ref, val_ref, wt_ref, out_ref):
@@ -114,21 +114,26 @@
     ring = lax.axis_size("tq")
     here = lax.axis_index("tq")
     own = hindcast_archive[0]
+    leads, members, fields, cells = own.shape
+    own = own.reshape(leads, members * fields, cells)
     outgoing = jnp.roll(own, here, axis=0)
     incoming = lax.all_to_all(outgoing, "tq", 0, 0, tiled=True)
     extended = extend(incoming[None])[0]
-    leads, members, fields, cells = extended.shape
-    ext_rows = extended.reshape(leads * members * fields, cells)
+    width = extended.shape[-1]
     adjoint_rows = observe(
-        ext_rows, op_blocks[0], block_index[0], obs_values[0], obs_weights[0], obs_counts[0]
+        extended.reshape(leads * members * fields, width),
+        op_blocks[0],
+        block_index[0],
+        obs_values[0],
+        obs_weights[0],
+        obs_counts[0],
     )
-    adjoint_ext = adjoint_rows.reshape(leads, members, fields, cells)[None]
-    interior = settle(adjoint_ext)[0]
+    interior = settle(adjoint_rows.reshape(1, leads, members * fields, width))[0]
     running = lax.dynamic_index_in_dim(interior, here, axis=0, keepdims=False)
     for shift in range(1, ring):
         back = lax.dynamic_index_in_dim(interior, (here - shift) % ring, axis=0, keepdims=False)
         running = running + passed_along(back, "tq", -shift)
-    return running[None]
+    return running.reshape(1, members, fields, cells)
 
 
 def solution(mesh):

time: 98.2 us -> 97.1 us (0.989)
  local copies, waits for them, and re-layouts: 2.34 us -> 4.5 us
  waiting for transfers between devices: 27.1 us -> 25.2 us
  other arithmetic: 3.66 us -> 2.21 us
    ppermute x5, waiting for transfers between devices: 25.4 us -> 23.3 us  [passed_along(): return lax.ppermute(value, axis, pairs)]
    concatenate x1, other arithmetic: 1.69 us -> 0.2 us  [body(): outgoing = jnp.roll(own, here, axis=0)]
    slice x1, local copies, waits for them, and re-layouts: 0.12 us -> 1.33 us  [settle(): interior = adjoint_ext[..., rim_width:-rim_width]]
    slice x1, local copies, waits for them, and re-layouts: 0.04 us -> 1.07 us  [settle(): upper_rim = adjoint_ext[..., -rim_width:]]
  transfers between devices with their start and end apart: 7 -> 7, of which waited for: 6 -> 6; matrix products, arithmetic and copies ran while one was open for 0% -> 2% of each run, Pallas kernels for 0% -> 0%
where the time goes in v7:
time: 97.1 us; the launch traced here: 96.4 us
  starting transfers between devices  29.9 us (31%)
  blocking collectives  25.8 us (27%)
  waiting for transfers between devices  25.2 us (26%)
  Pallas kernels  8.03 us (8%)
  local copies, waits for them, and re-layouts  4.5 us (5%)
  other arithmetic  2.21 us (2%)
    all_to_all x1, blocking collectives, body(): incoming = lax.all_to_all(outgoing, 'tq', 0, 0, tiled=True)  25.8 us
    ppermute x5, waiting for transfers between devices, passed_along(): return lax.ppermute(value, axis, pairs)  23.3 us
    ppermute x5, starting transfers between devices, passed_along(): return lax.ppermute(value, axis, pairs)  20.4 us
    pallas_call x1, Pallas kernels, observe(): pl.pallas_call(observe_kernel, grid_spec=grid_spec, out_shape=jax.ShapeDt...  8.03 us
    ppermute x1, starting transfers between devices, with_halo(): lax.ppermute(lax.slice_in_dim(block, 0, width, axis=dim), axis, backward)  6.01 us
    ppermute x1, starting transfers between devices, with_halo(): lax.ppermute(lax.slice_in_dim(block, block.shape[dim] - width, None, axis...  3.48 us
  transfers between devices with their start and end apart: 7, of which 6 were waited for; matrix products, arithmetic and copies ran while one was open for 2% of the time, Pallas kernels for 0%

profile of v7, /device:TPU:64, one launch (start us, length us, event | category | flops | bytes accessed | tf_op | source)
XLA Modules:
  0.0 96.4 jit_solution(3379092862426557905)
XLA Ops:
  0.0 1.2 %reshape_squeeze.4 = bf16[4,64,1024]{2,1,0:T(8,128)(2,1)S(1)} reshape(bf16[1,4,16,4,1024]{4,3,2,1,0:T(4,128)(2,1)} %param.10) | data formatting | bytes 1048576 | tf_op jit(solution)/shard_map/reshape;squeeze | solution.py:118
  1.2 0.2 fusion
  1.4 25.8 %all_to_all.5 = bf16[4,64,1024]{2,1,0:T(8,128)(2,1)S(1)} all-to-all(bf16[4,64,1024]{2,1,0:T(8,128)(2,1)S(1)} %fusion), channel_id=1, replica_groups=mesh['tq'=4,'tr'=4,'space'=32] {'tq'}, dimensions={0} | all-to-all | bytes 1048576 | tf_op jit(solution)/shard_map/all_to_all | solution.py:120
  27.2 3.5 %collective-permute-start = (bf16[1,4,64,256]{3,2,1,0:T(8,128)(2,1)S(1)}, bf16[1,4,64,256]{3,2,1,0:T(8,128)(2,1)S(1)}, u32[]{:S(2)}, u32[]{:S(2)}) collective-permute-start(bf16[1,4,64,256]{3,2,1,0:T(8,128)(2,1)S(1)} %get-tuple-element.34), channel_id=1, source_target_pairs={{0,1},{1,2},{2,3},{3,4},{4,5},{5,6},{6,7},{7,8},{8,9},{9,10},{10,1... | collective-permute-start | bytes 393224 | tf_op jit(solution)/shard_map/ppermute | solution.py:22
  30.7 6.0 %collective-permute-start.1 = (bf16[1,4,64,256]{3,2,1,0:T(8,128)(2,1)S(1)}, bf16[1,4,64,256]{3,2,1,0:T(8,128)(2,1)S(1)}, u32[]{:S(2)}, u32[]{:S(2)}) collective-permute-start(bf16[1,4,64,256]{3,2,1,0:T(8,128)(2,1)S(1)} %get-tuple-element.35), channel_id=1, source_target_pairs={{1,0},{2,1},{3,2},{4,3},{5,4},{6,5},{7,6},{8,7},{9,8},{10,9},{11,1... | collective-permute-start | bytes 393224 | tf_op jit(solution)/shard_map/ppermute | solution.py:25
  37.4 0.4 collective-permute-done
  37.7 1.5 %collective-permute-done.1 = bf16[1,4,64,256]{3,2,1,0:T(8,128)(2,1)S(1)} collective-permute-done((bf16[1,4,64,256]{3,2,1,0:T(8,128)(2,1)S(1)}, bf16[1,4,64,256]{3,2,1,0:T(8,128)(2,1)S(1)}, u32[]{:S(2)}, u32[]{:S(2)}) %collective-permute-start.1) | collective-permute-done | bytes 131104 | tf_op jit(solution)/shard_map/ppermute | solution.py:25
  39.2 0.9 pad_maximum_fusion.ext_ref
  40.1 8.0 %shard_map.64 = f32[256,1536]{1,0:T(8,128)} custom-call(s32[96]{0:T(128)} %bitcast.39, s32[1]{0:T(128)} %bitcast.27.cnt_ref, bf16[256,1536]{1,0:T(8,128)(2,1)} %pad_maximum_fusion.ext_ref, bf16[96,128,128]{2,1,0:T(8,128)(2,1)} %bitcast.36, bf16[4,12288]{1,0:T(4,128)(2,1)} %bitcast.37, bf16[4,12288]{1,0:T(4,128)(2,1)} %bitcast.38), custom_call_target="tpu_custom_call" | custom-call | flops 1610612736 | bytes 5701632 | tf_op jit(solution)/shard_map/pallas_call | solution.py:91
  48.2 1.1 %fusion.6 = (f32[1,4,64,256]{3,2,1,0:T(8,128)S(1)}, f32[1,4,64,256]{3,2,1,0:T(8,128)S(1)}) fusion(f32[1,4,64,1536]{3,2,1,0:T(8,128)} %bitcast.31), kind=kLoop, calls=%fused_computation.15 | loop fusion | bytes 1048576 | tf_op jit(solution)/shard_map/slice | solution.py:105
  49.2 7.7 %collective-permute-start.2 = (f32[1,4,64,256]{3,2,1,0:T(8,128)S(1)}, f32[1,4,64,256]{3,2,1,0:T(8,128)S(1)}, u32[]{:S(2)}, u32[]{:S(2)}) collective-permute-start(f32[1,4,64,256]{3,2,1,0:T(8,128)S(1)} %get-tuple-element.30), channel_id=1, source_target_pairs={{0,31},{1,0},{2,1},{3,2},{4,3},{5,4},{6,5},{7,6},{8,7},{9,8},{10,9... | collective-permute-start | bytes 786440 | tf_op jit(solution)/shard_map/ppermute | solution.py:33
  56.9 1.9 %collective-permute-start.3 = (f32[1,4,64,256]{3,2,1,0:T(8,128)S(1)}, f32[1,4,64,256]{3,2,1,0:T(8,128)S(1)}, u32[]{:S(2)}, u32[]{:S(2)}) collective-permute-start(f32[1,4,64,256]{3,2,1,0:T(8,128)S(1)} %get-tuple-element.29), channel_id=1, source_target_pairs={{0,1},{1,2},{2,3},{3,4},{4,5},{5,6},{6,7},{7,8},{8,9},{9,10},{10,1... | collective-permute-start | bytes 786440 | tf_op jit(solution)/shard_map/ppermute | solution.py:33
  58.9 1.3 %slice.83 = f32[1,4,64,1024]{3,2,1,0:T(8,128)S(1)} slice(f32[1,4,64,1536]{3,2,1,0:T(8,128)} %bitcast.32), slice={[0:1], [0:4], [0:64], [256:1280]} | slice | bytes 2097152 | tf_op jit(solution)/shard_map/slice | solution.py:106
  60.3 0.5 collective-permute-done.2
  60.8 1.0 %fusion.3 = f32[1,4,64,1024]{3,2,1,0:T(8,128)S(1)} fusion(f32[1,4,64,1024]{3,2,1,0:T(8,128)S(1)} %slice.83, f32[1,4,64,256]{3,2,1,0:T(8,128)S(1)} %collective-permute-done.2, f32[1,4,64,1536]{3,2,1,0:T(8,128)} %bitcast.33), kind=kLoop, calls=%fused_computation.8 | loop fusion | flops 65536 | bytes 786432 | tf_op jit(solution)/shard_map/scatter-add | solution.py:109
  61.8 0.1 copy.8
  61.9 6.6 %collective-permute-done.3 = f32[1,4,64,256]{3,2,1,0:T(8,128)S(1)} collective-permute-done((f32[1,4,64,256]{3,2,1,0:T(8,128)S(1)}, f32[1,4,64,256]{3,2,1,0:T(8,128)S(1)}, u32[]{:S(2)}, u32[]{:S(2)}) %collective-permute-start.3) | collective-permute-done | bytes 262176 | tf_op jit(solution)/shard_map/ppermute | solution.py:33
  68.6 0.1 dynamic-slice_bitcast_fusion.2
  68.6 4.0 %collective-permute-start.4 = (f32[64,1024]{1,0:T(8,128)S(1)}, f32[64,1024]{1,0:T(8,128)S(1)}, u32[]{:S(2)}, u32[]{:S(2)}) collective-permute-start(f32[64,1024]{1,0:T(8,128)S(1)} %get-tuple-element.31), channel_id=1, source_target_pairs={{0,384},{128,0},{256,128},{384,256},{1,385},{129,1},{257,129},{385... | collective-permute-start | bytes 786440 | tf_op jit(solution)/shard_map/ppermute | solution.py:33
  72.7 3.8 %collective-permute-start.5 = (f32[64,1024]{1,0:T(8,128)S(1)}, f32[64,1024]{1,0:T(8,128)S(1)}, u32[]{:S(2)}, u32[]{:S(2)}) collective-permute-start(f32[64,1024]{1,0:T(8,128)S(1)} %get-tuple-element.33), channel_id=1, source_target_pairs={{0,256},{128,384},{256,0},{384,128},{1,257},{129,385},{257,1},{385... | collective-permute-start | bytes 786440 | tf_op jit(solution)/shard_map/ppermute | solution.py:33
  76.6 2.9 %collective-permute-start.6 = (f32[64,1024]{1,0:T(8,128)S(1)}, f32[64,1024]{1,0:T(8,128)S(1)}, u32[]{:S(2)}, u32[]{:S(2)}) collective-permute-start(f32[64,1024]{1,0:T(8,128)S(1)} %get-tuple-element.32), channel_id=1, source_target_pairs={{0,128},{128,256},{256,384},{384,0},{1,129},{129,257},{257,385},{3... | collective-permute-start | bytes 786440 | tf_op jit(solution)/shard_map/ppermute | solution.py:33
  79.5 9.1 %collective-permute-done.4 = f32[64,1024]{1,0:T(8,128)S(1)} collective-permute-done((f32[64,1024]{1,0:T(8,128)S(1)}, f32[64,1024]{1,0:T(8,128)S(1)}, u32[]{:S(2)}, u32[]{:S(2)}) %collective-permute-start.4) | collective-permute-done | bytes 262176 | tf_op jit(solution)/shard_map/ppermute | solution.py:33
  88.6 0.0 collective-permute-done.5
  88.6 7.0 %collective-permute-done.6 = f32[64,1024]{1,0:T(8,128)S(1)} collective-permute-done((f32[64,1024]{1,0:T(8,128)S(1)}, f32[64,1024]{1,0:T(8,128)S(1)}, u32[]{:S(2)}, u32[]{:S(2)}) %collective-permute-start.6) | collective-permute-done | bytes 262176 | tf_op jit(solution)/shard_map/ppermute | solution.py:33
  95.6 0.1 fusion.5
  95.7 0.8 reshape.83
  (2 shorter events, 0.1 us)
Async XLA Ops:
  27.2 10.5 %collective-permute-start = (bf16[1,4,64,256]{3,2,1,0:T(8,128)(2,1)S(1)}, bf16[1,4,64,256]{3,2,1,0:T(8,128)(2,1)S(1)}, u32[]{:S(2)}, u32[]{:S(2)}) collective-permute-start(bf16[1,4,64,256]{3,2,1,0:T(8,128)(2,1)S(1)} %get-tuple-element.34), channel_id=1, source_target_pairs={{0,1},{1,2},{2,3},{3,4},{4,5},{5,6},{6,7},{7,8},{8,9},{9,10},{10,1... | collective-permute-start | bytes 393224 | tf_op jit(solution)/shard_map/ppermute | solution.py:22
  30.7 8.5 %collective-permute-start.1 = (bf16[1,4,64,256]{3,2,1,0:T(8,128)(2,1)S(1)}, bf16[1,4,64,256]{3,2,1,0:T(8,128)(2,1)S(1)}, u32[]{:S(2)}, u32[]{:S(2)}) collective-permute-start(bf16[1,4,64,256]{3,2,1,0:T(8,128)(2,1)S(1)} %get-tuple-element.35), channel_id=1, source_target_pairs={{1,0},{2,1},{3,2},{4,3},{5,4},{6,5},{7,6},{8,7},{9,8},{10,9},{11,1... | collective-permute-start | bytes 393224 | tf_op jit(solution)/shard_map/ppermute | solution.py:25
  49.2 11.6 %collective-permute-start.2 = (f32[1,4,64,256]{3,2,1,0:T(8,128)S(1)}, f32[1,4,64,256]{3,2,1,0:T(8,128)S(1)}, u32[]{:S(2)}, u32[]{:S(2)}) collective-permute-start(f32[1,4,64,256]{3,2,1,0:T(8,128)S(1)} %get-tuple-element.30), channel_id=1, source_target_pairs={{0,31},{1,0},{2,1},{3,2},{4,3},{5,4},{6,5},{7,6},{8,7},{9,8},{10,9... | collective-permute-start | bytes 786440 | tf_op jit(solution)/shard_map/ppermute | solution.py:33
  56.9 11.6 %collective-permute-start.3 = (f32[1,4,64,256]{3,2,1,0:T(8,128)S(1)}, f32[1,4,64,256]{3,2,1,0:T(8,128)S(1)}, u32[]{:S(2)}, u32[]{:S(2)}) collective-permute-start(f32[1,4,64,256]{3,2,1,0:T(8,128)S(1)} %get-tuple-element.29), channel_id=1, source_target_pairs={{0,1},{1,2},{2,3},{3,4},{4,5},{5,6},{6,7},{7,8},{8,9},{9,10},{10,1... | collective-permute-start | bytes 786440 | tf_op jit(solution)/shard_map/ppermute | solution.py:33
  68.6 20.0 %collective-permute-start.4 = (f32[64,1024]{1,0:T(8,128)S(1)}, f32[64,1024]{1,0:T(8,128)S(1)}, u32[]{:S(2)}, u32[]{:S(2)}) collective-permute-start(f32[64,1024]{1,0:T(8,128)S(1)} %get-tuple-element.31), channel_id=1, source_target_pairs={{0,384},{128,0},{256,128},{384,256},{1,385},{129,1},{257,129},{385... | collective-permute-start | bytes 786440 | tf_op jit(solution)/shard_map/ppermute | solution.py:33
  72.7 15.9 %collective-permute-start.5 = (f32[64,1024]{1,0:T(8,128)S(1)}, f32[64,1024]{1,0:T(8,128)S(1)}, u32[]{:S(2)}, u32[]{:S(2)}) collective-permute-start(f32[64,1024]{1,0:T(8,128)S(1)} %get-tuple-element.33), channel_id=1, source_target_pairs={{0,256},{128,384},{256,0},{384,128},{1,257},{129,385},{257,1},{385... | collective-permute-start | bytes 786440 | tf_op jit(solution)/shard_map/ppermute | solution.py:33
  76.6 19.1 %collective-permute-start.6 = (f32[64,1024]{1,0:T(8,128)S(1)}, f32[64,1024]{1,0:T(8,128)S(1)}, u32[]{:S(2)}, u32[]{:S(2)}) collective-permute-start(f32[64,1024]{1,0:T(8,128)S(1)} %get-tuple-element.32), channel_id=1, source_target_pairs={{0,128},{128,256},{256,384},{384,0},{1,129},{129,257},{257,385},{3... | collective-permute-start | bytes 786440 | tf_op jit(solution)/shard_map/ppermute | solution.py:33

commit v8 on v7

--- a/solution.py
+++ b/solution.py
@@ -27,6 +27,10 @@
     return block
 
 
+def ring_pairs(count, steps):
+    return [(source, (source + steps) % count) for source in range(count)]
+
+
 def passed_along(value, axis, steps):
     count = lax.axis_size(axis)
     pairs = [(source, (source + steps) % count) for source in range(count)]
@@ -37,16 +41,24 @@
     return with_halo(grouped, (("space", grouped.ndim - 1),), EDGE * GROUP_SITE_SPAN)
 
 
-def observe_kernel(idx_ref, cnt_ref, ext_ref, op_ref, val_ref, wt_ref, out_ref):
+def observe_kernel(
+    idx_ref, cnt_ref, low_ref, mid_ref, high_ref, op_ref, val_ref, wt_ref,
+    low_out, mid_out, high_out, ext_ref, acc_ref,
+):
     step = pl.program_id(0)
     width = GROUP_SITE_SPAN
     fields = val_ref.shape[0]
     rows = ext_ref.shape[0]
+    rim = low_ref.shape[1]
+    tile = mid_ref.shape[1]
     period = 8
 
     @pl.when(step == 0)
     def _():
-        out_ref[...] = jnp.zeros_like(out_ref)
+        ext_ref[:, :rim] = low_ref[...]
+        ext_ref[:, rim:rim + tile] = mid_ref[...]
+        ext_ref[:, rim + tile:] = high_ref[...]
+        acc_ref[...] = jnp.zeros_like(acc_ref)
 
     count = cnt_ref[0]
     lane = lax.broadcasted_iota(jnp.int32, (1, width), 1)
@@ -65,38 +77,61 @@
         scaling = jnp.concatenate([scaling] * (period // fields), axis=0)[None]
         misfit = ((images - observed) * scaling).reshape(rows, width).astype(jnp.bfloat16)
         adjoint = jnp.dot(misfit, op, preferred_element_type=jnp.float32)
-        out_ref[:, pl.ds(start, width)] += adjoint
+        acc_ref[:, pl.ds(start, width)] += adjoint
+
+    @pl.when(step == pl.num_programs(0) - 1)
+    def _():
+        low_out[...] = acc_ref[:, :rim]
+        mid_out[...] = acc_ref[:, rim:rim + tile]
+        high_out[...] = acc_ref[:, rim + tile:]
 
 
-def observe(ext_rows, operator, indices, values, weights, counts):
-    rows, cells = ext_rows.shape
+def observe(low, mid, high, operator, indices, values, weights, counts):
+    rows, tile = mid.shape
+    rim = low.shape[1]
+    cells = tile + 2 * rim
     obs_blocks = operator.shape[0]
     width = GROUP_SITE_SPAN
     fields = values.shape[0]
     steps = obs_blocks // BLOCKS_PER_STEP
     span = BLOCKS_PER_STEP * width
+    whole = lambda g, i, c: (0, 0)
     grid_spec = pltpu.PrefetchScalarGridSpec(
         num_scalar_prefetch=2,
         grid=(steps,),
         in_specs=[
-            pl.BlockSpec((rows, cells), lambda g, i, c: (0, 0)),
+            pl.BlockSpec((rows, rim), whole),
+            pl.BlockSpec((rows, tile), whole),
+            pl.BlockSpec((rows, rim), whole),
             pl.BlockSpec((BLOCKS_PER_STEP, width, width), lambda g, i, c: (g, 0, 0)),
             pl.BlockSpec((fields, span), lambda g, i, c: (0, g)),
             pl.BlockSpec((fields, span), lambda g, i, c: (0, g)),
         ],
-        out_specs=pl.BlockSpec((rows, cells), lambda g, i, c: (0, 0)),
+        out_specs=[
+            pl.BlockSpec((rows, rim), whole),
+            pl.BlockSpec((rows, tile), whole),
+            pl.BlockSpec((rows, rim), whole),
+        ],
+        scratch_shapes=[
+            pltpu.VMEM((rows, cells), mid.dtype),
+            pltpu.VMEM((rows, cells), jnp.float32),
+        ],
     )
     flops = 4 * obs_blocks * rows * width * width
-    bytes_accessed = operator.size * 2 + ext_rows.size * 2 + rows * cells * 4 + values.size * 4
+    bytes_accessed = operator.size * 2 + rows * cells * 6 + values.size * 4
     return pl.pallas_call(
         observe_kernel,
         grid_spec=grid_spec,
-        out_shape=jax.ShapeDtypeStruct((rows, cells), jnp.float32),
+        out_shape=[
+            jax.ShapeDtypeStruct((rows, rim), jnp.float32),
+            jax.ShapeDtypeStruct((rows, tile), jnp.float32),
+            jax.ShapeDtypeStruct((rows, rim), jnp.float32),
+        ],
         compiler_params=pltpu.CompilerParams(dimension_semantics=("arbitrary",)),
         cost_estimate=pl.CostEstimate(
             flops=flops, bytes_accessed=bytes_accessed, transcendentals=0
         ),
-    )(indices, counts, ext_rows, operator, values, weights)
+    )(indices, counts, low, mid, high, operator, values, weights)
 
 
 def settle(adjoint_ext):
@@ -111,24 +146,33 @@
 
 
 def body(hindcast_archive, op_blocks, block_index, obs_values, obs_weights, obs_counts):
+    rim = EDGE * GROUP_SITE_SPAN
+    space = lax.axis_size("space")
     ring = lax.axis_size("tq")
     here = lax.axis_index("tq")
     own = hindcast_archive[0]
     leads, members, fields, cells = own.shape
-    own = own.reshape(leads, members * fields, cells)
+    rows = members * fields
+    own = own.reshape(leads, rows, cells)
     outgoing = jnp.roll(own, here, axis=0)
     incoming = lax.all_to_all(outgoing, "tq", 0, 0, tiled=True)
-    extended = extend(incoming[None])[0]
-    width = extended.shape[-1]
-    adjoint_rows = observe(
-        extended.reshape(leads * members * fields, width),
+    low = lax.ppermute(incoming[..., cells - rim:], "space", ring_pairs(space, 1))
+    high = lax.ppermute(incoming[..., :rim], "space", ring_pairs(space, -1))
+    low_adj, interior, high_adj = observe(
+        low.reshape(leads * rows, rim),
+        incoming.reshape(leads * rows, cells),
+        high.reshape(leads * rows, rim),
         op_blocks[0],
         block_index[0],
         obs_values[0],
         obs_weights[0],
         obs_counts[0],
     )
-    interior = settle(adjoint_rows.reshape(1, leads, members * fields, width))[0]
+    from_above = lax.ppermute(low_adj.reshape(leads, rows, rim), "space", ring_pairs(space, -1))
+    from_below = lax.ppermute(high_adj.reshape(leads, rows, rim), "space", ring_pairs(space, 1))
+    interior = interior.reshape(leads, rows, cells)
+    interior = interior.at[..., cells - rim:].add(from_above)
+    interior = interior.at[..., :rim].add(from_below)
     running = lax.dynamic_index_in_dim(interior, here, axis=0, keepdims=False)
     for shift in range(1, ring):
         back = lax.dynamic_index_in_dim(interior, (here - shift) % ring, axis=0, keepdims=False)

time: 97.1 us -> 99.9 us (1.029)
  other arithmetic: 2.21 us -> 4.73 us
    ppermute x2 -> x4, starting transfers between devices: 9.49 us -> 19.1 us  [the longest x1 7.68 us: body(): lax.ppermute(low_adj.reshape(leads, rows, rim), 'space', ring_pairs(space...]
    ppermute x5 -> x3, starting transfers between devices: 20.4 us -> 10.8 us  [passed_along(): return lax.ppermute(value, axis, pairs)]
    ppermute x2 -> x4, waiting for transfers between devices: 1.85 us -> 9.89 us  [the longest x1 5.84 us: body(): lax.ppermute(high_adj.reshape(leads, rows, rim), 'space', ring_pairs(spac...]
    ppermute x5 -> x3, waiting for transfers between devices: 23.3 us -> 16.1 us  [passed_along(): return lax.ppermute(value, axis, pairs)]
    scatter-add x2, other arithmetic: 1.02 us -> 3.52 us  [the longest x1 1.77 us: body(): interior = interior.at[..., cells - rim:].add(from_above)]
    slice x3 -> x1, local copies, waits for them, and re-layouts: 2.42 us -> 0.02 us  [body(): high = lax.ppermute(incoming[..., :rim], 'space', ring_pairs(space, -1))]
    squeeze x1, local copies, waits for them, and re-layouts: 0.08 us -> 1.16 us  [body(): lax.dynamic_index_in_dim(interior, (here - shift) % ring, axis=0, keepdim...]
where the time goes in v8:
time: 99.9 us; the launch traced here: 99.2 us
  starting transfers between devices  29.9 us (30%)
  waiting for transfers between devices  26 us (26%)
  blocking collectives  25.8 us (26%)
  Pallas kernels  8.16 us (8%)
  other arithmetic  4.73 us (5%)
  local copies, waits for them, and re-layouts  3.77 us (4%)
    all_to_all x1, blocking collectives, body(): incoming = lax.all_to_all(outgoing, 'tq', 0, 0, tiled=True)  25.8 us
    ppermute x3, waiting for transfers between devices, passed_along(): return lax.ppermute(value, axis, pairs)  16.1 us
    ppermute x3, starting transfers between devices, passed_along(): return lax.ppermute(value, axis, pairs)  10.8 us
    pallas_call x1, Pallas kernels, observe(): pl.pallas_call(observe_kernel, grid_spec=grid_spec, out_shape=[jax.ShapeD...  8.16 us
    ppermute x1, starting transfers between devices, body(): lax.ppermute(low_adj.reshape(leads, rows, rim), 'space', ring_pairs(space...  7.68 us
    ppermute x1, starting transfers between devices, body(): high = lax.ppermute(incoming[..., :rim], 'space', ring_pairs(space, -1))  6.01 us
    ppermute x1, waiting for transfers between devices, body(): lax.ppermute(high_adj.reshape(leads, rows, rim), 'space', ring_pairs(spac...  5.84 us
    ppermute x1, starting transfers between devices, body(): lax.ppermute(incoming[..., cells - rim:], 'space', ring_pairs(space, 1))  3.48 us
  transfers between devices with their start and end apart: 7, of which 6 were waited for; matrix products, arithmetic and copies ran while one was open for 2% of the time, Pallas kernels for 0%

profile of v8, /device:TPU:64, one launch (start us, length us, event | category | flops | bytes accessed | tf_op | source)
XLA Modules:
  0.0 99.2 jit_solution(776675418703391064)
XLA Ops:
  0.0 1.2 %reshape_squeeze.3 = bf16[4,64,1024]{2,1,0:T(8,128)(2,1)S(1)} reshape(bf16[1,4,16,4,1024]{4,3,2,1,0:T(4,128)(2,1)} %param.10) | data formatting | bytes 1048576 | tf_op jit(solution)/shard_map/reshape;squeeze | solution.py:156
  1.2 0.2 fusion
  1.4 25.8 %all_to_all.5 = bf16[4,64,1024]{2,1,0:T(8,128)(2,1)S(1)} all-to-all(bf16[4,64,1024]{2,1,0:T(8,128)(2,1)S(1)} %fusion), channel_id=1, replica_groups=mesh['tq'=4,'tr'=4,'space'=32] {'tq'}, dimensions={0} | all-to-all | bytes 1048576 | tf_op jit(solution)/shard_map/all_to_all | solution.py:158
  27.2 0.0 copy-start
  27.2 3.5 %collective-permute-start = (bf16[4,64,256]{2,1,0:T(8,128)(2,1)S(1)}, bf16[4,64,256]{2,1,0:T(8,128)(2,1)S(1)}, u32[]{:S(2)}, u32[]{:S(2)}) collective-permute-start(bf16[4,64,256]{2,1,0:T(8,128)(2,1)S(1)} %get-tuple-element.39), channel_id=1, source_target_pairs={{0,1},{1,2},{2,3},{3,4},{4,5},{5,6},{6,7},{7,8},{8,9},{9,10},{10,1... | collective-permute-start | bytes 393224 | tf_op jit(solution)/shard_map/ppermute | solution.py:159
  30.7 6.0 %collective-permute-start.1 = (bf16[4,64,256]{2,1,0:T(8,128)(2,1)S(1)}, bf16[4,64,256]{2,1,0:T(8,128)(2,1)S(1)}, u32[]{:S(2)}, u32[]{:S(2)}) collective-permute-start(bf16[4,64,256]{2,1,0:T(8,128)(2,1)S(1)} %get-tuple-element.38), channel_id=1, source_target_pairs={{0,31},{1,0},{2,1},{3,2},{4,3},{5,4},{6,5},{7,6},{8,7},{9,8},{10,9... | collective-permute-start | bytes 393224 | tf_op jit(solution)/shard_map/ppermute | solution.py:160
  37.4 0.4 collective-permute-done
  37.7 0.0 copy-start.1
  37.7 1.5 %collective-permute-done.1 = bf16[4,64,256]{2,1,0:T(8,128)(2,1)S(1)} collective-permute-done((bf16[4,64,256]{2,1,0:T(8,128)(2,1)S(1)}, bf16[4,64,256]{2,1,0:T(8,128)(2,1)S(1)}, u32[]{:S(2)}, u32[]{:S(2)}) %collective-permute-start.1) | collective-permute-done | bytes 131104 | tf_op jit(solution)/shard_map/ppermute | solution.py:160
  39.2 0.0 copy-start.2
  39.2 0.0 copy-done
  39.2 0.0 copy-done.1
  39.2 0.6 copy-done.2
  39.9 8.2 %shard_map.64 = (f32[256,256]{1,0:T(8,128)}, f32[256,1024]{1,0:T(8,128)}, f32[256,256]{1,0:T(8,128)}) custom-call(s32[96]{0:T(128)} %bitcast.33, s32[1]{0:T(128)} %bitcast.23.cnt_ref, bf16[256,256]{1,0:T(8,128)(2,1)} %bitcast.29, bf16[256,1024]{1,0:T(8,128)(2,1)} %bitcast.25, bf16[256,256]{1,0:T(8,128)(2,1)} %bitcast.30, bf16[96,128,128]{2,1,0:T(8,128)(2,1)} %bitcast.26, ...), custom_call_target="tpu_custom_call" | custom-call | flops 1610612736 | bytes 5701632 | tf_op jit(solution)/shard_map/pallas_call | solution.py:122
  48.0 7.7 %collective-permute-start.2 = (f32[4,64,256]{2,1,0:T(8,128)}, f32[4,64,256]{2,1,0:T(8,128)S(1)}, u32[]{:S(2)}, u32[]{:S(2)}) collective-permute-start(f32[4,64,256]{2,1,0:T(8,128)} %bitcast.28), channel_id=1, source_target_pairs={{0,31},{1,0},{2,1},{3,2},{4,3},{5,4},{6,5},{7,6},{8,7},{9,8},{10,9... | collective-permute-start | bytes 786440 | tf_op jit(solution)/shard_map/ppermute | solution.py:171
  55.7 1.9 %collective-permute-start.3 = (f32[4,64,256]{2,1,0:T(8,128)}, f32[4,64,256]{2,1,0:T(8,128)S(1)}, u32[]{:S(2)}, u32[]{:S(2)}) collective-permute-start(f32[4,64,256]{2,1,0:T(8,128)} %bitcast.27), channel_id=1, source_target_pairs={{0,1},{1,2},{2,3},{3,4},{4,5},{5,6},{6,7},{7,8},{8,9},{9,10},{10,1... | collective-permute-start | bytes 786440 | tf_op jit(solution)/shard_map/ppermute | solution.py:172
  57.7 2.2 %collective-permute-done.2 = f32[4,64,256]{2,1,0:T(8,128)S(1)} collective-permute-done((f32[4,64,256]{2,1,0:T(8,128)}, f32[4,64,256]{2,1,0:T(8,128)S(1)}, u32[]{:S(2)}, u32[]{:S(2)}) %collective-permute-start.2) | collective-permute-done | bytes 262176 | tf_op jit(solution)/shard_map/ppermute | solution.py:171
  59.9 1.8 %fusion.2 = f32[4,64,1024]{2,1,0:T(8,128)} fusion(f32[4,64,1024]{2,1,0:T(8,128)} %bitcast.24, f32[4,64,256]{2,1,0:T(8,128)S(1)} %collective-permute-done.2), kind=kLoop, calls=%fused_computation.6 | loop fusion | flops 65536 | bytes 786432 | tf_op jit(solution)/shard_map/scatter-add | solution.py:174
  61.7 5.8 %collective-permute-done.3 = f32[4,64,256]{2,1,0:T(8,128)S(1)} collective-permute-done((f32[4,64,256]{2,1,0:T(8,128)}, f32[4,64,256]{2,1,0:T(8,128)S(1)}, u32[]{:S(2)}, u32[]{:S(2)}) %collective-permute-start.3) | collective-permute-done | bytes 262176 | tf_op jit(solution)/shard_map/ppermute | solution.py:172
  67.5 1.8 %fusion.1 = f32[4,64,1024]{2,1,0:T(8,128)} fusion(f32[4,64,1024]{2,1,0:T(8,128)} %fusion.2, f32[4,64,256]{2,1,0:T(8,128)S(1)} %collective-permute-done.3), kind=kLoop, calls=%fused_computation.4 | loop fusion | flops 65536 | bytes 786432 | tf_op jit(solution)/shard_map/scatter-add | solution.py:175
  69.3 1.2 %dynamic-slice_bitcast_fusion.2 = (f32[64,1024]{1,0:T(8,128)S(1)}, f32[64,1024]{1,0:T(8,128)S(1)}, f32[64,1024]{1,0:T(8,128)S(1)}) fusion(f32[4,64,1024]{2,1,0:T(8,128)} %fusion.1, s32[]{:T(128)S(6)} %select_n.44, s32[]{:T(128)S(6)} %select_n.48, s32[]{:T(128)S(6)} %select_n.46), kind=kLoop, calls=%fused_computation.12 | loop fusion | bytes 1572876 | tf_op jit(solution)/shard_map/jit(dynamic_index_in_dim)/squeeze | solution.py:178
  70.4 4.0 %collective-permute-start.4 = (f32[64,1024]{1,0:T(8,128)S(1)}, f32[64,1024]{1,0:T(8,128)S(1)}, u32[]{:S(2)}, u32[]{:S(2)}) collective-permute-start(f32[64,1024]{1,0:T(8,128)S(1)} %get-tuple-element.35), channel_id=1, source_target_pairs={{0,384},{128,0},{256,128},{384,256},{1,385},{129,1},{257,129},{385... | collective-permute-start | bytes 786440 | tf_op jit(solution)/shard_map/ppermute | solution.py:37
  74.5 3.9 %collective-permute-start.5 = (f32[64,1024]{1,0:T(8,128)S(1)}, f32[64,1024]{1,0:T(8,128)S(1)}, u32[]{:S(2)}, u32[]{:S(2)}) collective-permute-start(f32[64,1024]{1,0:T(8,128)S(1)} %get-tuple-element.37), channel_id=1, source_target_pairs={{0,256},{128,384},{256,0},{384,128},{1,257},{129,385},{257,1},{385... | collective-permute-start | bytes 786440 | tf_op jit(solution)/shard_map/ppermute | solution.py:37
  78.3 2.9 %collective-permute-start.6 = (f32[64,1024]{1,0:T(8,128)S(1)}, f32[64,1024]{1,0:T(8,128)S(1)}, u32[]{:S(2)}, u32[]{:S(2)}) collective-permute-start(f32[64,1024]{1,0:T(8,128)S(1)} %get-tuple-element.36), channel_id=1, source_target_pairs={{0,128},{128,256},{256,384},{384,0},{1,129},{129,257},{257,385},{3... | collective-permute-start | bytes 786440 | tf_op jit(solution)/shard_map/ppermute | solution.py:37
  81.3 9.1 %collective-permute-done.4 = f32[64,1024]{1,0:T(8,128)S(1)} collective-permute-done((f32[64,1024]{1,0:T(8,128)S(1)}, f32[64,1024]{1,0:T(8,128)S(1)}, u32[]{:S(2)}, u32[]{:S(2)}) %collective-permute-start.4) | collective-permute-done | bytes 262176 | tf_op jit(solution)/shard_map/ppermute | solution.py:37
  90.4 0.0 collective-permute-done.5
  90.4 7.0 %collective-permute-done.6 = f32[64,1024]{1,0:T(8,128)S(1)} collective-permute-done((f32[64,1024]{1,0:T(8,128)S(1)}, f32[64,1024]{1,0:T(8,128)S(1)}, u32[]{:S(2)}, u32[]{:S(2)}) %collective-permute-start.6) | collective-permute-done | bytes 262176 | tf_op jit(solution)/shard_map/ppermute | solution.py:37
  97.4 1.0 %fusion.4 = f32[64,1024]{1,0:T(8,128)S(1)} fusion(f32[64,1024]{1,0:T(8,128)S(1)} %collective-permute-done.6, f32[64,1024]{1,0:T(8,128)S(1)} %collective-permute-done.5, f32[64,1024]{1,0:T(8,128)S(1)} %collective-permute-done.4, f32[4,64,1024]{2,1,0:T(8,128)} %fusion.1, s32[]{:T(128)S(6)} %select_n.42), kind=kLoop, calls=%fused_computation.9 | loop fusion | flops 196608 | bytes 1310724 | tf_op jit(solution)/shard_map/add | solution.py:179
  98.4 0.8 reshape.87
  (1 shorter events, 0.0 us)
Async XLA Ops:
  27.2 12.0 %copy-start = (bf16[4,64,1024]{2,1,0:T(8,128)(2,1)}, bf16[4,64,1024]{2,1,0:T(8,128)(2,1)S(1)}, u32[]{:S(2)}) copy-start(bf16[4,64,1024]{2,1,0:T(8,128)(2,1)S(1)} %all_to_all.5) | copy-start | bytes 1572868
  27.2 10.5 %collective-permute-start = (bf16[4,64,256]{2,1,0:T(8,128)(2,1)S(1)}, bf16[4,64,256]{2,1,0:T(8,128)(2,1)S(1)}, u32[]{:S(2)}, u32[]{:S(2)}) collective-permute-start(bf16[4,64,256]{2,1,0:T(8,128)(2,1)S(1)} %get-tuple-element.39), channel_id=1, source_target_pairs={{0,1},{1,2},{2,3},{3,4},{4,5},{5,6},{6,7},{7,8},{8,9},{9,10},{10,1... | collective-permute-start | bytes 393224 | tf_op jit(solution)/shard_map/ppermute | solution.py:159
  30.7 8.5 %collective-permute-start.1 = (bf16[4,64,256]{2,1,0:T(8,128)(2,1)S(1)}, bf16[4,64,256]{2,1,0:T(8,128)(2,1)S(1)}, u32[]{:S(2)}, u32[]{:S(2)}) collective-permute-start(bf16[4,64,256]{2,1,0:T(8,128)(2,1)S(1)} %get-tuple-element.38), channel_id=1, source_target_pairs={{0,31},{1,0},{2,1},{3,2},{4,3},{5,4},{6,5},{7,6},{8,7},{9,8},{10,9... | collective-permute-start | bytes 393224 | tf_op jit(solution)/shard_map/ppermute | solution.py:160
  37.7 1.5 %copy-start.1 = (bf16[4,64,256]{2,1,0:T(8,128)(2,1)}, bf16[4,64,256]{2,1,0:T(8,128)(2,1)S(1)}, u32[]{:S(2)}) copy-start(bf16[4,64,256]{2,1,0:T(8,128)(2,1)S(1)} %collective-permute-done) | copy-start | bytes 393220
  39.2 0.7 copy-start.2
  48.0 11.9 %collective-permute-start.2 = (f32[4,64,256]{2,1,0:T(8,128)}, f32[4,64,256]{2,1,0:T(8,128)S(1)}, u32[]{:S(2)}, u32[]{:S(2)}) collective-permute-start(f32[4,64,256]{2,1,0:T(8,128)} %bitcast.28), channel_id=1, source_target_pairs={{0,31},{1,0},{2,1},{3,2},{4,3},{5,4},{6,5},{7,6},{8,7},{9,8},{10,9... | collective-permute-start | bytes 786440 | tf_op jit(solution)/shard_map/ppermute | solution.py:171
  55.7 11.8 %collective-permute-start.3 = (f32[4,64,256]{2,1,0:T(8,128)}, f32[4,64,256]{2,1,0:T(8,128)S(1)}, u32[]{:S(2)}, u32[]{:S(2)}) collective-permute-start(f32[4,64,256]{2,1,0:T(8,128)} %bitcast.27), channel_id=1, source_target_pairs={{0,1},{1,2},{2,3},{3,4},{4,5},{5,6},{6,7},{7,8},{8,9},{9,10},{10,1... | collective-permute-start | bytes 786440 | tf_op jit(solution)/shard_map/ppermute | solution.py:172
  70.4 20.0 %collective-permute-start.4 = (f32[64,1024]{1,0:T(8,128)S(1)}, f32[64,1024]{1,0:T(8,128)S(1)}, u32[]{:S(2)}, u32[]{:S(2)}) collective-permute-start(f32[64,1024]{1,0:T(8,128)S(1)} %get-tuple-element.35), channel_id=1, source_target_pairs={{0,384},{128,0},{256,128},{384,256},{1,385},{129,1},{257,129},{385... | collective-permute-start | bytes 786440 | tf_op jit(solution)/shard_map/ppermute | solution.py:37
  74.5 15.9 %collective-permute-start.5 = (f32[64,1024]{1,0:T(8,128)S(1)}, f32[64,1024]{1,0:T(8,128)S(1)}, u32[]{:S(2)}, u32[]{:S(2)}) collective-permute-start(f32[64,1024]{1,0:T(8,128)S(1)} %get-tuple-element.37), channel_id=1, source_target_pairs={{0,256},{128,384},{256,0},{384,128},{1,257},{129,385},{257,1},{385... | collective-permute-start | bytes 786440 | tf_op jit(solution)/shard_map/ppermute | solution.py:37
  78.3 19.0 %collective-permute-start.6 = (f32[64,1024]{1,0:T(8,128)S(1)}, f32[64,1024]{1,0:T(8,128)S(1)}, u32[]{:S(2)}, u32[]{:S(2)}) collective-permute-start(f32[64,1024]{1,0:T(8,128)S(1)} %get-tuple-element.36), channel_id=1, source_target_pairs={{0,128},{128,256},{256,384},{384,0},{1,129},{129,257},{257,385},{3... | collective-permute-start | bytes 786440 | tf_op jit(solution)/shard_map/ppermute | solution.py:37

commit v9 on v7

--- a/solution.py
+++ b/solution.py
@@ -130,7 +130,7 @@
     )
     interior = settle(adjoint_rows.reshape(1, leads, members * fields, width))[0]
     running = lax.dynamic_index_in_dim(interior, here, axis=0, keepdims=False)
-    for shift in range(1, ring):
+    for shift in sorted(range(1, ring), key=lambda d: -min(d, ring - d)):
         back = lax.dynamic_index_in_dim(interior, (here - shift) % ring, axis=0, keepdims=False)
         running = running + passed_along(back, "tq", -shift)
     return running.reshape(1, members, fields, cells)

time: 97.1 us -> 97.2 us (level)
  no operation moved by 1% of the time
where the time goes in v9:
time: 97.2 us; the launch traced here: 96.7 us
  starting transfers between devices  29.9 us (31%)
  blocking collectives  25.8 us (27%)
  waiting for transfers between devices  25.4 us (26%)
  Pallas kernels  8.03 us (8%)
  local copies, waits for them, and re-layouts  4.5 us (5%)
  other arithmetic  2.21 us (2%)
    all_to_all x1, blocking collectives, body(): incoming = lax.all_to_all(outgoing, 'tq', 0, 0, tiled=True)  25.8 us
    ppermute x5, waiting for transfers between devices, passed_along(): return lax.ppermute(value, axis, pairs)  23.5 us
    ppermute x5, starting transfers between devices, passed_along(): return lax.ppermute(value, axis, pairs)  20.4 us
    pallas_call x1, Pallas kernels, observe(): pl.pallas_call(observe_kernel, grid_spec=grid_spec, out_shape=jax.ShapeDt...  8.03 us
    ppermute x1, starting transfers between devices, with_halo(): lax.ppermute(lax.slice_in_dim(block, 0, width, axis=dim), axis, backward)  6.01 us
    ppermute x1, starting transfers between devices, with_halo(): lax.ppermute(lax.slice_in_dim(block, block.shape[dim] - width, None, axis...  3.48 us
  transfers between devices with their start and end apart: 7, of which 6 were waited for; matrix products, arithmetic and copies ran while one was open for 2% of the time, Pallas kernels for 0%

profile of v9, /device:TPU:64, one launch (start us, length us, event | category | flops | bytes accessed | tf_op | source)
XLA Modules:
  0.0 96.7 jit_solution(1966395934477333676)
XLA Ops:
  0.0 1.2 %reshape_squeeze.4 = bf16[4,64,1024]{2,1,0:T(8,128)(2,1)S(1)} reshape(bf16[1,4,16,4,1024]{4,3,2,1,0:T(4,128)(2,1)} %param.10) | data formatting | bytes 1048576 | tf_op jit(solution)/shard_map/reshape;squeeze | solution.py:118
  1.2 0.2 fusion
  1.4 25.8 %all_to_all.5 = bf16[4,64,1024]{2,1,0:T(8,128)(2,1)S(1)} all-to-all(bf16[4,64,1024]{2,1,0:T(8,128)(2,1)S(1)} %fusion), channel_id=1, replica_groups=mesh['tq'=4,'tr'=4,'space'=32] {'tq'}, dimensions={0} | all-to-all | bytes 1048576 | tf_op jit(solution)/shard_map/all_to_all | solution.py:120
  27.2 3.5 %collective-permute-start = (bf16[1,4,64,256]{3,2,1,0:T(8,128)(2,1)S(1)}, bf16[1,4,64,256]{3,2,1,0:T(8,128)(2,1)S(1)}, u32[]{:S(2)}, u32[]{:S(2)}) collective-permute-start(bf16[1,4,64,256]{3,2,1,0:T(8,128)(2,1)S(1)} %get-tuple-element.34), channel_id=1, source_target_pairs={{0,1},{1,2},{2,3},{3,4},{4,5},{5,6},{6,7},{7,8},{8,9},{9,10},{10,1... | collective-permute-start | bytes 393224 | tf_op jit(solution)/shard_map/ppermute | solution.py:22
  30.7 6.0 %collective-permute-start.1 = (bf16[1,4,64,256]{3,2,1,0:T(8,128)(2,1)S(1)}, bf16[1,4,64,256]{3,2,1,0:T(8,128)(2,1)S(1)}, u32[]{:S(2)}, u32[]{:S(2)}) collective-permute-start(bf16[1,4,64,256]{3,2,1,0:T(8,128)(2,1)S(1)} %get-tuple-element.35), channel_id=1, source_target_pairs={{1,0},{2,1},{3,2},{4,3},{5,4},{6,5},{7,6},{8,7},{9,8},{10,9},{11,1... | collective-permute-start | bytes 393224 | tf_op jit(solution)/shard_map/ppermute | solution.py:25
  37.4 0.4 collective-permute-done
  37.7 1.5 %collective-permute-done.1 = bf16[1,4,64,256]{3,2,1,0:T(8,128)(2,1)S(1)} collective-permute-done((bf16[1,4,64,256]{3,2,1,0:T(8,128)(2,1)S(1)}, bf16[1,4,64,256]{3,2,1,0:T(8,128)(2,1)S(1)}, u32[]{:S(2)}, u32[]{:S(2)}) %collective-permute-start.1) | collective-permute-done | bytes 131104 | tf_op jit(solution)/shard_map/ppermute | solution.py:25
  39.2 0.9 pad_maximum_fusion.ext_ref
  40.1 8.0 %shard_map.64 = f32[256,1536]{1,0:T(8,128)} custom-call(s32[96]{0:T(128)} %bitcast.39, s32[1]{0:T(128)} %bitcast.27.cnt_ref, bf16[256,1536]{1,0:T(8,128)(2,1)} %pad_maximum_fusion.ext_ref, bf16[96,128,128]{2,1,0:T(8,128)(2,1)} %bitcast.36, bf16[4,12288]{1,0:T(4,128)(2,1)} %bitcast.37, bf16[4,12288]{1,0:T(4,128)(2,1)} %bitcast.38), custom_call_target="tpu_custom_call" | custom-call | flops 1610612736 | bytes 5701632 | tf_op jit(solution)/shard_map/pallas_call | solution.py:91
  48.2 1.1 %fusion.6 = (f32[1,4,64,256]{3,2,1,0:T(8,128)S(1)}, f32[1,4,64,256]{3,2,1,0:T(8,128)S(1)}) fusion(f32[1,4,64,1536]{3,2,1,0:T(8,128)} %bitcast.31), kind=kLoop, calls=%fused_computation.15 | loop fusion | bytes 1048576 | tf_op jit(solution)/shard_map/slice | solution.py:105
  49.2 7.6 %collective-permute-start.2 = (f32[1,4,64,256]{3,2,1,0:T(8,128)S(1)}, f32[1,4,64,256]{3,2,1,0:T(8,128)S(1)}, u32[]{:S(2)}, u32[]{:S(2)}) collective-permute-start(f32[1,4,64,256]{3,2,1,0:T(8,128)S(1)} %get-tuple-element.30), channel_id=1, source_target_pairs={{0,31},{1,0},{2,1},{3,2},{4,3},{5,4},{6,5},{7,6},{8,7},{9,8},{10,9... | collective-permute-start | bytes 786440 | tf_op jit(solution)/shard_map/ppermute | solution.py:33
  56.9 1.9 %collective-permute-start.3 = (f32[1,4,64,256]{3,2,1,0:T(8,128)S(1)}, f32[1,4,64,256]{3,2,1,0:T(8,128)S(1)}, u32[]{:S(2)}, u32[]{:S(2)}) collective-permute-start(f32[1,4,64,256]{3,2,1,0:T(8,128)S(1)} %get-tuple-element.29), channel_id=1, source_target_pairs={{0,1},{1,2},{2,3},{3,4},{4,5},{5,6},{6,7},{7,8},{8,9},{9,10},{10,1... | collective-permute-start | bytes 786440 | tf_op jit(solution)/shard_map/ppermute | solution.py:33
  58.9 1.3 %slice.83 = f32[1,4,64,1024]{3,2,1,0:T(8,128)S(1)} slice(f32[1,4,64,1536]{3,2,1,0:T(8,128)} %bitcast.32), slice={[0:1], [0:4], [0:64], [256:1280]} | slice | bytes 2097152 | tf_op jit(solution)/shard_map/slice | solution.py:106
  60.2 0.5 collective-permute-done.2
  60.8 1.0 %fusion.3 = f32[1,4,64,1024]{3,2,1,0:T(8,128)S(1)} fusion(f32[1,4,64,1024]{3,2,1,0:T(8,128)S(1)} %slice.83, f32[1,4,64,256]{3,2,1,0:T(8,128)S(1)} %collective-permute-done.2, f32[1,4,64,1536]{3,2,1,0:T(8,128)} %bitcast.33), kind=kLoop, calls=%fused_computation.8 | loop fusion | flops 65536 | bytes 786432 | tf_op jit(solution)/shard_map/scatter-add | solution.py:109
  61.8 0.1 copy.8
  61.8 6.6 %collective-permute-done.3 = f32[1,4,64,256]{3,2,1,0:T(8,128)S(1)} collective-permute-done((f32[1,4,64,256]{3,2,1,0:T(8,128)S(1)}, f32[1,4,64,256]{3,2,1,0:T(8,128)S(1)}, u32[]{:S(2)}, u32[]{:S(2)}) %collective-permute-start.3) | collective-permute-done | bytes 262176 | tf_op jit(solution)/shard_map/ppermute | solution.py:33
  68.5 0.1 dynamic-slice_bitcast_fusion.2
  68.6 4.1 %collective-permute-start.4 = (f32[64,1024]{1,0:T(8,128)S(1)}, f32[64,1024]{1,0:T(8,128)S(1)}, u32[]{:S(2)}, u32[]{:S(2)}) collective-permute-start(f32[64,1024]{1,0:T(8,128)S(1)} %get-tuple-element.31), channel_id=1, source_target_pairs={{0,256},{128,384},{256,0},{384,128},{1,257},{129,385},{257,1},{385... | collective-permute-start | bytes 786440 | tf_op jit(solution)/shard_map/ppermute | solution.py:33
  72.7 3.8 %collective-permute-start.5 = (f32[64,1024]{1,0:T(8,128)S(1)}, f32[64,1024]{1,0:T(8,128)S(1)}, u32[]{:S(2)}, u32[]{:S(2)}) collective-permute-start(f32[64,1024]{1,0:T(8,128)S(1)} %get-tuple-element.33), channel_id=1, source_target_pairs={{0,384},{128,0},{256,128},{384,256},{1,385},{129,1},{257,129},{385... | collective-permute-start | bytes 786440 | tf_op jit(solution)/shard_map/ppermute | solution.py:33
  76.5 2.9 %collective-permute-start.6 = (f32[64,1024]{1,0:T(8,128)S(1)}, f32[64,1024]{1,0:T(8,128)S(1)}, u32[]{:S(2)}, u32[]{:S(2)}) collective-permute-start(f32[64,1024]{1,0:T(8,128)S(1)} %get-tuple-element.32), channel_id=1, source_target_pairs={{0,128},{128,256},{256,384},{384,0},{1,129},{129,257},{257,385},{3... | collective-permute-start | bytes 786440 | tf_op jit(solution)/shard_map/ppermute | solution.py:33
  79.5 9.2 %collective-permute-done.4 = f32[64,1024]{1,0:T(8,128)S(1)} collective-permute-done((f32[64,1024]{1,0:T(8,128)S(1)}, f32[64,1024]{1,0:T(8,128)S(1)}, u32[]{:S(2)}, u32[]{:S(2)}) %collective-permute-start.4) | collective-permute-done | bytes 262176 | tf_op jit(solution)/shard_map/ppermute | solution.py:33
  88.6 7.2 %collective-permute-done.5 = f32[64,1024]{1,0:T(8,128)S(1)} collective-permute-done((f32[64,1024]{1,0:T(8,128)S(1)}, f32[64,1024]{1,0:T(8,128)S(1)}, u32[]{:S(2)}, u32[]{:S(2)}) %collective-permute-start.5) | collective-permute-done | bytes 262176 | tf_op jit(solution)/shard_map/ppermute | solution.py:33
  95.8 0.0 collective-permute-done.6
  95.8 0.1 fusion.5
  95.9 0.8 reshape.83
  (2 shorter events, 0.1 us)
Async XLA Ops:
  27.2 10.5 %collective-permute-start = (bf16[1,4,64,256]{3,2,1,0:T(8,128)(2,1)S(1)}, bf16[1,4,64,256]{3,2,1,0:T(8,128)(2,1)S(1)}, u32[]{:S(2)}, u32[]{:S(2)}) collective-permute-start(bf16[1,4,64,256]{3,2,1,0:T(8,128)(2,1)S(1)} %get-tuple-element.34), channel_id=1, source_target_pairs={{0,1},{1,2},{2,3},{3,4},{4,5},{5,6},{6,7},{7,8},{8,9},{9,10},{10,1... | collective-permute-start | bytes 393224 | tf_op jit(solution)/shard_map/ppermute | solution.py:22
  30.7 8.5 %collective-permute-start.1 = (bf16[1,4,64,256]{3,2,1,0:T(8,128)(2,1)S(1)}, bf16[1,4,64,256]{3,2,1,0:T(8,128)(2,1)S(1)}, u32[]{:S(2)}, u32[]{:S(2)}) collective-permute-start(bf16[1,4,64,256]{3,2,1,0:T(8,128)(2,1)S(1)} %get-tuple-element.35), channel_id=1, source_target_pairs={{1,0},{2,1},{3,2},{4,3},{5,4},{6,5},{7,6},{8,7},{9,8},{10,9},{11,1... | collective-permute-start | bytes 393224 | tf_op jit(solution)/shard_map/ppermute | solution.py:25
  49.2 11.5 %collective-permute-start.2 = (f32[1,4,64,256]{3,2,1,0:T(8,128)S(1)}, f32[1,4,64,256]{3,2,1,0:T(8,128)S(1)}, u32[]{:S(2)}, u32[]{:S(2)}) collective-permute-start(f32[1,4,64,256]{3,2,1,0:T(8,128)S(1)} %get-tuple-element.30), channel_id=1, source_target_pairs={{0,31},{1,0},{2,1},{3,2},{4,3},{5,4},{6,5},{7,6},{8,7},{9,8},{10,9... | collective-permute-start | bytes 786440 | tf_op jit(solution)/shard_map/ppermute | solution.py:33
  56.9 11.6 %collective-permute-start.3 = (f32[1,4,64,256]{3,2,1,0:T(8,128)S(1)}, f32[1,4,64,256]{3,2,1,0:T(8,128)S(1)}, u32[]{:S(2)}, u32[]{:S(2)}) collective-permute-start(f32[1,4,64,256]{3,2,1,0:T(8,128)S(1)} %get-tuple-element.29), channel_id=1, source_target_pairs={{0,1},{1,2},{2,3},{3,4},{4,5},{5,6},{6,7},{7,8},{8,9},{9,10},{10,1... | collective-permute-start | bytes 786440 | tf_op jit(solution)/shard_map/ppermute | solution.py:33
  68.6 20.0 %collective-permute-start.4 = (f32[64,1024]{1,0:T(8,128)S(1)}, f32[64,1024]{1,0:T(8,128)S(1)}, u32[]{:S(2)}, u32[]{:S(2)}) collective-permute-start(f32[64,1024]{1,0:T(8,128)S(1)} %get-tuple-element.31), channel_id=1, source_target_pairs={{0,256},{128,384},{256,0},{384,128},{1,257},{129,385},{257,1},{385... | collective-permute-start | bytes 786440 | tf_op jit(solution)/shard_map/ppermute | solution.py:33
  72.7 23.1 %collective-permute-start.5 = (f32[64,1024]{1,0:T(8,128)S(1)}, f32[64,1024]{1,0:T(8,128)S(1)}, u32[]{:S(2)}, u32[]{:S(2)}) collective-permute-start(f32[64,1024]{1,0:T(8,128)S(1)} %get-tuple-element.33), channel_id=1, source_target_pairs={{0,384},{128,0},{256,128},{384,256},{1,385},{129,1},{257,129},{385... | collective-permute-start | bytes 786440 | tf_op jit(solution)/shard_map/ppermute | solution.py:33
  76.5 19.3 %collective-permute-start.6 = (f32[64,1024]{1,0:T(8,128)S(1)}, f32[64,1024]{1,0:T(8,128)S(1)}, u32[]{:S(2)}, u32[]{:S(2)}) collective-permute-start(f32[64,1024]{1,0:T(8,128)S(1)} %get-tuple-element.32), channel_id=1, source_target_pairs={{0,128},{128,256},{256,384},{384,0},{1,129},{129,257},{257,385},{3... | collective-permute-start | bytes 786440 | tf_op jit(solution)/shard_map/ppermute | solution.py:33

commit v10 on v9

--- a/solution.py
+++ b/solution.py
@@ -129,10 +129,10 @@
         obs_counts[0],
     )
     interior = settle(adjoint_rows.reshape(1, leads, members * fields, width))[0]
-    running = lax.dynamic_index_in_dim(interior, here, axis=0, keepdims=False)
-    for shift in sorted(range(1, ring), key=lambda d: -min(d, ring - d)):
-        back = lax.dynamic_index_in_dim(interior, (here - shift) % ring, axis=0, keepdims=False)
-        running = running + passed_along(back, "tq", -shift)
+    returned = lax.all_to_all(interior, "tq", 0, 0, tiled=True)
+    running = returned[0]
+    for slot in range(1, ring):
+        running = running + returned[slot]
     return running.reshape(1, members, fields, cells)
 
 

time: 97.2 us -> 95.4 us (0.981)
  blocking collectives: 25.8 us -> 51.2 us
  waiting for transfers between devices: 25.4 us -> 9.07 us
  starting transfers between devices: 29.9 us -> 19.1 us
    all_to_all x0 -> x1, blocking collectives: none -> 25.5 us  [body(): returned = lax.all_to_all(interior, 'tq', 0, 0, tiled=True)]
    ppermute x5 -> x2, waiting for transfers between devices: 23.5 us -> 7.22 us  [passed_along(): return lax.ppermute(value, axis, pairs)]
    ppermute x5 -> x2, starting transfers between devices: 20.4 us -> 9.59 us  [passed_along(): return lax.ppermute(value, axis, pairs)]
  transfers between devices with their start and end apart: 7 -> 4, of which waited for: 6 -> 4; matrix products, arithmetic and copies ran while one was open for 2% -> 3% of each run, Pallas kernels for 0% -> 0%
where the time goes in v10:
time: 95.4 us; the launch traced here: 94.8 us
  blocking collectives  51.2 us (54%)
  starting transfers between devices  19.1 us (20%)
  waiting for transfers between devices  9.07 us (10%)
  Pallas kernels  8.02 us (8%)
  local copies, waits for them, and re-layouts  4.45 us (5%)
  other arithmetic  2.23 us (2%)
    all_to_all x1, blocking collectives, body(): incoming = lax.all_to_all(outgoing, 'tq', 0, 0, tiled=True)  25.8 us
    all_to_all x1, blocking collectives, body(): returned = lax.all_to_all(interior, 'tq', 0, 0, tiled=True)  25.5 us
    ppermute x2, starting transfers between devices, passed_along(): return lax.ppermute(value, axis, pairs)  9.59 us
    pallas_call x1, Pallas kernels, observe(): pl.pallas_call(observe_kernel, grid_spec=grid_spec, out_shape=jax.ShapeDt...  8.02 us
    ppermute x2, waiting for transfers between devices, passed_along(): return lax.ppermute(value, axis, pairs)  7.22 us
    ppermute x1, starting transfers between devices, with_halo(): lax.ppermute(lax.slice_in_dim(block, 0, width, axis=dim), axis, backward)  6.01 us
    ppermute x1, starting transfers between devices, with_halo(): lax.ppermute(lax.slice_in_dim(block, block.shape[dim] - width, None, axis...  3.48 us
  transfers between devices with their start and end apart: 4, of which 4 were waited for; matrix products, arithmetic and copies ran while one was open for 3% of the time, Pallas kernels for 0%

profile of v10, /device:TPU:64, one launch (start us, length us, event | category | flops | bytes accessed | tf_op | source)
XLA Modules:
  0.0 94.8 jit_solution(356309143903374572)
XLA Ops:
  0.0 1.2 %reshape_squeeze.4 = bf16[4,64,1024]{2,1,0:T(8,128)(2,1)S(1)} reshape(bf16[1,4,16,4,1024]{4,3,2,1,0:T(4,128)(2,1)} %param.10) | data formatting | bytes 1048576 | tf_op jit(solution)/shard_map/reshape;squeeze | solution.py:118
  1.2 0.2 fusion
  1.4 25.8 %all_to_all.10 = bf16[4,64,1024]{2,1,0:T(8,128)(2,1)S(1)} all-to-all(bf16[4,64,1024]{2,1,0:T(8,128)(2,1)S(1)} %fusion), channel_id=1, replica_groups=mesh['tq'=4,'tr'=4,'space'=32] {'tq'}, dimensions={0} | all-to-all | bytes 1048576 | tf_op jit(solution)/shard_map/all_to_all | solution.py:120
  27.2 3.5 %collective-permute-start = (bf16[1,4,64,256]{3,2,1,0:T(8,128)(2,1)S(1)}, bf16[1,4,64,256]{3,2,1,0:T(8,128)(2,1)S(1)}, u32[]{:S(2)}, u32[]{:S(2)}) collective-permute-start(bf16[1,4,64,256]{3,2,1,0:T(8,128)(2,1)S(1)} %get-tuple-element.31), channel_id=1, source_target_pairs={{0,1},{1,2},{2,3},{3,4},{4,5},{5,6},{6,7},{7,8},{8,9},{9,10},{10,1... | collective-permute-start | bytes 393224 | tf_op jit(solution)/shard_map/ppermute | solution.py:22
  30.7 6.0 %collective-permute-start.1 = (bf16[1,4,64,256]{3,2,1,0:T(8,128)(2,1)S(1)}, bf16[1,4,64,256]{3,2,1,0:T(8,128)(2,1)S(1)}, u32[]{:S(2)}, u32[]{:S(2)}) collective-permute-start(bf16[1,4,64,256]{3,2,1,0:T(8,128)(2,1)S(1)} %get-tuple-element.32), channel_id=1, source_target_pairs={{1,0},{2,1},{3,2},{4,3},{5,4},{6,5},{7,6},{8,7},{9,8},{10,9},{11,1... | collective-permute-start | bytes 393224 | tf_op jit(solution)/shard_map/ppermute | solution.py:25
  37.4 0.4 collective-permute-done
  37.7 1.5 %collective-permute-done.1 = bf16[1,4,64,256]{3,2,1,0:T(8,128)(2,1)S(1)} collective-permute-done((bf16[1,4,64,256]{3,2,1,0:T(8,128)(2,1)S(1)}, bf16[1,4,64,256]{3,2,1,0:T(8,128)(2,1)S(1)}, u32[]{:S(2)}, u32[]{:S(2)}) %collective-permute-start.1) | collective-permute-done | bytes 131104 | tf_op jit(solution)/shard_map/ppermute | solution.py:25
  39.2 0.9 pad_maximum_fusion.ext_ref
  40.2 8.0 %shard_map.64 = f32[256,1536]{1,0:T(8,128)} custom-call(s32[96]{0:T(128)} %bitcast.27, s32[1]{0:T(128)} %bitcast.15.cnt_ref, bf16[256,1536]{1,0:T(8,128)(2,1)} %pad_maximum_fusion.ext_ref, bf16[96,128,128]{2,1,0:T(8,128)(2,1)} %bitcast.24, bf16[4,12288]{1,0:T(4,128)(2,1)} %bitcast.25, bf16[4,12288]{1,0:T(4,128)(2,1)} %bitcast.26), custom_call_target="tpu_custom_call" | custom-call | flops 1610612736 | bytes 5701632 | tf_op jit(solution)/shard_map/pallas_call | solution.py:91
  48.2 1.1 %fusion.4 = (f32[1,4,64,256]{3,2,1,0:T(8,128)S(1)}, f32[1,4,64,256]{3,2,1,0:T(8,128)S(1)}) fusion(f32[1,4,64,1536]{3,2,1,0:T(8,128)} %bitcast.19), kind=kLoop, calls=%fused_computation.12 | loop fusion | bytes 1048576 | tf_op jit(solution)/shard_map/slice | solution.py:105
  49.2 7.7 %collective-permute-start.2 = (f32[1,4,64,256]{3,2,1,0:T(8,128)S(1)}, f32[1,4,64,256]{3,2,1,0:T(8,128)S(1)}, u32[]{:S(2)}, u32[]{:S(2)}) collective-permute-start(f32[1,4,64,256]{3,2,1,0:T(8,128)S(1)} %get-tuple-element.30), channel_id=1, source_target_pairs={{0,31},{1,0},{2,1},{3,2},{4,3},{5,4},{6,5},{7,6},{8,7},{9,8},{10,9... | collective-permute-start | bytes 786440 | tf_op jit(solution)/shard_map/ppermute | solution.py:33
  56.9 1.9 %collective-permute-start.3 = (f32[1,4,64,256]{3,2,1,0:T(8,128)S(1)}, f32[1,4,64,256]{3,2,1,0:T(8,128)S(1)}, u32[]{:S(2)}, u32[]{:S(2)}) collective-permute-start(f32[1,4,64,256]{3,2,1,0:T(8,128)S(1)} %get-tuple-element.29), channel_id=1, source_target_pairs={{0,1},{1,2},{2,3},{3,4},{4,5},{5,6},{6,7},{7,8},{8,9},{9,10},{10,1... | collective-permute-start | bytes 786440 | tf_op jit(solution)/shard_map/ppermute | solution.py:33
  58.8 1.3 %slice.99 = f32[1,4,64,1024]{3,2,1,0:T(8,128)S(1)} slice(f32[1,4,64,1536]{3,2,1,0:T(8,128)} %bitcast.20), slice={[0:1], [0:4], [0:64], [256:1280]} | slice | bytes 2097152 | tf_op jit(solution)/shard_map/slice | solution.py:106
  60.2 0.6 collective-permute-done.2
  60.8 1.0 %fusion.3 = f32[1,4,64,1024]{3,2,1,0:T(8,128)S(1)} fusion(f32[1,4,64,1024]{3,2,1,0:T(8,128)S(1)} %slice.99, f32[1,4,64,256]{3,2,1,0:T(8,128)S(1)} %collective-permute-done.2, f32[1,4,64,1536]{3,2,1,0:T(8,128)} %bitcast.21), kind=kLoop, calls=%fused_computation.11 | loop fusion | flops 65536 | bytes 786432 | tf_op jit(solution)/shard_map/scatter-add | solution.py:109
  61.8 0.1 copy.8
  61.9 6.6 %collective-permute-done.3 = f32[1,4,64,256]{3,2,1,0:T(8,128)S(1)} collective-permute-done((f32[1,4,64,256]{3,2,1,0:T(8,128)S(1)}, f32[1,4,64,256]{3,2,1,0:T(8,128)S(1)}, u32[]{:S(2)}, u32[]{:S(2)}) %collective-permute-start.3) | collective-permute-done | bytes 262176 | tf_op jit(solution)/shard_map/ppermute | solution.py:33
  68.6 25.5 %all_to_all.11 = f32[4,64,1024]{2,1,0:T(8,128)S(1)} all-to-all(f32[4,64,1024]{2,1,0:T(8,128)S(1)} %fusion.2), channel_id=1, replica_groups=mesh['tq'=4,'tr'=4,'space'=32] {'tq'}, dimensions={0} | all-to-all | bytes 2097152 | tf_op jit(solution)/shard_map/all_to_all | solution.py:132
  94.0 0.1 slice_add_fusion
  94.1 0.8 add.66
  (2 shorter events, 0.1 us)
Async XLA Ops:
  27.2 10.5 %collective-permute-start = (bf16[1,4,64,256]{3,2,1,0:T(8,128)(2,1)S(1)}, bf16[1,4,64,256]{3,2,1,0:T(8,128)(2,1)S(1)}, u32[]{:S(2)}, u32[]{:S(2)}) collective-permute-start(bf16[1,4,64,256]{3,2,1,0:T(8,128)(2,1)S(1)} %get-tuple-element.31), channel_id=1, source_target_pairs={{0,1},{1,2},{2,3},{3,4},{4,5},{5,6},{6,7},{7,8},{8,9},{9,10},{10,1... | collective-permute-start | bytes 393224 | tf_op jit(solution)/shard_map/ppermute | solution.py:22
  30.7 8.5 %collective-permute-start.1 = (bf16[1,4,64,256]{3,2,1,0:T(8,128)(2,1)S(1)}, bf16[1,4,64,256]{3,2,1,0:T(8,128)(2,1)S(1)}, u32[]{:S(2)}, u32[]{:S(2)}) collective-permute-start(bf16[1,4,64,256]{3,2,1,0:T(8,128)(2,1)S(1)} %get-tuple-element.32), channel_id=1, source_target_pairs={{1,0},{2,1},{3,2},{4,3},{5,4},{6,5},{7,6},{8,7},{9,8},{10,9},{11,1... | collective-permute-start | bytes 393224 | tf_op jit(solution)/shard_map/ppermute | solution.py:25
  49.2 11.5 %collective-permute-start.2 = (f32[1,4,64,256]{3,2,1,0:T(8,128)S(1)}, f32[1,4,64,256]{3,2,1,0:T(8,128)S(1)}, u32[]{:S(2)}, u32[]{:S(2)}) collective-permute-start(f32[1,4,64,256]{3,2,1,0:T(8,128)S(1)} %get-tuple-element.30), channel_id=1, source_target_pairs={{0,31},{1,0},{2,1},{3,2},{4,3},{5,4},{6,5},{7,6},{8,7},{9,8},{10,9... | collective-permute-start | bytes 786440 | tf_op jit(solution)/shard_map/ppermute | solution.py:33
  56.9 11.6 %collective-permute-start.3 = (f32[1,4,64,256]{3,2,1,0:T(8,128)S(1)}, f32[1,4,64,256]{3,2,1,0:T(8,128)S(1)}, u32[]{:S(2)}, u32[]{:S(2)}) collective-permute-start(f32[1,4,64,256]{3,2,1,0:T(8,128)S(1)} %get-tuple-element.29), channel_id=1, source_target_pairs={{0,1},{1,2},{2,3},{3,4},{4,5},{5,6},{6,7},{7,8},{8,9},{9,10},{10,1... | collective-permute-start | bytes 786440 | tf_op jit(solution)/shard_map/ppermute | solution.py:33

commit v11 on v10

--- a/solution.py
+++ b/solution.py
@@ -10,7 +10,7 @@
 
 GROUP_SITE_SPAN = 128
 EDGE = 2
-BLOCKS_PER_STEP = 32
+BLOCKS_PER_STEP = 96
 
 
 def with_halo(block, sides, width):
@@ -27,6 +27,10 @@
     return block
 
 
+def ring_pairs(count, steps):
+    return [(source, (source + steps) % count) for source in range(count)]
+
+
 def passed_along(value, axis, steps):
     count = lax.axis_size(axis)
     pairs = [(source, (source + steps) % count) for source in range(count)]
@@ -37,21 +41,28 @@
     return with_halo(grouped, (("space", grouped.ndim - 1),), EDGE * GROUP_SITE_SPAN)
 
 
-def observe_kernel(idx_ref, cnt_ref, ext_ref, op_ref, val_ref, wt_ref, out_ref):
+def observe_kernel(idx_ref, cnt_ref, low_ref, mid_ref, high_ref, op_ref, val_ref, wt_ref, out_ref, ext_ref):
     step = pl.program_id(0)
     width = GROUP_SITE_SPAN
     fields = val_ref.shape[0]
     rows = ext_ref.shape[0]
+    rim = low_ref.shape[1]
+    tile = mid_ref.shape[1]
+    blocks = op_ref.shape[0]
     period = 8
 
     @pl.when(step == 0)
     def _():
+        ext_ref[:, :rim] = low_ref[...]
+        ext_ref[:, rim:rim + tile] = mid_ref[...]
+        ext_ref[:, rim + tile:] = high_ref[...]
         out_ref[...] = jnp.zeros_like(out_ref)
 
     count = cnt_ref[0]
     lane = lax.broadcasted_iota(jnp.int32, (1, width), 1)
-    for k in range(BLOCKS_PER_STEP):
-        b = step * BLOCKS_PER_STEP + k
+
+    def forward(k):
+        b = step * blocks + k
         start = pl.multiple_of(idx_ref[b] * width, width)
         x = ext_ref[:, pl.ds(start, width)]
         op = op_ref[k]
@@ -64,30 +75,45 @@
         scaling = jnp.where(live, wt_ref[:, k * width:(k + 1) * width].astype(jnp.float32), 0.0)
         scaling = jnp.concatenate([scaling] * (period // fields), axis=0)[None]
         misfit = ((images - observed) * scaling).reshape(rows, width).astype(jnp.bfloat16)
-        adjoint = jnp.dot(misfit, op, preferred_element_type=jnp.float32)
-        out_ref[:, pl.ds(start, width)] += adjoint
+        return start, misfit, op
+
+    def backward(start, misfit, op):
+        out_ref[:, pl.ds(start, width)] += jnp.dot(misfit, op, preferred_element_type=jnp.float32)
+
+    pending = forward(0)
+    for k in range(1, blocks):
+        ahead = forward(k)
+        backward(*pending)
+        pending = ahead
+    backward(*pending)
 
 
-def observe(ext_rows, operator, indices, values, weights, counts):
-    rows, cells = ext_rows.shape
+def observe(low, mid, high, operator, indices, values, weights, counts):
+    rows, tile = mid.shape
+    rim = low.shape[1]
+    cells = tile + 2 * rim
     obs_blocks = operator.shape[0]
     width = GROUP_SITE_SPAN
     fields = values.shape[0]
     steps = obs_blocks // BLOCKS_PER_STEP
     span = BLOCKS_PER_STEP * width
+    whole = lambda g, i, c: (0, 0)
     grid_spec = pltpu.PrefetchScalarGridSpec(
         num_scalar_prefetch=2,
         grid=(steps,),
         in_specs=[
-            pl.BlockSpec((rows, cells), lambda g, i, c: (0, 0)),
+            pl.BlockSpec((rows, rim), whole),
+            pl.BlockSpec((rows, tile), whole),
+            pl.BlockSpec((rows, rim), whole),
             pl.BlockSpec((BLOCKS_PER_STEP, width, width), lambda g, i, c: (g, 0, 0)),
             pl.BlockSpec((fields, span), lambda g, i, c: (0, g)),
             pl.BlockSpec((fields, span), lambda g, i, c: (0, g)),
         ],
-        out_specs=pl.BlockSpec((rows, cells), lambda g, i, c: (0, 0)),
+        out_specs=pl.BlockSpec((rows, cells), whole),
+        scratch_shapes=[pltpu.VMEM((rows, cells), mid.dtype)],
     )
     flops = 4 * obs_blocks * rows * width * width
-    bytes_accessed = operator.size * 2 + ext_rows.size * 2 + rows * cells * 4 + values.size * 4
+    bytes_accessed = operator.size * 2 + rows * cells * 6 + values.size * 4
     return pl.pallas_call(
         observe_kernel,
         grid_spec=grid_spec,
@@ -96,7 +122,7 @@
         cost_estimate=pl.CostEstimate(
             flops=flops, bytes_accessed=bytes_accessed, transcendentals=0
         ),
-    )(indices, counts, ext_rows, operator, values, weights)
+    )(indices, counts, low, mid, high, operator, values, weights)
 
 
 def settle(adjoint_ext):
@@ -118,10 +144,15 @@
     own = own.reshape(leads, members * fields, cells)
     outgoing = jnp.roll(own, here, axis=0)
     incoming = lax.all_to_all(outgoing, "tq", 0, 0, tiled=True)
-    extended = extend(incoming[None])[0]
-    width = extended.shape[-1]
+    rim = EDGE * GROUP_SITE_SPAN
+    space = lax.axis_size("space")
+    low = lax.ppermute(incoming[..., cells - rim:], "space", ring_pairs(space, 1))
+    high = lax.ppermute(incoming[..., :rim], "space", ring_pairs(space, -1))
+    width = cells + 2 * rim
     adjoint_rows = observe(
-        extended.reshape(leads * members * fields, width),
+        low.reshape(leads * members * fields, rim),
+        incoming.reshape(leads * members * fields, cells),
+        high.reshape(leads * members * fields, rim),
         op_blocks[0],
         block_index[0],
         obs_values[0],

time: 95.4 us -> 94.8 us (level)
  starting transfers between devices: 19.1 us -> 15.3 us
  waiting for transfers between devices: 9.07 us -> 12.8 us
    ppermute x2, waiting for transfers between devices: 1.85 us -> 7.59 us  [the longest x1 7.59 us: body(): lax.ppermute(incoming[..., cells - rim:], 'space', ring_pairs(space, 1))]
    ppermute x2, starting transfers between devices: 9.59 us -> 5.84 us  [passed_along(): return lax.ppermute(value, axis, pairs)]
    ppermute x2, waiting for transfers between devices: 7.22 us -> 5.22 us  [passed_along(): return lax.ppermute(value, axis, pairs)]
  transfers between devices with their start and end apart: 4 -> 4, of which waited for: 4 -> 3; matrix products, arithmetic and copies ran while one was open for 3% -> 3% of each run, Pallas kernels for 0% -> 0%
where the time goes in v11:
time: 94.8 us; the launch traced here: 94.2 us
  blocking collectives  51.2 us (54%)
  starting transfers between devices  15.3 us (16%)
  waiting for transfers between devices  12.8 us (14%)
  Pallas kernels  7.71 us (8%)
  local copies, waits for them, and re-layouts  5.1 us (5%)
  other arithmetic  1.28 us (1%)
    all_to_all x1, blocking collectives, body(): incoming = lax.all_to_all(outgoing, 'tq', 0, 0, tiled=True)  25.8 us
    all_to_all x1, blocking collectives, body(): returned = lax.all_to_all(interior, 'tq', 0, 0, tiled=True)  25.5 us
    pallas_call x1, Pallas kernels, observe(): pl.pallas_call(observe_kernel, grid_spec=grid_spec, out_shape=jax.ShapeDt...  7.71 us
    ppermute x1, waiting for transfers between devices, body(): lax.ppermute(incoming[..., cells - rim:], 'space', ring_pairs(space, 1))  7.59 us
    ppermute x1, starting transfers between devices, body(): high = lax.ppermute(incoming[..., :rim], 'space', ring_pairs(space, -1))  7.57 us
    ppermute x2, starting transfers between devices, passed_along(): return lax.ppermute(value, axis, pairs)  5.84 us
    ppermute x2, waiting for transfers between devices, passed_along(): return lax.ppermute(value, axis, pairs)  5.22 us
    ppermute x1, starting transfers between devices, body(): lax.ppermute(incoming[..., cells - rim:], 'space', ring_pairs(space, 1))  1.92 us
  transfers between devices with their start and end apart: 4, of which 3 were waited for; matrix products, arithmetic and copies ran while one was open for 3% of the time, Pallas kernels for 0%

profile of v11, /device:TPU:64, one launch (start us, length us, event | category | flops | bytes accessed | tf_op | source)
XLA Modules:
  0.0 94.2 jit_solution(8571721466199030533)
XLA Ops:
  0.0 1.2 %reshape_squeeze.3 = bf16[4,64,1024]{2,1,0:T(8,128)(2,1)S(1)} reshape(bf16[1,4,16,4,1024]{4,3,2,1,0:T(4,128)(2,1)} %param.10) | data formatting | bytes 1048576 | tf_op jit(solution)/shard_map/reshape;squeeze | solution.py:144
  1.2 0.2 fusion
  1.4 25.8 %all_to_all.10 = bf16[4,64,1024]{2,1,0:T(8,128)(2,1)S(1)} all-to-all(bf16[4,64,1024]{2,1,0:T(8,128)(2,1)S(1)} %fusion), channel_id=1, replica_groups=mesh['tq'=4,'tr'=4,'space'=32] {'tq'}, dimensions={0} | all-to-all | bytes 1048576 | tf_op jit(solution)/shard_map/all_to_all | solution.py:146
  27.2 0.0 copy-start
  27.2 7.6 %collective-permute-start.1 = (bf16[4,64,256]{2,1,0:T(8,128)(2,1)S(1)}, bf16[4,64,256]{2,1,0:T(8,128)(2,1)S(1)}, u32[]{:S(2)}, u32[]{:S(2)}) collective-permute-start(bf16[4,64,256]{2,1,0:T(8,128)(2,1)S(1)} %get-tuple-element.31), channel_id=1, source_target_pairs={{0,31},{1,0},{2,1},{3,2},{4,3},{5,4},{6,5},{7,6},{8,7},{9,8},{10,9... | collective-permute-start | bytes 393224 | tf_op jit(solution)/shard_map/ppermute | solution.py:150
  34.8 1.9 %collective-permute-start = (bf16[4,64,256]{2,1,0:T(8,128)(2,1)S(1)}, bf16[4,64,256]{2,1,0:T(8,128)(2,1)S(1)}, u32[]{:S(2)}, u32[]{:S(2)}) collective-permute-start(bf16[4,64,256]{2,1,0:T(8,128)(2,1)S(1)} %get-tuple-element.32), channel_id=1, source_target_pairs={{0,1},{1,2},{2,3},{3,4},{4,5},{5,6},{6,7},{7,8},{8,9},{9,10},{10,1... | collective-permute-start | bytes 393224 | tf_op jit(solution)/shard_map/ppermute | solution.py:149
  37.4 0.0 collective-permute-done.1
  37.4 0.0 copy-start.1
  37.4 7.6 %collective-permute-done = bf16[4,64,256]{2,1,0:T(8,128)(2,1)S(1)} collective-permute-done((bf16[4,64,256]{2,1,0:T(8,128)(2,1)S(1)}, bf16[4,64,256]{2,1,0:T(8,128)(2,1)S(1)}, u32[]{:S(2)}, u32[]{:S(2)}) %collective-permute-start) | collective-permute-done | bytes 131104 | tf_op jit(solution)/shard_map/ppermute | solution.py:149
  45.0 0.0 copy-start.2
  45.0 0.0 copy-done
  45.0 0.0 copy-done.1
  45.0 0.6 copy-done.2
  45.6 7.7 %shard_map.64 = f32[256,1536]{1,0:T(8,128)} custom-call(s32[96]{0:T(128)} %bitcast.25, s32[1]{0:T(128)} %bitcast.14.cnt_ref, bf16[256,256]{1,0:T(8,128)(2,1)} %bitcast.22, bf16[256,1024]{1,0:T(8,128)(2,1)} %bitcast.19, bf16[256,256]{1,0:T(8,128)(2,1)} %bitcast.21, bf16[96,128,128]{2,1,0:T(8,128)(2,1)} %bitcast.20, bf16[4,12288]{1,0:T(4,128)(2,1)} %bitcast.23, ...), custom_call_target="tpu_custom_call" | custom-call | flops 1610612736 | bytes 5701632 | tf_op jit(solution)/shard_map/pallas_call | solution.py:117
  53.3 1.1 %fusion.4 = (f32[1,4,64,256]{3,2,1,0:T(8,128)S(1)}, f32[1,4,64,256]{3,2,1,0:T(8,128)S(1)}) fusion(f32[1,4,64,1536]{3,2,1,0:T(8,128)} %bitcast.16), kind=kLoop, calls=%fused_computation.11 | loop fusion | bytes 1048576 | tf_op jit(solution)/shard_map/slice | solution.py:131
  54.4 1.9 %collective-permute-start.2 = (f32[1,4,64,256]{3,2,1,0:T(8,128)S(1)}, f32[1,4,64,256]{3,2,1,0:T(8,128)S(1)}, u32[]{:S(2)}, u32[]{:S(2)}) collective-permute-start(f32[1,4,64,256]{3,2,1,0:T(8,128)S(1)} %get-tuple-element.30), channel_id=1, source_target_pairs={{0,31},{1,0},{2,1},{3,2},{4,3},{5,4},{6,5},{7,6},{8,7},{9,8},{10,9... | collective-permute-start | bytes 786440 | tf_op jit(solution)/shard_map/ppermute | solution.py:37
  56.3 3.9 %collective-permute-start.3 = (f32[1,4,64,256]{3,2,1,0:T(8,128)S(1)}, f32[1,4,64,256]{3,2,1,0:T(8,128)S(1)}, u32[]{:S(2)}, u32[]{:S(2)}) collective-permute-start(f32[1,4,64,256]{3,2,1,0:T(8,128)S(1)} %get-tuple-element.29), channel_id=1, source_target_pairs={{0,1},{1,2},{2,3},{3,4},{4,5},{5,6},{6,7},{7,8},{8,9},{9,10},{10,1... | collective-permute-start | bytes 786440 | tf_op jit(solution)/shard_map/ppermute | solution.py:37
  60.3 1.3 %slice.99 = f32[1,4,64,1024]{3,2,1,0:T(8,128)S(1)} slice(f32[1,4,64,1536]{3,2,1,0:T(8,128)} %bitcast.17), slice={[0:1], [0:4], [0:64], [256:1280]} | slice | bytes 2097152 | tf_op jit(solution)/shard_map/slice | solution.py:132
  61.6 1.1 %collective-permute-done.2 = f32[1,4,64,256]{3,2,1,0:T(8,128)S(1)} collective-permute-done((f32[1,4,64,256]{3,2,1,0:T(8,128)S(1)}, f32[1,4,64,256]{3,2,1,0:T(8,128)S(1)}, u32[]{:S(2)}, u32[]{:S(2)}) %collective-permute-start.2) | collective-permute-done | bytes 262176 | tf_op jit(solution)/shard_map/ppermute | solution.py:37
  62.7 1.0 %fusion.3 = f32[1,4,64,1024]{3,2,1,0:T(8,128)S(1)} fusion(f32[1,4,64,1024]{3,2,1,0:T(8,128)S(1)} %slice.99, f32[1,4,64,256]{3,2,1,0:T(8,128)S(1)} %collective-permute-done.2, f32[1,4,64,1536]{3,2,1,0:T(8,128)} %bitcast.18), kind=kLoop, calls=%fused_computation.10 | loop fusion | flops 65536 | bytes 786432 | tf_op jit(solution)/shard_map/scatter-add | solution.py:135
  63.7 0.1 copy.8
  63.8 4.1 %collective-permute-done.3 = f32[1,4,64,256]{3,2,1,0:T(8,128)S(1)} collective-permute-done((f32[1,4,64,256]{3,2,1,0:T(8,128)S(1)}, f32[1,4,64,256]{3,2,1,0:T(8,128)S(1)}, u32[]{:S(2)}, u32[]{:S(2)}) %collective-permute-start.3) | collective-permute-done | bytes 262176 | tf_op jit(solution)/shard_map/ppermute | solution.py:37
  68.0 25.5 %all_to_all.11 = f32[4,64,1024]{2,1,0:T(8,128)S(1)} all-to-all(f32[4,64,1024]{2,1,0:T(8,128)S(1)} %fusion.2), channel_id=1, replica_groups=mesh['tq'=4,'tr'=4,'space'=32] {'tq'}, dimensions={0} | all-to-all | bytes 2097152 | tf_op jit(solution)/shard_map/all_to_all | solution.py:163
  93.4 0.1 slice_add_fusion
  93.5 0.8 add.66
  (2 shorter events, 0.1 us)
Async XLA Ops:
  27.2 17.8 %copy-start = (bf16[4,64,1024]{2,1,0:T(8,128)(2,1)}, bf16[4,64,1024]{2,1,0:T(8,128)(2,1)S(1)}, u32[]{:S(2)}) copy-start(bf16[4,64,1024]{2,1,0:T(8,128)(2,1)S(1)} %all_to_all.10) | copy-start | bytes 1572868
  27.2 10.2 %collective-permute-start.1 = (bf16[4,64,256]{2,1,0:T(8,128)(2,1)S(1)}, bf16[4,64,256]{2,1,0:T(8,128)(2,1)S(1)}, u32[]{:S(2)}, u32[]{:S(2)}) collective-permute-start(bf16[4,64,256]{2,1,0:T(8,128)(2,1)S(1)} %get-tuple-element.31), channel_id=1, source_target_pairs={{0,31},{1,0},{2,1},{3,2},{4,3},{5,4},{6,5},{7,6},{8,7},{9,8},{10,9... | collective-permute-start | bytes 393224 | tf_op jit(solution)/shard_map/ppermute | solution.py:150
  34.8 10.2 %collective-permute-start = (bf16[4,64,256]{2,1,0:T(8,128)(2,1)S(1)}, bf16[4,64,256]{2,1,0:T(8,128)(2,1)S(1)}, u32[]{:S(2)}, u32[]{:S(2)}) collective-permute-start(bf16[4,64,256]{2,1,0:T(8,128)(2,1)S(1)} %get-tuple-element.32), channel_id=1, source_target_pairs={{0,1},{1,2},{2,3},{3,4},{4,5},{5,6},{6,7},{7,8},{8,9},{9,10},{10,1... | collective-permute-start | bytes 393224 | tf_op jit(solution)/shard_map/ppermute | solution.py:149
  37.4 7.6 %copy-start.1 = (bf16[4,64,256]{2,1,0:T(8,128)(2,1)}, bf16[4,64,256]{2,1,0:T(8,128)(2,1)S(1)}, u32[]{:S(2)}) copy-start(bf16[4,64,256]{2,1,0:T(8,128)(2,1)S(1)} %collective-permute-done.1) | copy-start | bytes 393220
  45.0 0.7 copy-start.2
  54.4 8.3 %collective-permute-start.2 = (f32[1,4,64,256]{3,2,1,0:T(8,128)S(1)}, f32[1,4,64,256]{3,2,1,0:T(8,128)S(1)}, u32[]{:S(2)}, u32[]{:S(2)}) collective-permute-start(f32[1,4,64,256]{3,2,1,0:T(8,128)S(1)} %get-tuple-element.30), channel_id=1, source_target_pairs={{0,31},{1,0},{2,1},{3,2},{4,3},{5,4},{6,5},{7,6},{8,7},{9,8},{10,9... | collective-permute-start | bytes 786440 | tf_op jit(solution)/shard_map/ppermute | solution.py:37
  56.3 11.6 %collective-permute-start.3 = (f32[1,4,64,256]{3,2,1,0:T(8,128)S(1)}, f32[1,4,64,256]{3,2,1,0:T(8,128)S(1)}, u32[]{:S(2)}, u32[]{:S(2)}) collective-permute-start(f32[1,4,64,256]{3,2,1,0:T(8,128)S(1)} %get-tuple-element.29), channel_id=1, source_target_pairs={{0,1},{1,2},{2,3},{3,4},{4,5},{5,6},{6,7},{7,8},{8,9},{9,10},{10,1... | collective-permute-start | bytes 786440 | tf_op jit(solution)/shard_map/ppermute | solution.py:37

commit v12 on v11

--- a/solution.py
+++ b/solution.py
@@ -41,7 +41,10 @@
     return with_halo(grouped, (("space", grouped.ndim - 1),), EDGE * GROUP_SITE_SPAN)
 
 
-def observe_kernel(idx_ref, cnt_ref, low_ref, mid_ref, high_ref, op_ref, val_ref, wt_ref, out_ref, ext_ref):
+def observe_kernel(
+    idx_ref, cnt_ref, low_ref, mid_ref, high_ref, op_ref, val_ref, wt_ref,
+    low_out, mid_out, high_out, ext_ref, out_ref,
+):
     step = pl.program_id(0)
     width = GROUP_SITE_SPAN
     fields = val_ref.shape[0]
@@ -87,6 +90,12 @@
         pending = ahead
     backward(*pending)
 
+    @pl.when(step == pl.num_programs(0) - 1)
+    def _():
+        low_out[...] = out_ref[:, :rim]
+        mid_out[...] = out_ref[:, rim:rim + tile]
+        high_out[...] = out_ref[:, rim + tile:]
+
 
 def observe(low, mid, high, operator, indices, values, weights, counts):
     rows, tile = mid.shape
@@ -109,20 +118,60 @@
             pl.BlockSpec((fields, span), lambda g, i, c: (0, g)),
             pl.BlockSpec((fields, span), lambda g, i, c: (0, g)),
         ],
-        out_specs=pl.BlockSpec((rows, cells), whole),
-        scratch_shapes=[pltpu.VMEM((rows, cells), mid.dtype)],
+        out_specs=[
+            pl.BlockSpec((rows, rim), whole),
+            pl.BlockSpec((rows, tile), whole),
+            pl.BlockSpec((rows, rim), whole),
+        ],
+        scratch_shapes=[
+            pltpu.VMEM((rows, cells), mid.dtype),
+            pltpu.VMEM((rows, cells), jnp.float32),
+        ],
     )
     flops = 4 * obs_blocks * rows * width * width
     bytes_accessed = operator.size * 2 + rows * cells * 6 + values.size * 4
     return pl.pallas_call(
         observe_kernel,
         grid_spec=grid_spec,
-        out_shape=jax.ShapeDtypeStruct((rows, cells), jnp.float32),
+        out_shape=[
+            jax.ShapeDtypeStruct((rows, rim), jnp.float32),
+            jax.ShapeDtypeStruct((rows, tile), jnp.float32),
+            jax.ShapeDtypeStruct((rows, rim), jnp.float32),
+        ],
         compiler_params=pltpu.CompilerParams(dimension_semantics=("arbitrary",)),
         cost_estimate=pl.CostEstimate(
             flops=flops, bytes_accessed=bytes_accessed, transcendentals=0
         ),
     )(indices, counts, low, mid, high, operator, values, weights)
+
+
+def rim_kernel(below_ref, above_ref, edge_ref, out_ref):
+    side = pl.program_id(0)
+
+    @pl.when(side == 0)
+    def _():
+        out_ref[...] = edge_ref[...] + below_ref[...]
+
+    @pl.when(side == 1)
+    def _():
+        out_ref[...] = edge_ref[...] + above_ref[...]
+
+
+def add_rims(interior, from_below, from_above):
+    rows, tile = interior.shape
+    rim = from_below.shape[1]
+    last = tile // rim - 1
+    edge = pl.BlockSpec((rows, rim), lambda side: (0, side * last))
+    whole = pl.BlockSpec((rows, rim), lambda side: (0, 0))
+    return pl.pallas_call(
+        rim_kernel,
+        grid=(2,),
+        in_specs=[whole, whole, edge],
+        out_specs=edge,
+        out_shape=jax.ShapeDtypeStruct(interior.shape, interior.dtype),
+        input_output_aliases={2: 0},
+        compiler_params=pltpu.CompilerParams(dimension_semantics=("arbitrary",)),
+    )(from_below, from_above, interior)
 
 
 def settle(adjoint_ext):
@@ -148,18 +197,20 @@
     space = lax.axis_size("space")
     low = lax.ppermute(incoming[..., cells - rim:], "space", ring_pairs(space, 1))
     high = lax.ppermute(incoming[..., :rim], "space", ring_pairs(space, -1))
-    width = cells + 2 * rim
-    adjoint_rows = observe(
-        low.reshape(leads * members * fields, rim),
-        incoming.reshape(leads * members * fields, cells),
-        high.reshape(leads * members * fields, rim),
+    rows = leads * members * fields
+    low_adj, interior, high_adj = observe(
+        low.reshape(rows, rim),
+        incoming.reshape(rows, cells),
+        high.reshape(rows, rim),
         op_blocks[0],
         block_index[0],
         obs_values[0],
         obs_weights[0],
         obs_counts[0],
     )
-    interior = settle(adjoint_rows.reshape(1, leads, members * fields, width))[0]
+    from_above = lax.ppermute(low_adj, "space", ring_pairs(space, -1))
+    from_below = lax.ppermute(high_adj, "space", ring_pairs(space, 1))
+    interior = add_rims(interior, from_below, from_above).reshape(leads, members * fields, cells)
     returned = lax.all_to_all(interior, "tq", 0, 0, tiled=True)
     running = returned[0]
     for slot in range(1, ring):

time: 94.8 us -> 98 us (1.034)
  the two profiles are of different devices: /device:TPU:64 before, /device:TPU:62 now
where the time goes in v12:
time: 98 us; the launch traced here: 97.6 us
  blocking collectives  53.1 us (54%)
  starting transfers between devices  18.7 us (19%)
  waiting for transfers between devices  11.7 us (12%)
  Pallas kernels  9.77 us (10%)
  local copies, waits for them, and re-layouts  3.3 us (3%)
    all_to_all x1, blocking collectives, body(): incoming = lax.all_to_all(outgoing, 'tq', 0, 0, tiled=True)  27.1 us
    all_to_all x1, blocking collectives, body(): returned = lax.all_to_all(interior, 'tq', 0, 0, tiled=True)  26 us
    pallas_call x1, Pallas kernels, observe(): pl.pallas_call(observe_kernel, grid_spec=grid_spec, out_shape=[jax.ShapeD...  7.76 us
    ppermute x1, starting transfers between devices, body(): from_below = lax.ppermute(high_adj, 'space', ring_pairs(space, 1))  7.66 us
    ppermute x1, waiting for transfers between devices, body(): from_above = lax.ppermute(low_adj, 'space', ring_pairs(space, -1))  7.61 us
    ppermute x1, starting transfers between devices, body(): lax.ppermute(incoming[..., cells - rim:], 'space', ring_pairs(space, 1))  5.91 us
    ppermute x1, starting transfers between devices, body(): high = lax.ppermute(incoming[..., :rim], 'space', ring_pairs(space, -1))  3.26 us
    ppermute x1, waiting for transfers between devices, body(): from_below = lax.ppermute(high_adj, 'space', ring_pairs(space, 1))  2.26 us
  transfers between devices with their start and end apart: 4, of which 4 were waited for; matrix products, arithmetic and copies ran while one was open for 0% of the time, Pallas kernels for 0%

profile of v12, /device:TPU:62, one launch (start us, length us, event | category | flops | bytes accessed | tf_op | source)
XLA Modules:
  0.0 97.6 jit_solution(4389735265191360659)
XLA Ops:
  0.0 1.2 %reshape_squeeze.3 = bf16[4,64,1024]{2,1,0:T(8,128)(2,1)S(1)} reshape(bf16[1,4,16,4,1024]{4,3,2,1,0:T(4,128)(2,1)} %param.6) | data formatting | bytes 1048576 | tf_op jit(solution)/shard_map/reshape;squeeze | solution.py:193
  1.2 0.2 fusion
  1.4 27.1 %all_to_all.10 = bf16[4,64,1024]{2,1,0:T(8,128)(2,1)S(1)} all-to-all(bf16[4,64,1024]{2,1,0:T(8,128)(2,1)S(1)} %fusion), channel_id=1, replica_groups=mesh['tq'=4,'tr'=4,'space'=32] {'tq'}, dimensions={0} | all-to-all | bytes 1048576 | tf_op jit(solution)/shard_map/all_to_all | solution.py:195
  28.5 0.0 copy-start
  28.5 3.3 %collective-permute-start.1 = (bf16[4,64,256]{2,1,0:T(8,128)(2,1)S(1)}, bf16[4,64,256]{2,1,0:T(8,128)(2,1)S(1)}, u32[]{:S(2)}, u32[]{:S(2)}) collective-permute-start(bf16[4,64,256]{2,1,0:T(8,128)(2,1)S(1)} %get-tuple-element.11), channel_id=1, source_target_pairs={{0,31},{1,0},{2,1},{3,2},{4,3},{5,4},{6,5},{7,6},{8,7},{9,8},{10,9... | collective-permute-start | bytes 393224 | tf_op jit(solution)/shard_map/ppermute | solution.py:199
  31.8 5.9 %collective-permute-start = (bf16[4,64,256]{2,1,0:T(8,128)(2,1)S(1)}, bf16[4,64,256]{2,1,0:T(8,128)(2,1)S(1)}, u32[]{:S(2)}, u32[]{:S(2)}) collective-permute-start(bf16[4,64,256]{2,1,0:T(8,128)(2,1)S(1)} %get-tuple-element.12), channel_id=1, source_target_pairs={{0,1},{1,2},{2,3},{3,4},{4,5},{5,6},{6,7},{7,8},{8,9},{9,10},{10,1... | collective-permute-start | bytes 393224 | tf_op jit(solution)/shard_map/ppermute | solution.py:198
  38.3 0.4 collective-permute-done.1
  38.7 0.0 copy-start.3
  38.7 1.5 %collective-permute-done = bf16[4,64,256]{2,1,0:T(8,128)(2,1)S(1)} collective-permute-done((bf16[4,64,256]{2,1,0:T(8,128)(2,1)S(1)}, bf16[4,64,256]{2,1,0:T(8,128)(2,1)S(1)}, u32[]{:S(2)}, u32[]{:S(2)}) %collective-permute-start) | collective-permute-done | bytes 131104 | tf_op jit(solution)/shard_map/ppermute | solution.py:198
  40.2 0.0 copy-start.4
  40.2 0.0 copy-done
  40.2 0.0 copy-done.3
  40.2 0.6 copy-done.4
  40.8 7.8 %shard_map.64 = (f32[256,256]{1,0:T(8,128)}, f32[256,1024]{1,0:T(8,128)}, f32[256,256]{1,0:T(8,128)}) custom-call(s32[96]{0:T(128)} %bitcast.17, s32[1]{0:T(128)} %bitcast.9.cnt_ref, bf16[256,256]{1,0:T(8,128)(2,1)} %bitcast.14, bf16[256,1024]{1,0:T(8,128)(2,1)} %bitcast.11, bf16[256,256]{1,0:T(8,128)(2,1)} %bitcast.13, bf16[96,128,128]{2,1,0:T(8,128)(2,1)} %bitcast.12, ...), custom_call_target="tpu_custom_call" | custom-call | flops 1610612736 | bytes 5701632 | tf_op jit(solution)/shard_map/pallas_call | solution.py:133
  48.6 7.7 %collective-permute-start.2 = (f32[256,256]{1,0:T(8,128)}, f32[256,256]{1,0:T(8,128)S(1)}, u32[]{:S(2)}, u32[]{:S(2)}) collective-permute-start(f32[256,256]{1,0:T(8,128)} %get-tuple-element.8), channel_id=1, source_target_pairs={{0,1},{1,2},{2,3},{3,4},{4,5},{5,6},{6,7},{7,8},{8,9},{9,10},{10,1... | collective-permute-start | bytes 786440 | tf_op jit(solution)/shard_map/ppermute | solution.py:212
  56.2 1.9 %collective-permute-start.3 = (f32[256,256]{1,0:T(8,128)}, f32[256,256]{1,0:T(8,128)S(1)}, u32[]{:S(2)}, u32[]{:S(2)}) collective-permute-start(f32[256,256]{1,0:T(8,128)} %get-tuple-element.9), channel_id=1, source_target_pairs={{0,31},{1,0},{2,1},{3,2},{4,3},{5,4},{6,5},{7,6},{8,7},{9,8},{10,9... | collective-permute-start | bytes 786440 | tf_op jit(solution)/shard_map/ppermute | solution.py:211
  58.2 2.3 %collective-permute-done.2.below_ref = f32[256,256]{1,0:T(8,128)S(1)} collective-permute-done((f32[256,256]{1,0:T(8,128)}, f32[256,256]{1,0:T(8,128)S(1)}, u32[]{:S(2)}, u32[]{:S(2)}) %collective-permute-start.2) | collective-permute-done | bytes 262176 | tf_op jit(solution)/shard_map/ppermute | solution.py:212
  60.4 0.0 copy-start.1
  60.4 7.6 %collective-permute-done.3.above_ref = f32[256,256]{1,0:T(8,128)S(1)} collective-permute-done((f32[256,256]{1,0:T(8,128)}, f32[256,256]{1,0:T(8,128)S(1)}, u32[]{:S(2)}, u32[]{:S(2)}) %collective-permute-start.3) | collective-permute-done | bytes 262176 | tf_op jit(solution)/shard_map/ppermute | solution.py:211
  68.0 0.0 copy-start.2
  68.0 0.0 copy-done.1
  68.0 0.7 copy-done.2
  68.7 2.0 %shard_map.65 = f32[256,1024]{1,0:T(8,128)} custom-call(f32[256,256]{1,0:T(8,128)} %copy-done.1, f32[256,256]{1,0:T(8,128)} %copy-done.2, f32[256,1024]{1,0:T(8,128)} %get-tuple-element.10.edge_ref), custom_call_target="tpu_custom_call", output_to_operand_aliasing={{}: (2, {})} | custom-call | tf_op jit(solution)/shard_map/pallas_call | solution.py:166
  70.7 26.0 %all_to_all.11 = f32[4,64,1024]{2,1,0:T(8,128)S(1)} all-to-all(f32[4,64,1024]{2,1,0:T(8,128)} %bitcast.10), channel_id=1, replica_groups=mesh['tq'=4,'tr'=4,'space'=32] {'tq'}, dimensions={0} | all-to-all | bytes 2097152 | tf_op jit(solution)/shard_map/all_to_all | solution.py:214
  96.8 0.1 slice_add_fusion
  96.8 0.8 add.50
  (1 shorter events, 0.0 us)
Async XLA Ops:
  28.5 11.7 %copy-start = (bf16[4,64,1024]{2,1,0:T(8,128)(2,1)}, bf16[4,64,1024]{2,1,0:T(8,128)(2,1)S(1)}, u32[]{:S(2)}) copy-start(bf16[4,64,1024]{2,1,0:T(8,128)(2,1)S(1)} %all_to_all.10) | copy-start | bytes 1572868
  28.5 10.2 %collective-permute-start.1 = (bf16[4,64,256]{2,1,0:T(8,128)(2,1)S(1)}, bf16[4,64,256]{2,1,0:T(8,128)(2,1)S(1)}, u32[]{:S(2)}, u32[]{:S(2)}) collective-permute-start(bf16[4,64,256]{2,1,0:T(8,128)(2,1)S(1)} %get-tuple-element.11), channel_id=1, source_target_pairs={{0,31},{1,0},{2,1},{3,2},{4,3},{5,4},{6,5},{7,6},{8,7},{9,8},{10,9... | collective-permute-start | bytes 393224 | tf_op jit(solution)/shard_map/ppermute | solution.py:199
  31.8 8.4 %collective-permute-start = (bf16[4,64,256]{2,1,0:T(8,128)(2,1)S(1)}, bf16[4,64,256]{2,1,0:T(8,128)(2,1)S(1)}, u32[]{:S(2)}, u32[]{:S(2)}) collective-permute-start(bf16[4,64,256]{2,1,0:T(8,128)(2,1)S(1)} %get-tuple-element.12), channel_id=1, source_target_pairs={{0,1},{1,2},{2,3},{3,4},{4,5},{5,6},{6,7},{7,8},{8,9},{9,10},{10,1... | collective-permute-start | bytes 393224 | tf_op jit(solution)/shard_map/ppermute | solution.py:198
  38.7 1.5 %copy-start.3 = (bf16[4,64,256]{2,1,0:T(8,128)(2,1)}, bf16[4,64,256]{2,1,0:T(8,128)(2,1)S(1)}, u32[]{:S(2)}) copy-start(bf16[4,64,256]{2,1,0:T(8,128)(2,1)S(1)} %collective-permute-done.1) | copy-start | bytes 393220
  40.2 0.6 copy-start.4
  48.6 11.9 %collective-permute-start.2 = (f32[256,256]{1,0:T(8,128)}, f32[256,256]{1,0:T(8,128)S(1)}, u32[]{:S(2)}, u32[]{:S(2)}) collective-permute-start(f32[256,256]{1,0:T(8,128)} %get-tuple-element.8), channel_id=1, source_target_pairs={{0,1},{1,2},{2,3},{3,4},{4,5},{5,6},{6,7},{7,8},{8,9},{9,10},{10,1... | collective-permute-start | bytes 786440 | tf_op jit(solution)/shard_map/ppermute | solution.py:212
  56.2 11.8 %collective-permute-start.3 = (f32[256,256]{1,0:T(8,128)}, f32[256,256]{1,0:T(8,128)S(1)}, u32[]{:S(2)}, u32[]{:S(2)}) collective-permute-start(f32[256,256]{1,0:T(8,128)} %get-tuple-element.9), channel_id=1, source_target_pairs={{0,31},{1,0},{2,1},{3,2},{4,3},{5,4},{6,5},{7,6},{8,7},{9,8},{10,9... | collective-permute-start | bytes 786440 | tf_op jit(solution)/shard_map/ppermute | solution.py:211
  60.4 7.6 %copy-start.1 = (f32[256,256]{1,0:T(8,128)}, f32[256,256]{1,0:T(8,128)S(1)}, u32[]{:S(2)}) copy-start(f32[256,256]{1,0:T(8,128)S(1)} %collective-permute-done.2.below_ref) | copy-start | bytes 786436
  68.0 0.7 copy-start.2

commit v13 on v11

--- a/solution.py
+++ b/solution.py
@@ -41,21 +41,16 @@
     return with_halo(grouped, (("space", grouped.ndim - 1),), EDGE * GROUP_SITE_SPAN)
 
 
-def observe_kernel(idx_ref, cnt_ref, low_ref, mid_ref, high_ref, op_ref, val_ref, wt_ref, out_ref, ext_ref):
+def observe_kernel(idx_ref, cnt_ref, ext_ref, op_ref, val_ref, wt_ref, out_ref):
     step = pl.program_id(0)
     width = GROUP_SITE_SPAN
     fields = val_ref.shape[0]
     rows = ext_ref.shape[0]
-    rim = low_ref.shape[1]
-    tile = mid_ref.shape[1]
     blocks = op_ref.shape[0]
     period = 8
 
     @pl.when(step == 0)
     def _():
-        ext_ref[:, :rim] = low_ref[...]
-        ext_ref[:, rim:rim + tile] = mid_ref[...]
-        ext_ref[:, rim + tile:] = high_ref[...]
         out_ref[...] = jnp.zeros_like(out_ref)
 
     count = cnt_ref[0]
@@ -88,10 +83,8 @@
     backward(*pending)
 
 
-def observe(low, mid, high, operator, indices, values, weights, counts):
-    rows, tile = mid.shape
-    rim = low.shape[1]
-    cells = tile + 2 * rim
+def observe(ext_rows, operator, indices, values, weights, counts):
+    rows, cells = ext_rows.shape
     obs_blocks = operator.shape[0]
     width = GROUP_SITE_SPAN
     fields = values.shape[0]
@@ -102,15 +95,12 @@
         num_scalar_prefetch=2,
         grid=(steps,),
         in_specs=[
-            pl.BlockSpec((rows, rim), whole),
-            pl.BlockSpec((rows, tile), whole),
-            pl.BlockSpec((rows, rim), whole),
+            pl.BlockSpec((rows, cells), whole),
             pl.BlockSpec((BLOCKS_PER_STEP, width, width), lambda g, i, c: (g, 0, 0)),
             pl.BlockSpec((fields, span), lambda g, i, c: (0, g)),
             pl.BlockSpec((fields, span), lambda g, i, c: (0, g)),
         ],
         out_specs=pl.BlockSpec((rows, cells), whole),
-        scratch_shapes=[pltpu.VMEM((rows, cells), mid.dtype)],
     )
     flops = 4 * obs_blocks * rows * width * width
     bytes_accessed = operator.size * 2 + rows * cells * 6 + values.size * 4
@@ -122,7 +112,7 @@
         cost_estimate=pl.CostEstimate(
             flops=flops, bytes_accessed=bytes_accessed, transcendentals=0
         ),
-    )(indices, counts, low, mid, high, operator, values, weights)
+    )(indices, counts, ext_rows, operator, values, weights)
 
 
 def settle(adjoint_ext):
@@ -142,17 +132,16 @@
     own = hindcast_archive[0]
     leads, members, fields, cells = own.shape
     own = own.reshape(leads, members * fields, cells)
-    outgoing = jnp.roll(own, here, axis=0)
-    incoming = lax.all_to_all(outgoing, "tq", 0, 0, tiled=True)
     rim = EDGE * GROUP_SITE_SPAN
     space = lax.axis_size("space")
-    low = lax.ppermute(incoming[..., cells - rim:], "space", ring_pairs(space, 1))
-    high = lax.ppermute(incoming[..., :rim], "space", ring_pairs(space, -1))
+    low = lax.ppermute(own[..., cells - rim:], "space", ring_pairs(space, 1))
+    high = lax.ppermute(own[..., :rim], "space", ring_pairs(space, -1))
+    extended = jnp.concatenate([low, own, high], axis=-1)
+    outgoing = jnp.roll(extended, here, axis=0)
+    incoming = lax.all_to_all(outgoing, "tq", 0, 0, tiled=True)
     width = cells + 2 * rim
     adjoint_rows = observe(
-        low.reshape(leads * members * fields, rim),
-        incoming.reshape(leads * members * fields, cells),
-        high.reshape(leads * members * fields, rim),
+        incoming.reshape(leads * members * fields, width),
         op_blocks[0],
         block_index[0],
         obs_values[0],

time: 94.8 us -> 102 us (1.076)
  the two profiles are of different devices: /device:TPU:64 before, /device:TPU:128 now
where the time goes in v13:
time: 102 us
  waiting for transfers between devices  31.6 us (31%)
  blocking collectives  29.4 us (29%)
  starting transfers between devices  24.4 us (24%)
  Pallas kernels  7.65 us (8%)
  local copies, waits for them, and re-layouts  5.33 us (5%)
  other arithmetic  2.59 us (3%)
    all_to_all x1, blocking collectives, body(): returned = lax.all_to_all(interior, 'tq', 0, 0, tiled=True)  29.4 us
    all_to_all x1, waiting for transfers between devices, body(): incoming = lax.all_to_all(outgoing, 'tq', 0, 0, tiled=True)  18.2 us
    all_to_all x1, starting transfers between devices, body(): incoming = lax.all_to_all(outgoing, 'tq', 0, 0, tiled=True)  9.04 us
    pallas_call x1, Pallas kernels, observe(): pl.pallas_call(observe_kernel, grid_spec=grid_spec, out_shape=jax.ShapeDt...  7.65 us
    ppermute x1, starting transfers between devices, body(): high = lax.ppermute(own[..., :rim], 'space', ring_pairs(space, -1))  7.57 us
    ppermute x1, waiting for transfers between devices, body(): low = lax.ppermute(own[..., cells - rim:], 'space', ring_pairs(space, 1))  7.45 us
    ppermute x2, starting transfers between devices, passed_along(): return lax.ppermute(value, axis, pairs)  5.84 us
    ppermute x2, waiting for transfers between devices, passed_along(): return lax.ppermute(value, axis, pairs)  5.22 us
  transfers between devices with their start and end apart: 5, of which 5 were waited for; matrix products, arithmetic and copies ran while one was open for 2% of the time, Pallas kernels for 0%

profile of v13, /device:TPU:128, one launch (start us, length us, event | category | flops | bytes accessed | tf_op | source)
XLA Modules:
  0.0 101.7 jit_solution(65315135859366826)
XLA Ops:
  0.0 1.2 %reshape_squeeze.3 = bf16[4,64,1024]{2,1,0:T(8,128)(2,1)S(1)} reshape(bf16[1,4,16,4,1024]{4,3,2,1,0:T(4,128)(2,1)} %param.10) | data formatting | bytes 1048576 | tf_op jit(solution)/shard_map/reshape;squeeze | solution.py:134
  1.2 7.6 %collective-permute-start.1 = (bf16[4,64,256]{2,1,0:T(8,128)(2,1)S(1)}, bf16[4,64,256]{2,1,0:T(8,128)(2,1)S(1)}, u32[]{:S(2)}, u32[]{:S(2)}) collective-permute-start(bf16[4,64,256]{2,1,0:T(8,128)(2,1)S(1)} %get-tuple-element.31), channel_id=1, source_target_pairs={{0,31},{1,0},{2,1},{3,2},{4,3},{5,4},{6,5},{7,6},{8,7},{9,8},{10,9... | collective-permute-start | bytes 393224 | tf_op jit(solution)/shard_map/ppermute | solution.py:138
  8.8 1.9 %collective-permute-start = (bf16[4,64,256]{2,1,0:T(8,128)(2,1)S(1)}, bf16[4,64,256]{2,1,0:T(8,128)(2,1)S(1)}, u32[]{:S(2)}, u32[]{:S(2)}) collective-permute-start(bf16[4,64,256]{2,1,0:T(8,128)(2,1)S(1)} %get-tuple-element.32), channel_id=1, source_target_pairs={{0,1},{1,2},{2,3},{3,4},{4,5},{5,6},{6,7},{7,8},{8,9},{9,10},{10,1... | collective-permute-start | bytes 393224 | tf_op jit(solution)/shard_map/ppermute | solution.py:137
  10.7 0.8 collective-permute-done.1
  11.5 7.4 %collective-permute-done = bf16[4,64,256]{2,1,0:T(8,128)(2,1)S(1)} collective-permute-done((bf16[4,64,256]{2,1,0:T(8,128)(2,1)S(1)}, bf16[4,64,256]{2,1,0:T(8,128)(2,1)S(1)}, u32[]{:S(2)}, u32[]{:S(2)}) %collective-permute-start) | collective-permute-done | bytes 131104 | tf_op jit(solution)/shard_map/ppermute | solution.py:137
  19.0 1.5 %fusion.2 = bf16[4,64,1536]{2,1,0:T(8,128)(2,1)} fusion(s32[]{:T(128)S(6)} %select_n.14, bf16[4,64,256]{2,1,0:T(8,128)(2,1)S(1)} %collective-permute-done, bf16[4,64,1024]{2,1,0:T(8,128)(2,1)S(1)} %reshape_squeeze.3, bf16[4,64,256]{2,1,0:T(8,128)(2,1)S(1)} %collective-permute-done.1), kind=kLoop, calls=%fused_computation.8 | loop fusion | flops 4718592 | bytes 1572868 | tf_op jit(solution)/shard_map/jit(_roll_dynamic)/concatenate | solution.py:140
  20.5 9.0 %all-to-all-start = ((bf16[4,64,1536]{2,1,0:T(8,128)(2,1)}), bf16[4,64,1536]{2,1,0:T(8,128)(2,1)S(1)}, u32[]{:S(2)}, u32[]{:S(2)}) async-start(bf16[4,64,1536]{2,1,0:T(8,128)(2,1)} %fusion.2), calls=%async_computation | async-start | bytes 1572864 | tf_op jit(solution)/shard_map/all_to_all | solution.py:141
  30.2 18.2 %all-to-all-done = bf16[4,64,1536]{2,1,0:T(8,128)(2,1)S(1)} async-done(((bf16[4,64,1536]{2,1,0:T(8,128)(2,1)}), bf16[4,64,1536]{2,1,0:T(8,128)(2,1)S(1)}, u32[]{:S(2)}, u32[]{:S(2)}) %all-to-all-start) | async-done | bytes 786464 | tf_op jit(solution)/shard_map/all_to_all | solution.py:141
  48.3 0.0 copy-start
  48.3 0.9 copy-done
  49.2 7.7 %shard_map.64 = f32[256,1536]{1,0:T(8,128)} custom-call(s32[96]{0:T(128)} %bitcast.21, s32[1]{0:T(128)} %bitcast.12.cnt_ref, bf16[256,1536]{1,0:T(8,128)(2,1)} %bitcast.17, bf16[96,128,128]{2,1,0:T(8,128)(2,1)} %bitcast.18, bf16[4,12288]{1,0:T(4,128)(2,1)} %bitcast.19, bf16[4,12288]{1,0:T(4,128)(2,1)} %bitcast.20), custom_call_target="tpu_custom_call" | custom-call | flops 1610612736 | bytes 5701632 | tf_op jit(solution)/shard_map/pallas_call | solution.py:107
  56.8 1.1 %fusion.8 = (f32[1,4,64,256]{3,2,1,0:T(8,128)S(1)}, f32[1,4,64,256]{3,2,1,0:T(8,128)S(1)}) fusion(f32[1,4,64,1536]{3,2,1,0:T(8,128)} %bitcast.14), kind=kLoop, calls=%fused_computation.19 | loop fusion | bytes 1048576 | tf_op jit(solution)/shard_map/slice | solution.py:121
  57.9 1.9 %collective-permute-start.2 = (f32[1,4,64,256]{3,2,1,0:T(8,128)S(1)}, f32[1,4,64,256]{3,2,1,0:T(8,128)S(1)}, u32[]{:S(2)}, u32[]{:S(2)}) collective-permute-start(f32[1,4,64,256]{3,2,1,0:T(8,128)S(1)} %get-tuple-element.30), channel_id=1, source_target_pairs={{0,31},{1,0},{2,1},{3,2},{4,3},{5,4},{6,5},{7,6},{8,7},{9,8},{10,9... | collective-permute-start | bytes 786440 | tf_op jit(solution)/shard_map/ppermute | solution.py:37
  59.8 3.9 %collective-permute-start.3 = (f32[1,4,64,256]{3,2,1,0:T(8,128)S(1)}, f32[1,4,64,256]{3,2,1,0:T(8,128)S(1)}, u32[]{:S(2)}, u32[]{:S(2)}) collective-permute-start(f32[1,4,64,256]{3,2,1,0:T(8,128)S(1)} %get-tuple-element.29), channel_id=1, source_target_pairs={{0,1},{1,2},{2,3},{3,4},{4,5},{5,6},{6,7},{7,8},{8,9},{9,10},{10,1... | collective-permute-start | bytes 786440 | tf_op jit(solution)/shard_map/ppermute | solution.py:37
  63.8 1.3 %slice.99 = f32[1,4,64,1024]{3,2,1,0:T(8,128)S(1)} slice(f32[1,4,64,1536]{3,2,1,0:T(8,128)} %bitcast.15), slice={[0:1], [0:4], [0:64], [256:1280]} | slice | bytes 2097152 | tf_op jit(solution)/shard_map/slice | solution.py:122
  65.1 1.1 %collective-permute-done.2 = f32[1,4,64,256]{3,2,1,0:T(8,128)S(1)} collective-permute-done((f32[1,4,64,256]{3,2,1,0:T(8,128)S(1)}, f32[1,4,64,256]{3,2,1,0:T(8,128)S(1)}, u32[]{:S(2)}, u32[]{:S(2)}) %collective-permute-start.2) | collective-permute-done | bytes 262176 | tf_op jit(solution)/shard_map/ppermute | solution.py:37
  66.2 1.0 fusion.7
  67.2 0.1 copy.8
  67.3 4.1 %collective-permute-done.3 = f32[1,4,64,256]{3,2,1,0:T(8,128)S(1)} collective-permute-done((f32[1,4,64,256]{3,2,1,0:T(8,128)S(1)}, f32[1,4,64,256]{3,2,1,0:T(8,128)S(1)}, u32[]{:S(2)}, u32[]{:S(2)}) %collective-permute-start.3) | collective-permute-done | bytes 262176 | tf_op jit(solution)/shard_map/ppermute | solution.py:37
  71.5 29.4 %all_to_all.10 = f32[4,64,1024]{2,1,0:T(8,128)S(1)} all-to-all(f32[4,64,1024]{2,1,0:T(8,128)S(1)} %fusion.6), channel_id=1, replica_groups=mesh['tq'=4,'tr'=4,'space'=32] {'tq'}, dimensions={0} | all-to-all | bytes 2097152 | tf_op jit(solution)/shard_map/all_to_all | solution.py:152
  100.9 0.1 slice_add_fusion
  101.0 0.8 add.66
  (2 shorter events, 0.1 us)
Async XLA Ops:
  1.2 10.3 %collective-permute-start.1 = (bf16[4,64,256]{2,1,0:T(8,128)(2,1)S(1)}, bf16[4,64,256]{2,1,0:T(8,128)(2,1)S(1)}, u32[]{:S(2)}, u32[]{:S(2)}) collective-permute-start(bf16[4,64,256]{2,1,0:T(8,128)(2,1)S(1)} %get-tuple-element.31), channel_id=1, source_target_pairs={{0,31},{1,0},{2,1},{3,2},{4,3},{5,4},{6,5},{7,6},{8,7},{9,8},{10,9... | collective-permute-start | bytes 393224 | tf_op jit(solution)/shard_map/ppermute | solution.py:138
  8.8 10.2 %collective-permute-start = (bf16[4,64,256]{2,1,0:T(8,128)(2,1)S(1)}, bf16[4,64,256]{2,1,0:T(8,128)(2,1)S(1)}, u32[]{:S(2)}, u32[]{:S(2)}) collective-permute-start(bf16[4,64,256]{2,1,0:T(8,128)(2,1)S(1)} %get-tuple-element.32), channel_id=1, source_target_pairs={{0,1},{1,2},{2,3},{3,4},{4,5},{5,6},{6,7},{7,8},{8,9},{9,10},{10,1... | collective-permute-start | bytes 393224 | tf_op jit(solution)/shard_map/ppermute | solution.py:137
  20.5 27.8 %all-to-all-start = ((bf16[4,64,1536]{2,1,0:T(8,128)(2,1)}), bf16[4,64,1536]{2,1,0:T(8,128)(2,1)S(1)}, u32[]{:S(2)}, u32[]{:S(2)}) async-start(bf16[4,64,1536]{2,1,0:T(8,128)(2,1)} %fusion.2), calls=%async_computation | async-start | bytes 1572864 | tf_op jit(solution)/shard_map/all_to_all | solution.py:141
  48.3 0.9 copy-start
  57.9 8.3 %collective-permute-start.2 = (f32[1,4,64,256]{3,2,1,0:T(8,128)S(1)}, f32[1,4,64,256]{3,2,1,0:T(8,128)S(1)}, u32[]{:S(2)}, u32[]{:S(2)}) collective-permute-start(f32[1,4,64,256]{3,2,1,0:T(8,128)S(1)} %get-tuple-element.30), channel_id=1, source_target_pairs={{0,31},{1,0},{2,1},{3,2},{4,3},{5,4},{6,5},{7,6},{8,7},{9,8},{10,9... | collective-permute-start | bytes 786440 | tf_op jit(solution)/shard_map/ppermute | solution.py:37
  59.8 11.6 %collective-permute-start.3 = (f32[1,4,64,256]{3,2,1,0:T(8,128)S(1)}, f32[1,4,64,256]{3,2,1,0:T(8,128)S(1)}, u32[]{:S(2)}, u32[]{:S(2)}) collective-permute-start(f32[1,4,64,256]{3,2,1,0:T(8,128)S(1)} %get-tuple-element.29), channel_id=1, source_target_pairs={{0,1},{1,2},{2,3},{3,4},{4,5},{5,6},{6,7},{7,8},{8,9},{9,10},{10,1... | collective-permute-start | bytes 786440 | tf_op jit(solution)/shard_map/ppermute | solution.py:37

commit v14 on v10

v14 whole, which is shorter than its diff:
```python
import functools

import functools

import jax
import jax.numpy as jnp
from jax import lax
from jax.experimental import pallas as pl
from jax.experimental.pallas import tpu as pltpu
from jax.sharding import Mesh
from jax.sharding import PartitionSpec as P

GROUP_SITE_SPAN = 128
EDGE = 2
BLOCKS_PER_STEP = 96


def with_halo(block, sides, width):
    for axis, dim in sides:
        count = lax.axis_size(axis)
        forward = [(i, i + 1) for i in range(count - 1)]
        forward.append((count - 1, 0))
        backward = [(target, source) for source, target in forward]
        low = lax.ppermute(
            lax.slice_in_dim(block, block.shape[dim] - width, None, axis=dim), axis, forward
        )
        high = lax.ppermute(lax.slice_in_dim(block, 0, width, axis=dim), axis, backward)
        block = jnp.concatenate([low, block, high], axis=dim)
    return block


def ring_pairs(count, steps):
    return [(source, (source + steps) % count) for source in range(count)]


def passed_along(value, axis, steps):
    count = lax.axis_size(axis)
    pairs = [(source, (source + steps) % count) for source in range(count)]
    return lax.ppermute(value, axis, pairs)


def extend(grouped):
    return with_halo(grouped, (("space", grouped.ndim - 1),), EDGE * GROUP_SITE_SPAN)


def pass_kernel(edge, idx_ref, cnt_ref, src_ref, op_ref, val_ref, wt_ref, *rest):
    if edge:
        acc_ref, out_ref = rest
    else:
        (out_ref,) = rest
    width = GROUP_SITE_SPAN
    fields = val_ref.shape[0]
    rows = src_ref.shape[0]
    blocks = op_ref.shape[0]
    low_blocks = EDGE
    own_blocks = out_ref.shape[1] // width - 2 * EDGE
    period = 8
    if edge:
        out_ref[...] = acc_ref[...]
    else:
        out_ref[...] = jnp.zeros_like(out_ref)
    count = cnt_ref[0]
    lane = lax.broadcasted_iota(jnp.int32, (1, width), 1)
    for k in range(blocks):
        index = idx_ref[k]
        inside = jnp.logical_and(index >= low_blocks, index < low_blocks + own_blocks)
        take = jnp.logical_not(inside) if edge else inside

        @pl.when(take)
        def _():
            if edge:
                column = jnp.where(index < low_blocks, index, index - own_blocks)
            else:
                column = index - low_blocks
            x = src_ref[:, pl.ds(pl.multiple_of(column * width, width), width)]
            op = op_ref[k]
            images = lax.dot_general(
                x, op, (((1,), (1,)), ((), ())), preferred_element_type=jnp.float32
            ).reshape(rows // period, period, width)
            observed = val_ref[:, k * width:(k + 1) * width].astype(jnp.float32)
            observed = jnp.concatenate([observed] * (period // fields), axis=0)[None]
            live = (k * width + lane) < count
            scaling = jnp.where(live, wt_ref[:, k * width:(k + 1) * width].astype(jnp.float32), 0.0)
            scaling = jnp.concatenate([scaling] * (period // fields), axis=0)[None]
            misfit = ((images - observed) * scaling).reshape(rows, width).astype(jnp.bfloat16)
            start = pl.multiple_of(index * width, width)
            out_ref[:, pl.ds(start, width)] += jnp.dot(
                misfit, op, preferred_element_type=jnp.float32
            )


def observe_pass(edge, src, operator, indices, values, weights, counts, acc, cells):
    rows = src.shape[0]
    full = lambda *a: pl.BlockSpec(memory_space=pltpu.VMEM)
    operands = [indices, counts, src, operator, values, weights] + ([acc] if edge else [])
    flops = 2 * operator.shape[0] * rows * GROUP_SITE_SPAN * GROUP_SITE_SPAN
    return pl.pallas_call(
        functools.partial(pass_kernel, edge),
        in_specs=[pl.BlockSpec(memory_space=pltpu.SMEM)] * 2 + [full()] * (len(operands) - 2),
        out_specs=full(),
        out_shape=jax.ShapeDtypeStruct((rows, cells), jnp.float32),
        cost_estimate=pl.CostEstimate(
            flops=flops, bytes_accessed=operator.size * 2 + rows * cells * 8, transcendentals=0
        ),
    )(*operands)


def settle(adjoint_ext):
    rim_width = EDGE * GROUP_SITE_SPAN
    lower_rim = adjoint_ext[..., :rim_width]
    upper_rim = adjoint_ext[..., -rim_width:]
    interior = adjoint_ext[..., rim_width:-rim_width]
    from_above = passed_along(lower_rim, "space", -1)
    from_below = passed_along(upper_rim, "space", 1)
    interior = interior.at[..., -rim_width:].add(from_above)
    return interior.at[..., :rim_width].add(from_below)


def body(hindcast_archive, op_blocks, block_index, obs_values, obs_weights, obs_counts):
    ring = lax.axis_size("tq")
    here = lax.axis_index("tq")
    own = hindcast_archive[0]
    leads, members, fields, cells = own.shape
    own = own.reshape(leads, members * fields, cells)
    outgoing = jnp.roll(own, here, axis=0)
    incoming = lax.all_to_all(outgoing, "tq", 0, 0, tiled=True)
    rim = EDGE * GROUP_SITE_SPAN
    space = lax.axis_size("space")
    rows = leads * members * fields
    width = cells + 2 * rim
    args = (op_blocks[0], block_index[0], obs_values[0], obs_weights[0], obs_counts[0])
    low = lax.ppermute(incoming[..., cells - rim:], "space", ring_pairs(space, 1))
    high = lax.ppermute(incoming[..., :rim], "space", ring_pairs(space, -1))
    partial = observe_pass(False, incoming.reshape(rows, cells), *args, None, width)
    rims = jnp.concatenate([low.reshape(rows, rim), high.reshape(rows, rim)], axis=1)
    adjoint_rows = observe_pass(True, rims, *args, partial, width)
    interior = settle(adjoint_rows.reshape(1, leads, members * fields, width))[0]
    returned = lax.all_to_all(interior, "tq", 0, 0, tiled=True)
    running = returned[0]
    for slot in range(1, ring):
        running = running + returned[slot]
    return running.reshape(1, members, fields, cells)


def solution(mesh):
    tm_size = mesh.shape["tm"]
    lead_count = 4
    devices = mesh.devices.reshape(lead_count, tm_size // lead_count, mesh.shape["space"])
    ring_mesh = Mesh(devices, ("tq", "tr", "space"))
    tm = ("tq", "tr")
    in_specs = (
        P(tm, None, None, None, "space"),
        P(tm, "space", None, None),
        P(tm, "space"),
        P(tm, None, "space"),
        P(tm, None, "space"),
        P(tm, "space"),
    )
    out_specs = P(tm, None, None, "space")
    return jax.shard_map(body, mesh=ring_mesh, in_specs=in_specs, out_specs=out_specs, check_vma=False)
```

time: 95.4 us -> 120 us (1.26)
  Pallas kernels: 8.02 us -> 37.2 us
  starting transfers between devices: 19.1 us -> 15.3 us
  waiting for transfers between devices: 9.07 us -> 7.13 us
  blocking collectives: 51.2 us -> 53 us
    pallas_call x1 -> x2, Pallas kernels: 8.02 us -> 37.2 us  [observe_pass(): pl.pallas_call(functools.partial(pass_kernel, edge), in_specs=[pl.BlockSp...]
    ppermute x2, starting transfers between devices: 9.59 us -> 5.84 us  [passed_along(): return lax.ppermute(value, axis, pairs)]
    ppermute x2, waiting for transfers between devices: 1.85 us -> 0.01 us  [the longest x1 0.01 us: body(): lax.ppermute(incoming[..., cells - rim:], 'space', ring_pairs(space, 1))]
    all_to_all x1, blocking collectives: 25.5 us -> 27.2 us  [body(): returned = lax.all_to_all(interior, 'tq', 0, 0, tiled=True)]
  transfers between devices with their start and end apart: 4 -> 4, of which waited for: 4 -> 2; matrix products, arithmetic and copies ran while one was open for 3% -> 2% of each run, Pallas kernels for 0% -> 20%
where the time goes in v14:
time: 120 us
  blocking collectives  53 us (44%)
  Pallas kernels  37.2 us (31%)
  starting transfers between devices  15.3 us (13%)
  waiting for transfers between devices  7.13 us (6%)
  local copies, waits for them, and re-layouts  4.45 us (4%)
  other arithmetic  2.01 us (2%)
    pallas_call x2, Pallas kernels, observe_pass(): pl.pallas_call(functools.partial(pass_kernel, edge), in_specs=[pl.BlockSp...  37.2 us
    all_to_all x1, blocking collectives, body(): returned = lax.all_to_all(interior, 'tq', 0, 0, tiled=True)  27.2 us
    all_to_all x1, blocking collectives, body(): incoming = lax.all_to_all(outgoing, 'tq', 0, 0, tiled=True)  25.8 us
    ppermute x2, waiting for transfers between devices, passed_along(): return lax.ppermute(value, axis, pairs)  7.13 us
    ppermute x1, starting transfers between devices, body(): high = lax.ppermute(incoming[..., :rim], 'space', ring_pairs(space, -1))  6.01 us
    ppermute x2, starting transfers between devices, passed_along(): return lax.ppermute(value, axis, pairs)  5.84 us
    ppermute x1, starting transfers between devices, body(): lax.ppermute(incoming[..., cells - rim:], 'space', ring_pairs(space, 1))  3.48 us
  transfers between devices with their start and end apart: 4, of which 2 were waited for; matrix products, arithmetic and copies ran while one was open for 2% of the time, Pallas kernels for 20%

profile of v14, /device:TPU:64, one launch (start us, length us, event | category | flops | bytes accessed | tf_op | source)
XLA Modules:
  0.0 119.9 jit_solution(7207933339364197024)
XLA Ops:
  0.0 1.2 reshape_squeeze.3
  1.2 0.2 fusion
  1.4 25.8 %all_to_all.10 = bf16[4,64,1024]{2,1,0:T(8,128)(2,1)S(1)} all-to-all(bf16[4,64,1024]{2,1,0:T(8,128)(2,1)S(1)} %fusion), channel_id=1, replica_groups=mesh['tq'=4,'tr'=4,'space'=32] {'tq'}, dimensions={0} | all-to-all | bytes 1048576 | tf_op jit(solution)/shard_map/all_to_all | solution.py:126
  27.2 0.0 copy-start
  27.2 3.5 %collective-permute-start = (bf16[4,64,256]{2,1,0:T(8,128)(2,1)S(1)}, bf16[4,64,256]{2,1,0:T(8,128)(2,1)S(1)}, u32[]{:S(2)}, u32[]{:S(2)}) collective-permute-start(bf16[4,64,256]{2,1,0:T(8,128)(2,1)S(1)} %get-tuple-element.31), channel_id=1, source_target_pairs={{0,1},{1,2},{2,3},{3,4},{4,5},{5,6},{6,7},{7,8},{8,9},{9,10},{10,1... | collective-permute-start | bytes 393224 | tf_op jit(solution)/shard_map/ppermute | solution.py:132
  30.7 6.0 %collective-permute-start.1 = (bf16[4,64,256]{2,1,0:T(8,128)(2,1)S(1)}, bf16[4,64,256]{2,1,0:T(8,128)(2,1)S(1)}, u32[]{:S(2)}, u32[]{:S(2)}) collective-permute-start(bf16[4,64,256]{2,1,0:T(8,128)(2,1)S(1)} %get-tuple-element.32), channel_id=1, source_target_pairs={{0,31},{1,0},{2,1},{3,2},{4,3},{5,4},{6,5},{7,6},{8,7},{9,8},{10,9... | collective-permute-start | bytes 393224 | tf_op jit(solution)/shard_map/ppermute | solution.py:133
  37.4 0.0 copy-done
  37.4 23.8 %shard_map.64.rest_0_ = f32[256,1536]{1,0:T(8,128)} custom-call(s32[96]{0:T(128)} %bitcast.29, s32[1]{0:T(128)} %bitcast.14.cnt_ref, bf16[256,1024]{1,0:T(8,128)(2,1)} %bitcast.22, bf16[96,128,128]{2,1,0:T(8,128)(2,1)} %bitcast.16, bf16[4,12288]{1,0:T(4,128)(2,1)} %bitcast.23, bf16[4,12288]{1,0:T(4,128)(2,1)} %bitcast.25), custom_call_target="tpu_custom_call" | custom-call | flops 805306368 | bytes 6291456 | tf_op jit(solution)/shard_map/pallas_call | solution.py:97
  61.2 0.0 collective-permute-done
  61.2 0.0 collective-permute-done.1
  61.2 0.7 pad_maximum_fusion.src_ref
  61.9 13.3 %shard_map.65 = f32[256,1536]{1,0:T(8,128)} custom-call(s32[96]{0:T(128)} %bitcast.30, s32[1]{0:T(128)} %bitcast.15.cnt_ref, bf16[256,512]{1,0:T(8,128)(2,1)} %pad_maximum_fusion.src_ref, bf16[96,128,128]{2,1,0:T(8,128)(2,1)} %bitcast.17, bf16[4,12288]{1,0:T(4,128)(2,1)} %bitcast.24, bf16[4,12288]{1,0:T(4,128)(2,1)} %bitcast.26, f32[256,1536]{1,0:T(8,128)} %shard_map.64.rest_0_), custom_call_target="tpu_custom_call" | custom-call | flops 805306368 | bytes 6291456 | tf_op jit(solution)/shard_map/pallas_call | solution.py:97
  75.3 1.1 fusion.4
  76.3 3.8 %collective-permute-start.2 = (f32[1,4,64,256]{3,2,1,0:T(8,128)S(1)}, f32[1,4,64,256]{3,2,1,0:T(8,128)S(1)}, u32[]{:S(2)}, u32[]{:S(2)}) collective-permute-start(f32[1,4,64,256]{3,2,1,0:T(8,128)S(1)} %get-tuple-element.30), channel_id=1, source_target_pairs={{0,31},{1,0},{2,1},{3,2},{4,3},{5,4},{6,5},{7,6},{8,7},{9,8},{10,9... | collective-permute-start | bytes 786440 | tf_op jit(solution)/shard_map/ppermute | solution.py:39
  80.2 2.0 %collective-permute-start.3 = (f32[1,4,64,256]{3,2,1,0:T(8,128)S(1)}, f32[1,4,64,256]{3,2,1,0:T(8,128)S(1)}, u32[]{:S(2)}, u32[]{:S(2)}) collective-permute-start(f32[1,4,64,256]{3,2,1,0:T(8,128)S(1)} %get-tuple-element.29), channel_id=1, source_target_pairs={{0,1},{1,2},{2,3},{3,4},{4,5},{5,6},{6,7},{7,8},{8,9},{9,10},{10,1... | collective-permute-start | bytes 786440 | tf_op jit(solution)/shard_map/ppermute | solution.py:39
  82.2 1.3 %slice.99 = f32[1,4,64,1024]{3,2,1,0:T(8,128)S(1)} slice(f32[1,4,64,1536]{3,2,1,0:T(8,128)} %bitcast.19), slice={[0:1], [0:4], [0:64], [256:1280]} | slice | bytes 2097152 | tf_op jit(solution)/shard_map/slice | solution.py:112
  83.5 1.4 %collective-permute-done.2 = f32[1,4,64,256]{3,2,1,0:T(8,128)S(1)} collective-permute-done((f32[1,4,64,256]{3,2,1,0:T(8,128)S(1)}, f32[1,4,64,256]{3,2,1,0:T(8,128)S(1)}, u32[]{:S(2)}, u32[]{:S(2)}) %collective-permute-start.2) | collective-permute-done | bytes 262176 | tf_op jit(solution)/shard_map/ppermute | solution.py:39
  85.0 1.0 fusion.3
  85.9 0.1 copy.8
  86.1 5.7 %collective-permute-done.3 = f32[1,4,64,256]{3,2,1,0:T(8,128)S(1)} collective-permute-done((f32[1,4,64,256]{3,2,1,0:T(8,128)S(1)}, f32[1,4,64,256]{3,2,1,0:T(8,128)S(1)}, u32[]{:S(2)}, u32[]{:S(2)}) %collective-permute-start.3) | collective-permute-done | bytes 262176 | tf_op jit(solution)/shard_map/ppermute | solution.py:39
  91.8 27.2 %all_to_all.11 = f32[4,64,1024]{2,1,0:T(8,128)S(1)} all-to-all(f32[4,64,1024]{2,1,0:T(8,128)S(1)} %fusion.2), channel_id=1, replica_groups=mesh['tq'=4,'tr'=4,'space'=32] {'tq'}, dimensions={0} | all-to-all | bytes 2097152 | tf_op jit(solution)/shard_map/all_to_all | solution.py:138
  119.0 0.1 slice_add_fusion
  119.1 0.8 add.66
  (2 shorter events, 0.1 us)
Async XLA Ops:
  27.2 10.2 %copy-start = (bf16[4,64,1024]{2,1,0:T(8,128)(2,1)}, bf16[4,64,1024]{2,1,0:T(8,128)(2,1)S(1)}, u32[]{:S(2)}) copy-start(bf16[4,64,1024]{2,1,0:T(8,128)(2,1)S(1)} %all_to_all.10) | copy-start | bytes 1572868
  27.2 34.0 %collective-permute-start = (bf16[4,64,256]{2,1,0:T(8,128)(2,1)S(1)}, bf16[4,64,256]{2,1,0:T(8,128)(2,1)S(1)}, u32[]{:S(2)}, u32[]{:S(2)}) collective-permute-start(bf16[4,64,256]{2,1,0:T(8,128)(2,1)S(1)} %get-tuple-element.31), channel_id=1, source_target_pairs={{0,1},{1,2},{2,3},{3,4},{4,5},{5,6},{6,7},{7,8},{8,9},{9,10},{10,1... | collective-permute-start | bytes 393224 | tf_op jit(solution)/shard_map/ppermute | solution.py:132
  30.7 30.5 %collective-permute-start.1 = (bf16[4,64,256]{2,1,0:T(8,128)(2,1)S(1)}, bf16[4,64,256]{2,1,0:T(8,128)(2,1)S(1)}, u32[]{:S(2)}, u32[]{:S(2)}) collective-permute-start(bf16[4,64,256]{2,1,0:T(8,128)(2,1)S(1)} %get-tuple-element.32), channel_id=1, source_target_pairs={{0,31},{1,0},{2,1},{3,2},{4,3},{5,4},{6,5},{7,6},{8,7},{9,8},{10,9... | collective-permute-start | bytes 393224 | tf_op jit(solution)/shard_map/ppermute | solution.py:133
  76.3 8.6 %collective-permute-start.2 = (f32[1,4,64,256]{3,2,1,0:T(8,128)S(1)}, f32[1,4,64,256]{3,2,1,0:T(8,128)S(1)}, u32[]{:S(2)}, u32[]{:S(2)}) collective-permute-start(f32[1,4,64,256]{3,2,1,0:T(8,128)S(1)} %get-tuple-element.30), channel_id=1, source_target_pairs={{0,31},{1,0},{2,1},{3,2},{4,3},{5,4},{6,5},{7,6},{8,7},{9,8},{10,9... | collective-permute-start | bytes 786440 | tf_op jit(solution)/shard_map/ppermute | solution.py:39
  80.2 11.6 %collective-permute-start.3 = (f32[1,4,64,256]{3,2,1,0:T(8,128)S(1)}, f32[1,4,64,256]{3,2,1,0:T(8,128)S(1)}, u32[]{:S(2)}, u32[]{:S(2)}) collective-permute-start(f32[1,4,64,256]{3,2,1,0:T(8,128)S(1)} %get-tuple-element.29), channel_id=1, source_target_pairs={{0,1},{1,2},{2,3},{3,4},{4,5},{5,6},{6,7},{7,8},{8,9},{9,10},{10,1... | collective-permute-start | bytes 786440 | tf_op jit(solution)/shard_map/ppermute | solution.py:39

commit v15 on v11

--- a/solution.py
+++ b/solution.py
@@ -41,7 +41,9 @@
     return with_halo(grouped, (("space", grouped.ndim - 1),), EDGE * GROUP_SITE_SPAN)
 
 
-def observe_kernel(idx_ref, cnt_ref, low_ref, mid_ref, high_ref, op_ref, val_ref, wt_ref, out_ref, ext_ref):
+def observe_kernel(
+    idx_ref, cnt_ref, low_ref, mid_ref, high_ref, op_ref, val_ref, wt_ref, out_ref, low_out, high_out, ext_ref,
+):
     step = pl.program_id(0)
     width = GROUP_SITE_SPAN
     fields = val_ref.shape[0]
@@ -86,6 +88,8 @@
         backward(*pending)
         pending = ahead
     backward(*pending)
+    low_out[...] = out_ref[:, :rim]
+    high_out[...] = out_ref[:, rim + tile:]
 
 
 def observe(low, mid, high, operator, indices, values, weights, counts):
@@ -109,7 +113,11 @@
             pl.BlockSpec((fields, span), lambda g, i, c: (0, g)),
             pl.BlockSpec((fields, span), lambda g, i, c: (0, g)),
         ],
-        out_specs=pl.BlockSpec((rows, cells), whole),
+        out_specs=[
+            pl.BlockSpec((rows, cells), whole),
+            pl.BlockSpec((rows, rim), whole),
+            pl.BlockSpec((rows, rim), whole),
+        ],
         scratch_shapes=[pltpu.VMEM((rows, cells), mid.dtype)],
     )
     flops = 4 * obs_blocks * rows * width * width
@@ -117,7 +125,11 @@
     return pl.pallas_call(
         observe_kernel,
         grid_spec=grid_spec,
-        out_shape=jax.ShapeDtypeStruct((rows, cells), jnp.float32),
+        out_shape=[
+            jax.ShapeDtypeStruct((rows, cells), jnp.float32),
+            jax.ShapeDtypeStruct((rows, rim), jnp.float32),
+            jax.ShapeDtypeStruct((rows, rim), jnp.float32),
+        ],
         compiler_params=pltpu.CompilerParams(dimension_semantics=("arbitrary",)),
         cost_estimate=pl.CostEstimate(
             flops=flops, bytes_accessed=bytes_accessed, transcendentals=0
@@ -149,7 +161,7 @@
     low = lax.ppermute(incoming[..., cells - rim:], "space", ring_pairs(space, 1))
     high = lax.ppermute(incoming[..., :rim], "space", ring_pairs(space, -1))
     width = cells + 2 * rim
-    adjoint_rows = observe(
+    adjoint_rows, low_adj, high_adj = observe(
         low.reshape(leads * members * fields, rim),
         incoming.reshape(leads * members * fields, cells),
         high.reshape(leads * members * fields, rim),
@@ -159,7 +171,11 @@
         obs_weights[0],
         obs_counts[0],
     )
-    interior = settle(adjoint_rows.reshape(1, leads, members * fields, width))[0]
+    from_above = passed_along(low_adj.reshape(leads, members * fields, rim), "space", -1)
+    from_below = passed_along(high_adj.reshape(leads, members * fields, rim), "space", 1)
+    interior = adjoint_rows.reshape(leads, members * fields, width)[..., rim:rim + cells]
+    interior = interior.at[..., cells - rim:].add(from_above)
+    interior = interior.at[..., :rim].add(from_below)
     returned = lax.all_to_all(interior, "tq", 0, 0, tiled=True)
     running = returned[0]
     for slot in range(1, ring):

time: 94.8 us -> 94.1 us (level)
  local copies, waits for them, and re-layouts: 5.1 us -> 3.95 us
    slice x2 -> x1, local copies, waits for them, and re-layouts: 2.39 us -> 1.33 us  [body(): adjoint_rows.reshape(leads, members * fields, width)[..., rim:rim + cells]]
  transfers between devices with their start and end apart: 4 -> 4, of which waited for: 3 -> 3; matrix products, arithmetic and copies ran while one was open for 3% -> 2% of each run, Pallas kernels for 0% -> 0%
where the time goes in v15:
time: 94.1 us; the launch traced here: 93.5 us
  blocking collectives  51.2 us (54%)
  starting transfers between devices  15.3 us (16%)
  waiting for transfers between devices  13.1 us (14%)
  Pallas kernels  7.87 us (8%)
  local copies, waits for them, and re-layouts  3.95 us (4%)
  other arithmetic  1.31 us (1%)
    all_to_all x1, blocking collectives, body(): incoming = lax.all_to_all(outgoing, 'tq', 0, 0, tiled=True)  25.8 us
    all_to_all x1, blocking collectives, body(): returned = lax.all_to_all(interior, 'tq', 0, 0, tiled=True)  25.4 us
    pallas_call x1, Pallas kernels, observe(): pl.pallas_call(observe_kernel, grid_spec=grid_spec, out_shape=[jax.ShapeD...  7.87 us
    ppermute x1, waiting for transfers between devices, body(): lax.ppermute(incoming[..., cells - rim:], 'space', ring_pairs(space, 1))  7.59 us
    ppermute x1, starting transfers between devices, body(): high = lax.ppermute(incoming[..., :rim], 'space', ring_pairs(space, -1))  7.57 us
    ppermute x2, starting transfers between devices, passed_along(): return lax.ppermute(value, axis, pairs)  5.83 us
    ppermute x2, waiting for transfers between devices, passed_along(): return lax.ppermute(value, axis, pairs)  5.54 us
    ppermute x1, starting transfers between devices, body(): lax.ppermute(incoming[..., cells - rim:], 'space', ring_pairs(space, 1))  1.92 us
  transfers between devices with their start and end apart: 4, of which 3 were waited for; matrix products, arithmetic and copies ran while one was open for 2% of the time, Pallas kernels for 0%

profile of v15, /device:TPU:64, one launch (start us, length us, event | category | flops | bytes accessed | tf_op | source)
XLA Modules:
  0.0 93.5 jit_solution(17790186937335136171)
XLA Ops:
  0.0 1.2 %reshape_squeeze.3 = bf16[4,64,1024]{2,1,0:T(8,128)(2,1)S(1)} reshape(bf16[1,4,16,4,1024]{4,3,2,1,0:T(4,128)(2,1)} %param.10) | data formatting | bytes 1048576 | tf_op jit(solution)/shard_map/reshape;squeeze | solution.py:156
  1.2 0.2 fusion
  1.4 25.8 %all_to_all.10 = bf16[4,64,1024]{2,1,0:T(8,128)(2,1)S(1)} all-to-all(bf16[4,64,1024]{2,1,0:T(8,128)(2,1)S(1)} %fusion), channel_id=1, replica_groups=mesh['tq'=4,'tr'=4,'space'=32] {'tq'}, dimensions={0} | all-to-all | bytes 1048576 | tf_op jit(solution)/shard_map/all_to_all | solution.py:158
  27.2 0.0 copy-start
  27.2 7.6 %collective-permute-start.1 = (bf16[4,64,256]{2,1,0:T(8,128)(2,1)S(1)}, bf16[4,64,256]{2,1,0:T(8,128)(2,1)S(1)}, u32[]{:S(2)}, u32[]{:S(2)}) collective-permute-start(bf16[4,64,256]{2,1,0:T(8,128)(2,1)S(1)} %get-tuple-element.35), channel_id=1, source_target_pairs={{0,31},{1,0},{2,1},{3,2},{4,3},{5,4},{6,5},{7,6},{8,7},{9,8},{10,9... | collective-permute-start | bytes 393224 | tf_op jit(solution)/shard_map/ppermute | solution.py:162
  34.8 1.9 %collective-permute-start = (bf16[4,64,256]{2,1,0:T(8,128)(2,1)S(1)}, bf16[4,64,256]{2,1,0:T(8,128)(2,1)S(1)}, u32[]{:S(2)}, u32[]{:S(2)}) collective-permute-start(bf16[4,64,256]{2,1,0:T(8,128)(2,1)S(1)} %get-tuple-element.36), channel_id=1, source_target_pairs={{0,1},{1,2},{2,3},{3,4},{4,5},{5,6},{6,7},{7,8},{8,9},{9,10},{10,1... | collective-permute-start | bytes 393224 | tf_op jit(solution)/shard_map/ppermute | solution.py:161
  37.4 0.0 collective-permute-done.1
  37.4 0.0 copy-start.1
  37.4 7.6 %collective-permute-done = bf16[4,64,256]{2,1,0:T(8,128)(2,1)S(1)} collective-permute-done((bf16[4,64,256]{2,1,0:T(8,128)(2,1)S(1)}, bf16[4,64,256]{2,1,0:T(8,128)(2,1)S(1)}, u32[]{:S(2)}, u32[]{:S(2)}) %collective-permute-start) | collective-permute-done | bytes 131104 | tf_op jit(solution)/shard_map/ppermute | solution.py:161
  45.0 0.0 copy-start.2
  45.0 0.0 copy-done
  45.0 0.0 copy-done.1
  45.0 0.7 copy-done.2
  45.6 7.9 %shard_map.64 = (f32[256,1536]{1,0:T(8,128)}, f32[256,256]{1,0:T(8,128)}, f32[256,256]{1,0:T(8,128)}) custom-call(s32[96]{0:T(128)} %bitcast.22, s32[1]{0:T(128)} %bitcast.11.cnt_ref, bf16[256,256]{1,0:T(8,128)(2,1)} %bitcast.19, bf16[256,1024]{1,0:T(8,128)(2,1)} %bitcast.12, bf16[256,256]{1,0:T(8,128)(2,1)} %bitcast.18, bf16[96,128,128]{2,1,0:T(8,128)(2,1)} %bitcast.15, ...), custom_call_target="tpu_custom_call" | custom-call | flops 1610612736 | bytes 5701632 | tf_op jit(solution)/shard_map/pallas_call | solution.py:125
  53.5 1.9 %collective-permute-start.2 = (f32[4,64,256]{2,1,0:T(8,128)}, f32[4,64,256]{2,1,0:T(8,128)S(1)}, u32[]{:S(2)}, u32[]{:S(2)}) collective-permute-start(f32[4,64,256]{2,1,0:T(8,128)} %bitcast.17), channel_id=1, source_target_pairs={{0,31},{1,0},{2,1},{3,2},{4,3},{5,4},{6,5},{7,6},{8,7},{9,8},{10,9... | collective-permute-start | bytes 786440 | tf_op jit(solution)/shard_map/ppermute | solution.py:37
  55.4 3.9 %collective-permute-start.3 = (f32[4,64,256]{2,1,0:T(8,128)}, f32[4,64,256]{2,1,0:T(8,128)S(1)}, u32[]{:S(2)}, u32[]{:S(2)}) collective-permute-start(f32[4,64,256]{2,1,0:T(8,128)} %bitcast.16), channel_id=1, source_target_pairs={{0,1},{1,2},{2,3},{3,4},{4,5},{5,6},{6,7},{7,8},{8,9},{9,10},{10,1... | collective-permute-start | bytes 786440 | tf_op jit(solution)/shard_map/ppermute | solution.py:37
  59.3 1.3 %slice.81 = f32[4,64,1024]{2,1,0:T(8,128)S(1)} slice(f32[4,64,1536]{2,1,0:T(8,128)} %bitcast.13), slice={[0:4], [0:64], [256:1280]} | slice | bytes 2097152 | tf_op jit(solution)/shard_map/slice | solution.py:176
  60.7 1.3 %collective-permute-done.2 = f32[4,64,256]{2,1,0:T(8,128)S(1)} collective-permute-done((f32[4,64,256]{2,1,0:T(8,128)}, f32[4,64,256]{2,1,0:T(8,128)S(1)}, u32[]{:S(2)}, u32[]{:S(2)}) %collective-permute-start.2) | collective-permute-done | bytes 262176 | tf_op jit(solution)/shard_map/ppermute | solution.py:37
  62.0 1.0 %fusion.2 = f32[4,64,1024]{2,1,0:T(8,128)S(1)} fusion(f32[4,64,1024]{2,1,0:T(8,128)S(1)} %slice.81, f32[4,64,256]{2,1,0:T(8,128)S(1)} %collective-permute-done.2, f32[4,64,1536]{2,1,0:T(8,128)} %bitcast.14), kind=kLoop, calls=%fused_computation.9 | loop fusion | flops 65536 | bytes 786432 | tf_op jit(solution)/shard_map/scatter-add | solution.py:177
  62.9 4.3 %collective-permute-done.3 = f32[4,64,256]{2,1,0:T(8,128)S(1)} collective-permute-done((f32[4,64,256]{2,1,0:T(8,128)}, f32[4,64,256]{2,1,0:T(8,128)S(1)}, u32[]{:S(2)}, u32[]{:S(2)}) %collective-permute-start.3) | collective-permute-done | bytes 262176 | tf_op jit(solution)/shard_map/ppermute | solution.py:37
  67.2 0.1 fusion.1
  67.3 25.4 %all_to_all.11 = f32[4,64,1024]{2,1,0:T(8,128)S(1)} all-to-all(f32[4,64,1024]{2,1,0:T(8,128)S(1)} %fusion.1), channel_id=1, replica_groups=mesh['tq'=4,'tr'=4,'space'=32] {'tq'}, dimensions={0} | all-to-all | bytes 2097152 | tf_op jit(solution)/shard_map/all_to_all | solution.py:179
  92.7 0.1 slice_add_fusion
  92.8 0.8 add.66
  (1 shorter events, 0.0 us)
Async XLA Ops:
  27.2 17.8 %copy-start = (bf16[4,64,1024]{2,1,0:T(8,128)(2,1)}, bf16[4,64,1024]{2,1,0:T(8,128)(2,1)S(1)}, u32[]{:S(2)}) copy-start(bf16[4,64,1024]{2,1,0:T(8,128)(2,1)S(1)} %all_to_all.10) | copy-start | bytes 1572868
  27.2 10.2 %collective-permute-start.1 = (bf16[4,64,256]{2,1,0:T(8,128)(2,1)S(1)}, bf16[4,64,256]{2,1,0:T(8,128)(2,1)S(1)}, u32[]{:S(2)}, u32[]{:S(2)}) collective-permute-start(bf16[4,64,256]{2,1,0:T(8,128)(2,1)S(1)} %get-tuple-element.35), channel_id=1, source_target_pairs={{0,31},{1,0},{2,1},{3,2},{4,3},{5,4},{6,5},{7,6},{8,7},{9,8},{10,9... | collective-permute-start | bytes 393224 | tf_op jit(solution)/shard_map/ppermute | solution.py:162
  34.8 10.2 %collective-permute-start = (bf16[4,64,256]{2,1,0:T(8,128)(2,1)S(1)}, bf16[4,64,256]{2,1,0:T(8,128)(2,1)S(1)}, u32[]{:S(2)}, u32[]{:S(2)}) collective-permute-start(bf16[4,64,256]{2,1,0:T(8,128)(2,1)S(1)} %get-tuple-element.36), channel_id=1, source_target_pairs={{0,1},{1,2},{2,3},{3,4},{4,5},{5,6},{6,7},{7,8},{8,9},{9,10},{10,1... | collective-permute-start | bytes 393224 | tf_op jit(solution)/shard_map/ppermute | solution.py:161
  37.4 7.6 %copy-start.1 = (bf16[4,64,256]{2,1,0:T(8,128)(2,1)}, bf16[4,64,256]{2,1,0:T(8,128)(2,1)S(1)}, u32[]{:S(2)}) copy-start(bf16[4,64,256]{2,1,0:T(8,128)(2,1)S(1)} %collective-permute-done.1) | copy-start | bytes 393220
  45.0 0.7 copy-start.2
  53.5 8.5 %collective-permute-start.2 = (f32[4,64,256]{2,1,0:T(8,128)}, f32[4,64,256]{2,1,0:T(8,128)S(1)}, u32[]{:S(2)}, u32[]{:S(2)}) collective-permute-start(f32[4,64,256]{2,1,0:T(8,128)} %bitcast.17), channel_id=1, source_target_pairs={{0,31},{1,0},{2,1},{3,2},{4,3},{5,4},{6,5},{7,6},{8,7},{9,8},{10,9... | collective-permute-start | bytes 786440 | tf_op jit(solution)/shard_map/ppermute | solution.py:37
  55.4 11.8 %collective-permute-start.3 = (f32[4,64,256]{2,1,0:T(8,128)}, f32[4,64,256]{2,1,0:T(8,128)S(1)}, u32[]{:S(2)}, u32[]{:S(2)}) collective-permute-start(f32[4,64,256]{2,1,0:T(8,128)} %bitcast.16), channel_id=1, source_target_pairs={{0,1},{1,2},{2,3},{3,4},{4,5},{5,6},{6,7},{7,8},{8,9},{9,10},{10,1... | collective-permute-start | bytes 786440 | tf_op jit(solution)/shard_map/ppermute | solution.py:37

commit v16 on v15

--- a/solution.py
+++ b/solution.py
@@ -82,12 +82,12 @@
     def backward(start, misfit, op):
         out_ref[:, pl.ds(start, width)] += jnp.dot(misfit, op, preferred_element_type=jnp.float32)
 
-    pending = forward(0)
-    for k in range(1, blocks):
-        ahead = forward(k)
-        backward(*pending)
-        pending = ahead
-    backward(*pending)
+    pending = [forward(0), forward(1)]
+    for k in range(2, blocks):
+        pending.append(forward(k))
+        backward(*pending.pop(0))
+    for item in pending:
+        backward(*item)
     low_out[...] = out_ref[:, :rim]
     high_out[...] = out_ref[:, rim + tile:]
 

time: 94.1 us -> 94.1 us (level)
  no operation moved by 1% of the time
where the time goes in v16:
time: 94.1 us; the launch traced here: 93.6 us
  blocking collectives  51.2 us (54%)
  starting transfers between devices  15.3 us (16%)
  waiting for transfers between devices  13.1 us (14%)
  Pallas kernels  7.88 us (8%)
  local copies, waits for them, and re-layouts  3.95 us (4%)
  other arithmetic  1.31 us (1%)
    all_to_all x1, blocking collectives, body(): incoming = lax.all_to_all(outgoing, 'tq', 0, 0, tiled=True)  25.8 us
    all_to_all x1, blocking collectives, body(): returned = lax.all_to_all(interior, 'tq', 0, 0, tiled=True)  25.4 us
    pallas_call x1, Pallas kernels, observe(): pl.pallas_call(observe_kernel, grid_spec=grid_spec, out_shape=[jax.ShapeD...  7.88 us
    ppermute x1, waiting for transfers between devices, body(): lax.ppermute(incoming[..., cells - rim:], 'space', ring_pairs(space, 1))  7.59 us
    ppermute x1, starting transfers between devices, body(): high = lax.ppermute(incoming[..., :rim], 'space', ring_pairs(space, -1))  7.57 us
    ppermute x2, starting transfers between devices, passed_along(): return lax.ppermute(value, axis, pairs)  5.83 us
    ppermute x2, waiting for transfers between devices, passed_along(): return lax.ppermute(value, axis, pairs)  5.54 us
    ppermute x1, starting transfers between devices, body(): lax.ppermute(incoming[..., cells - rim:], 'space', ring_pairs(space, 1))  1.92 us
  transfers between devices with their start and end apart: 4, of which 3 were waited for; matrix products, arithmetic and copies ran while one was open for 2% of the time, Pallas kernels for 0%

profile of v16, /device:TPU:64, one launch (start us, length us, event | category | flops | bytes accessed | tf_op | source)
XLA Modules:
  0.0 93.6 jit_solution(5634732273412910899)
XLA Ops:
  0.0 1.2 %reshape_squeeze.3 = bf16[4,64,1024]{2,1,0:T(8,128)(2,1)S(1)} reshape(bf16[1,4,16,4,1024]{4,3,2,1,0:T(4,128)(2,1)} %param.10) | data formatting | bytes 1048576 | tf_op jit(solution)/shard_map/reshape;squeeze | solution.py:156
  1.2 0.2 fusion
  1.4 25.8 %all_to_all.10 = bf16[4,64,1024]{2,1,0:T(8,128)(2,1)S(1)} all-to-all(bf16[4,64,1024]{2,1,0:T(8,128)(2,1)S(1)} %fusion), channel_id=1, replica_groups=mesh['tq'=4,'tr'=4,'space'=32] {'tq'}, dimensions={0} | all-to-all | bytes 1048576 | tf_op jit(solution)/shard_map/all_to_all | solution.py:158
  27.2 0.0 copy-start
  27.2 7.6 %collective-permute-start.1 = (bf16[4,64,256]{2,1,0:T(8,128)(2,1)S(1)}, bf16[4,64,256]{2,1,0:T(8,128)(2,1)S(1)}, u32[]{:S(2)}, u32[]{:S(2)}) collective-permute-start(bf16[4,64,256]{2,1,0:T(8,128)(2,1)S(1)} %get-tuple-element.35), channel_id=1, source_target_pairs={{0,31},{1,0},{2,1},{3,2},{4,3},{5,4},{6,5},{7,6},{8,7},{9,8},{10,9... | collective-permute-start | bytes 393224 | tf_op jit(solution)/shard_map/ppermute | solution.py:162
  34.8 1.9 %collective-permute-start = (bf16[4,64,256]{2,1,0:T(8,128)(2,1)S(1)}, bf16[4,64,256]{2,1,0:T(8,128)(2,1)S(1)}, u32[]{:S(2)}, u32[]{:S(2)}) collective-permute-start(bf16[4,64,256]{2,1,0:T(8,128)(2,1)S(1)} %get-tuple-element.36), channel_id=1, source_target_pairs={{0,1},{1,2},{2,3},{3,4},{4,5},{5,6},{6,7},{7,8},{8,9},{9,10},{10,1... | collective-permute-start | bytes 393224 | tf_op jit(solution)/shard_map/ppermute | solution.py:161
  37.4 0.0 collective-permute-done.1
  37.4 0.0 copy-start.1
  37.4 7.6 %collective-permute-done = bf16[4,64,256]{2,1,0:T(8,128)(2,1)S(1)} collective-permute-done((bf16[4,64,256]{2,1,0:T(8,128)(2,1)S(1)}, bf16[4,64,256]{2,1,0:T(8,128)(2,1)S(1)}, u32[]{:S(2)}, u32[]{:S(2)}) %collective-permute-start) | collective-permute-done | bytes 131104 | tf_op jit(solution)/shard_map/ppermute | solution.py:161
  45.0 0.0 copy-start.2
  45.0 0.0 copy-done
  45.0 0.0 copy-done.1
  45.0 0.7 copy-done.2
  45.6 7.9 %shard_map.64 = (f32[256,1536]{1,0:T(8,128)}, f32[256,256]{1,0:T(8,128)}, f32[256,256]{1,0:T(8,128)}) custom-call(s32[96]{0:T(128)} %bitcast.22, s32[1]{0:T(128)} %bitcast.11.cnt_ref, bf16[256,256]{1,0:T(8,128)(2,1)} %bitcast.19, bf16[256,1024]{1,0:T(8,128)(2,1)} %bitcast.12, bf16[256,256]{1,0:T(8,128)(2,1)} %bitcast.18, bf16[96,128,128]{2,1,0:T(8,128)(2,1)} %bitcast.15, ...), custom_call_target="tpu_custom_call" | custom-call | flops 1610612736 | bytes 5701632 | tf_op jit(solution)/shard_map/pallas_call | solution.py:125
  53.5 1.9 %collective-permute-start.2 = (f32[4,64,256]{2,1,0:T(8,128)}, f32[4,64,256]{2,1,0:T(8,128)S(1)}, u32[]{:S(2)}, u32[]{:S(2)}) collective-permute-start(f32[4,64,256]{2,1,0:T(8,128)} %bitcast.17), channel_id=1, source_target_pairs={{0,31},{1,0},{2,1},{3,2},{4,3},{5,4},{6,5},{7,6},{8,7},{9,8},{10,9... | collective-permute-start | bytes 786440 | tf_op jit(solution)/shard_map/ppermute | solution.py:37
  55.4 3.9 %collective-permute-start.3 = (f32[4,64,256]{2,1,0:T(8,128)}, f32[4,64,256]{2,1,0:T(8,128)S(1)}, u32[]{:S(2)}, u32[]{:S(2)}) collective-permute-start(f32[4,64,256]{2,1,0:T(8,128)} %bitcast.16), channel_id=1, source_target_pairs={{0,1},{1,2},{2,3},{3,4},{4,5},{5,6},{6,7},{7,8},{8,9},{9,10},{10,1... | collective-permute-start | bytes 786440 | tf_op jit(solution)/shard_map/ppermute | solution.py:37
  59.3 1.3 %slice.81 = f32[4,64,1024]{2,1,0:T(8,128)S(1)} slice(f32[4,64,1536]{2,1,0:T(8,128)} %bitcast.13), slice={[0:4], [0:64], [256:1280]} | slice | bytes 2097152 | tf_op jit(solution)/shard_map/slice | solution.py:176
  60.7 1.3 %collective-permute-done.2 = f32[4,64,256]{2,1,0:T(8,128)S(1)} collective-permute-done((f32[4,64,256]{2,1,0:T(8,128)}, f32[4,64,256]{2,1,0:T(8,128)S(1)}, u32[]{:S(2)}, u32[]{:S(2)}) %collective-permute-start.2) | collective-permute-done | bytes 262176 | tf_op jit(solution)/shard_map/ppermute | solution.py:37
  62.0 1.0 %fusion.2 = f32[4,64,1024]{2,1,0:T(8,128)S(1)} fusion(f32[4,64,1024]{2,1,0:T(8,128)S(1)} %slice.81, f32[4,64,256]{2,1,0:T(8,128)S(1)} %collective-permute-done.2, f32[4,64,1536]{2,1,0:T(8,128)} %bitcast.14), kind=kLoop, calls=%fused_computation.9 | loop fusion | flops 65536 | bytes 786432 | tf_op jit(solution)/shard_map/scatter-add | solution.py:177
  63.0 4.3 %collective-permute-done.3 = f32[4,64,256]{2,1,0:T(8,128)S(1)} collective-permute-done((f32[4,64,256]{2,1,0:T(8,128)}, f32[4,64,256]{2,1,0:T(8,128)S(1)}, u32[]{:S(2)}, u32[]{:S(2)}) %collective-permute-start.3) | collective-permute-done | bytes 262176 | tf_op jit(solution)/shard_map/ppermute | solution.py:37
  67.2 0.1 fusion.1
  67.3 25.4 %all_to_all.11 = f32[4,64,1024]{2,1,0:T(8,128)S(1)} all-to-all(f32[4,64,1024]{2,1,0:T(8,128)S(1)} %fusion.1), channel_id=1, replica_groups=mesh['tq'=4,'tr'=4,'space'=32] {'tq'}, dimensions={0} | all-to-all | bytes 2097152 | tf_op jit(solution)/shard_map/all_to_all | solution.py:179
  92.7 0.1 slice_add_fusion
  92.8 0.8 add.66
  (1 shorter events, 0.0 us)
Async XLA Ops:
  27.2 17.8 %copy-start = (bf16[4,64,1024]{2,1,0:T(8,128)(2,1)}, bf16[4,64,1024]{2,1,0:T(8,128)(2,1)S(1)}, u32[]{:S(2)}) copy-start(bf16[4,64,1024]{2,1,0:T(8,128)(2,1)S(1)} %all_to_all.10) | copy-start | bytes 1572868
  27.2 10.2 %collective-permute-start.1 = (bf16[4,64,256]{2,1,0:T(8,128)(2,1)S(1)}, bf16[4,64,256]{2,1,0:T(8,128)(2,1)S(1)}, u32[]{:S(2)}, u32[]{:S(2)}) collective-permute-start(bf16[4,64,256]{2,1,0:T(8,128)(2,1)S(1)} %get-tuple-element.35), channel_id=1, source_target_pairs={{0,31},{1,0},{2,1},{3,2},{4,3},{5,4},{6,5},{7,6},{8,7},{9,8},{10,9... | collective-permute-start | bytes 393224 | tf_op jit(solution)/shard_map/ppermute | solution.py:162
  34.8 10.2 %collective-permute-start = (bf16[4,64,256]{2,1,0:T(8,128)(2,1)S(1)}, bf16[4,64,256]{2,1,0:T(8,128)(2,1)S(1)}, u32[]{:S(2)}, u32[]{:S(2)}) collective-permute-start(bf16[4,64,256]{2,1,0:T(8,128)(2,1)S(1)} %get-tuple-element.36), channel_id=1, source_target_pairs={{0,1},{1,2},{2,3},{3,4},{4,5},{5,6},{6,7},{7,8},{8,9},{9,10},{10,1... | collective-permute-start | bytes 393224 | tf_op jit(solution)/shard_map/ppermute | solution.py:161
  37.4 7.6 %copy-start.1 = (bf16[4,64,256]{2,1,0:T(8,128)(2,1)}, bf16[4,64,256]{2,1,0:T(8,128)(2,1)S(1)}, u32[]{:S(2)}) copy-start(bf16[4,64,256]{2,1,0:T(8,128)(2,1)S(1)} %collective-permute-done.1) | copy-start | bytes 393220
  45.0 0.7 copy-start.2
  53.5 8.5 %collective-permute-start.2 = (f32[4,64,256]{2,1,0:T(8,128)}, f32[4,64,256]{2,1,0:T(8,128)S(1)}, u32[]{:S(2)}, u32[]{:S(2)}) collective-permute-start(f32[4,64,256]{2,1,0:T(8,128)} %bitcast.17), channel_id=1, source_target_pairs={{0,31},{1,0},{2,1},{3,2},{4,3},{5,4},{6,5},{7,6},{8,7},{9,8},{10,9... | collective-permute-start | bytes 786440 | tf_op jit(solution)/shard_map/ppermute | solution.py:37
  55.4 11.8 %collective-permute-start.3 = (f32[4,64,256]{2,1,0:T(8,128)}, f32[4,64,256]{2,1,0:T(8,128)S(1)}, u32[]{:S(2)}, u32[]{:S(2)}) collective-permute-start(f32[4,64,256]{2,1,0:T(8,128)} %bitcast.16), channel_id=1, source_target_pairs={{0,1},{1,2},{2,3},{3,4},{4,5},{5,6},{6,7},{7,8},{8,9},{9,10},{10,1... | collective-permute-start | bytes 786440 | tf_op jit(solution)/shard_map/ppermute | solution.py:37
